TPU v7x, 128 devices: a whole 4x4x4 slice. The times are simulated.
128 devices in a mesh: grp: 4 (over y), dev: 32 (over z, x, core).
Axes of the slice: x: 4, y: 4, z: 4, core: 2. Of those that a mesh axis runs over, the one named last changes fastest.
Arguments:
- ref_volume: bfloat16 [1024, 128, 1024], P('dev', None, 'grp'), may hold values from -6 to 6
- def_volume: bfloat16 [1024, 128, 1024], P('dev', None, 'grp'), may hold values from -6 to 6
- shifts: int32 [4, 32], P('grp', 'dev'), may hold values from -8 to 8, as said below
- init_disp: float32 [3, 65, 9, 65], replicated, may hold values from -3 to 3
- precond: float32 [3, 65, 9, 65], replicated, may hold values from 0.001 to 0.01
Outputs:
- displacement: float32 [3, 65, 9, 65], replicated
- residual: float32 [1024, 128, 1024], P('dev', None, 'grp')
- misfit: float32 [], replicated
Inputs may be any that keep to these rules, and one draw needn't show every extreme that they name: `shifts`: every entry lies within 8 in magnitude; both 8 and -8 occur in every draw.
All inputs are finite; a program needn't handle non-finite values.
Results may differ from a plain program's by a relative error of at most 0.0003.
Values may be sent and summed in bfloat16 or wider, within the bound.
No kernel may reach another device: no remote copies, remote signals or barrier semaphores. Data moves between devices by JAX's collectives and lax.ppermute only.
A program may use at most 128 MiB of HBM per device.

v0:
```python
import jax
import jax.numpy as jnp
from jax import lax
from jax.sharding import PartitionSpec as P

E = 16
SMAX = 8
ITERS = 2


epsilon = 1e-06


def with_halo(shard, sides, width):
    for axis, dim in sides:
        devices, length = (lax.axis_size(axis), shard.shape[dim])
        up = [(i, (i + 1) % devices) for i in range(devices - 1)]
        down = [(j, i) for i, j in up]
        last = lax.slice_in_dim(shard, length - width, length, axis=dim)
        initial = lax.slice_in_dim(shard, 0, width, axis=dim)
        before = lax.ppermute(last, axis, up)
        after = lax.ppermute(initial, axis, down)
        shard = jnp.concatenate([before, shard, after], axis=dim)
    return shard


def hat_matrix(voxels, nodes):
    positions = jnp.arange(voxels, dtype=jnp.int32)
    element = positions // E
    fraction = (positions - element * E).astype(jnp.float32) / E
    columns = jnp.arange(nodes, dtype=jnp.int32)
    left_part = (columns[None, :] == element[:, None]).astype(jnp.float32) * (1.0 - fraction)[
        :, None
    ]
    right_part = (columns[None, :] == element[:, None] + 1).astype(jnp.float32) * fraction[:, None]
    return left_part + right_part


def smooth(values, direction):
    extent = values.shape[direction]
    lower = lax.slice_in_dim(values, 0, extent - 2, axis=direction)
    middle = lax.slice_in_dim(values, 1, extent - 1, axis=direction)
    upper = lax.slice_in_dim(values, 2, extent, axis=direction)
    return (lower + 4.0 * middle + upper) / 6.0


def differ(values, direction):
    extent = values.shape[direction]
    lower = lax.slice_in_dim(values, 0, extent - 2, axis=direction)
    upper = lax.slice_in_dim(values, 2, extent, axis=direction)
    return 0.5 * (upper - lower)


def gradients(window):
    smooth_z = smooth(window, 2)
    slope_x = differ(smooth(smooth_z, 1), 0)
    slope_y = smooth(differ(smooth_z, 1), 0)
    slope_z = smooth(smooth(differ(window, 2), 1), 0)
    return jnp.stack([slope_x, slope_y, slope_z])


def interpolate(local_nodes, hat_y, hat_z):
    highest = lax.Precision.HIGHEST
    partial_z = jnp.einsum("cijk,zk->cijz", local_nodes, hat_z, precision=highest)
    return jnp.einsum("cijz,yj->ciyz", partial_z, hat_y, precision=highest)


def expand_x(partial_y, hat_x):
    return sum(
        hat_x[None, :, i, None, None] * partial_y[:, i, None] for i in range(hat_x.shape[1])
    )


def restrict(terms, hat_x, hat_y, hat_z):
    highest = lax.Precision.HIGHEST
    partial_x = jnp.stack(
        [jnp.sum(terms * hat_x[None, :, i, None, None], axis=1) for i in range(hat_x.shape[1])],
        axis=1,
    )
    partial_y = jnp.einsum("ciyz,yj->cijz", partial_x, hat_y, precision=highest)
    return jnp.einsum("cijz,zk->cijk", partial_y, hat_z, precision=highest)


def scatter_matrix(bricks, elements):
    columns = jnp.arange(bricks * elements + 1, dtype=jnp.int32)
    starts = jnp.arange(bricks, dtype=jnp.int32)[:, None] * elements
    rows = starts + jnp.arange(elements + 1, dtype=jnp.int32)[None, :]
    return (rows[:, :, None] == columns[None, None, :]).astype(jnp.float32)


def allsum(values):
    for axis in ("dev", "grp"):
        devices = lax.axis_size(axis)
        assert devices & (devices - 1) == 0
        step = 1
        while step < devices:
            pairs = [(i, i ^ step) for i in range(devices)]
            values = values + lax.ppermute(values, axis, pairs)
            step *= 2
    return values


def share_nodes(slab):
    for axis, dim in (("dev", 1), ("grp", 3)):
        devices, length = (lax.axis_size(axis), slab.shape[dim])
        up = [(i, i + 1) for i in range(devices - 1)]
        down = [(j, i) for i, j in up]
        last = lax.index_in_dim(slab, length - 1, axis=dim, keepdims=False)
        first = lax.index_in_dim(slab, 0, axis=dim, keepdims=False)
        before = lax.ppermute(last, axis, up)
        after = lax.ppermute(first, axis, down)
        head = lax.index_in_dim(slab, 0, axis=dim) + jnp.expand_dims(before, dim)
        tail = lax.index_in_dim(slab, length - 1, axis=dim) + jnp.expand_dims(after, dim)
        middle = lax.slice_in_dim(slab, 1, length - 1, axis=dim)
        slab = jnp.concatenate([head, middle, tail], axis=dim)
    return slab


def assemble(gathered):
    groups, bricks, comps, nbx, nby, nbz = gathered.shape
    highest = lax.Precision.HIGHEST
    place_x = scatter_matrix(bricks, nbx - 1)
    place_z = scatter_matrix(groups, nbz - 1)
    along_x = jnp.einsum("pqcijk,qix->pcxjk", gathered, place_x, precision=highest)
    return jnp.einsum("pcxjk,pkz->cxjz", along_x, place_z, precision=highest)


def local(ref_volume, def_volume, shifts, init_disp, precond):
    width_x, rows_y, depth_z = ref_volume.shape
    dev_count = lax.axis_size("dev")
    grp_count = lax.axis_size("grp")
    grp_index = lax.axis_index("grp")
    dev_index = lax.axis_index("dev")
    voxel_count = float(width_x * rows_y * depth_z * dev_count * grp_count)
    margin = SMAX + 1
    offset = shifts[0, 0]
    widened = with_halo(def_volume, (("dev", 0),), margin)
    framed = with_halo(widened, (("grp", 2),), 1)
    window = lax.dynamic_slice_in_dim(framed, offset + margin - 1, width_x + 2, 0)
    window = jnp.pad(window, ((0, 0), (1, 1), (0, 0))).astype(jnp.float32)
    slopes = gradients(window)
    sample = window[1:-1, 1:-1, 1:-1]
    target = ref_volume.astype(jnp.float32)
    elements_x = width_x // E
    elements_z = depth_z // E
    nodes_y = rows_y // E + 1
    hat_x = hat_matrix(width_x, elements_x + 1)
    hat_y = hat_matrix(rows_y, nodes_y)
    hat_z = hat_matrix(depth_z, elements_z + 1)
    corner = (0, dev_index * elements_x, 0, grp_index * elements_z)
    extent = (3, elements_x + 1, nodes_y, elements_z + 1)
    local_nodes = lax.dynamic_slice(init_disp, corner, extent)
    local_precond = lax.dynamic_slice(precond, corner, extent)
    target_sums = jnp.stack([jnp.sum(target), jnp.sum(target * target)])
    residual = target
    total_slab = None
    mean_ref = var_ref = None
    for iteration in range(ITERS):
        shift_field = expand_x(interpolate(local_nodes, hat_y, hat_z), hat_x)
        warped = sample + jnp.sum(shift_field * slopes, axis=0)
        image_sums = jnp.stack([jnp.sum(warped), jnp.sum(warped * warped)])
        if iteration == 0:
            sums = allsum(jnp.concatenate([target_sums, image_sums]))
            mean_ref = sums[0] / voxel_count
            var_ref = sums[1] / voxel_count - mean_ref * mean_ref
            image_sums = sums[2:]
        else:
            image_sums = allsum(image_sums)
        mean_img = image_sums[0] / voxel_count
        var_img = image_sums[1] / voxel_count - mean_img * mean_img
        ratio = jnp.sqrt((var_ref + epsilon) / (var_img + epsilon))
        residual = target - mean_ref - ratio * (warped - mean_img)
        slab = restrict(slopes * residual[None], hat_x, hat_y, hat_z)
        total_slab = slab if total_slab is None else total_slab + slab
        if iteration + 1 < ITERS:
            local_nodes = local_nodes + local_precond * share_nodes(slab)
    squares = jnp.sum(residual * residual)
    packed = jnp.concatenate([total_slab.reshape(-1), squares[None]])
    gathered = lax.all_gather(packed.reshape(2, -1), ("grp", "dev")).reshape(grp_count * dev_count, -1)
    pieces = gathered[:, :-1].reshape((grp_count, dev_count) + total_slab.shape)
    forces = assemble(pieces)
    motion = init_disp + precond * forces
    misfit = jnp.sqrt(jnp.sum(gathered[:, -1]) / voxel_count)
    return (motion, residual, misfit)


def solution(mesh):
    placed = (P("dev", None, "grp"), P("dev", None, "grp"), P("grp", "dev"), P(), P())
    return jax.shard_map(
        local,
        mesh=mesh,
        in_specs=placed,
        out_specs=(P(), P("dev", None, "grp"), P()),
        check_vma=False,
    )
```

profile of v0, /device:TPU:1, one launch (start us, length us, event | category | flops | bytes accessed | tf_op | source)
XLA Modules:
  0.0 331.6 jit_solution(13047743051610024724)
XLA Ops:
  0.6 2.2 fusion.126
  2.8 3.3 collective-permute-start.1
  6.1 3.1 collective-permute-start
  9.3 4.5 %copy.56 = bf16[32,128,256]{1,0,2:T(8,128)(2,1)} copy(bf16[32,128,256]{2,1,0:T(8,128)(2,1)} %param.6) | data formatting | bytes 4194304 | tf_op args[1]
  13.8 3.4 %copy.58 = bf16[32,128,256]{1,0,2:T(8,128)(2,1)S(1)} copy(bf16[32,128,256]{2,1,0:T(8,128)(2,1)} %param.5) | data formatting | bytes 4194304 | tf_op args[0]
  18.0 1.8 constant_dynamic-slice_fusion
  22.8 1.7 convert_reduce_fusion
  24.5 1.8 copy.57
  26.4 2.6 copy.55
  30.3 3.8 %collective-permute-start.2 = (bf16[50,128,1]{1,0,2:T(8,128)(2,1)}, bf16[50,128,1]{1,0,2:T(8,128)(2,1)}, u32[]{:S(2)}, u32[]{:S(2)}) collective-permute-start(bf16[50,128,1]{1,0,2:T(8,128)(2,1)} %get-tuple-element.30), channel_id=1, source_target_pairs={{0,32},{32,64},{64,96},{1,33},{33,65},{65,97},{2,34},{34,66},{66,9... | collective-permute-start | bytes 38408 | tf_op jit(solution)/shard_map/ppermute | solution.py:21
  36.9 1.9 copy.62
  38.8 1.9 copy.61
  42.3 6.1 %fusion.22 = bf16[34,128,258]{1,0,2:T(8,128)(2,1)S(1)} fusion(s32[]{:T(128)S(6)} %select_n.100, bf16[50,128,1]{1,0,2:T(8,128)(2,1)} %collective-permute-done.2, bf16[9,128,256]{1,0,2:T(8,128)(2,1)} %copy.55, bf16[32,128,256]{1,0,2:T(8,128)(2,1)} %copy.56, bf16[9,128,256]{1,0,2:T(8,128)(2,1)S(1)} %copy.57, bf16[50,128,1]{1,0,2:T(8,128)(2,1)} %collective-permute-done.3), kind=kLoop, calls=%fused_computation.56 | loop fusion | flops 11228160 | bytes 5548036 | tf_op jit(solution)/shard_map/concatenate | solution.py:23
  49.9 9.2 %fusion.2 = (f32[34,130,256]{1,0,2:T(8,128)}, f32[34,130,256]{1,0,2:T(8,128)}) fusion(f32[34,130,258]{1,0,2:T(8,128)S(1)} %pad_convert_fusion), kind=kLoop, calls=%fused_computation.12 | loop fusion | flops 6789120 | bytes 22630400 | tf_op jit(solution)/shard_map/div | solution.py:44
  59.1 13.0 %fusion.3 = f32[34,128,256]{1,0,2:T(8,128)} fusion(f32[34,130,256]{1,0,2:T(8,128)} %get-tuple-element.26), kind=kLoop, calls=%fused_computation.19 | loop fusion | flops 4456448 | bytes 17825792 | tf_op jit(solution)/shard_map/div | solution.py:44
  72.1 13.9 %fusion.7 = (f32[34,128,256]{1,0,2:T(8,128)}, f32[34,128,256]{1,0,2:T(8,128)}) fusion(f32[34,130,256]{1,0,2:T(8,128)} %get-tuple-element.25), kind=kLoop, calls=%fused_computation.25 | loop fusion | flops 6684672 | bytes 22282240 | tf_op jit(solution)/shard_map/div | solution.py:44
  86.0 4.6 %fusion.18 = f32[1,32,128,256]{2,1,3,0:T(8,128)S(1)} fusion(f32[34,128,256]{1,0,2:T(8,128)} %get-tuple-element.27), kind=kLoop, calls=%fused_computation.42 | loop fusion | flops 2097152 | bytes 12582912 | tf_op jit(solution)/shard_map/stack | solution.py:59
  90.7 14.2 %fusion.12 = (f32[1,32,128,256]{2,1,3,0:T(8,128)}, f32[1,32,128,256]{2,1,3,0:T(8,128)}) fusion(f32[34,128,256]{1,0,2:T(8,128)} %fusion.3, f32[34,128,256]{1,0,2:T(8,128)} %get-tuple-element.28), kind=kLoop, calls=%fused_computation.32 | loop fusion | flops 8388608 | bytes 33554432 | tf_op jit(solution)/shard_map/stack | solution.py:59
  104.9 11.8 %multiply_reduce_fusion.7 = f32[32,128,256]{1,0,2:T(8,128)} fusion(f32[3,128,256]{1,2,0:T(8,128)S(1)} %copy-done.5, f32[32]{0:T(128)S(1)} %copy-done.14, f32[3,128,256]{1,2,0:T(8,128)S(1)} %copy-done.6, f32[32]{0:T(128)S(1)} %copy-done.15, f32[3,128,256]{1,2,0:T(8,128)S(1)} %copy-done.7, f32[32]{0:T(128)S(1)} %copy-done.13, ...), kind=kLoop, calls=%fused_computation.8 | loop fusion | flops 27262976 | bytes 17957248 | tf_op jit(solution)/shard_map/reduce_sum | solution.py:160
  116.8 4.1 %fusion.123 = (f32[]{:T(128)}, f32[]{:T(128)}) fusion(f32[32,128,256]{1,0,2:T(8,128)} %multiply_reduce_fusion.7, f32[34,130,258]{1,0,2:T(8,128)S(1)} %pad_convert_fusion), kind=kLoop, calls=%fused_computation.218 | loop fusion | flops 4194302 | bytes 8388616 | tf_op jit(solution)/shard_map/reduce_sum | solution.py:161
  120.8 2.5 pad_maximum_fusion.6
  124.6 2.5 fusion.135
  129.5 2.5 fusion.137
  132.0 4.2 %collective-permute-start.6 = (f32[4]{0:T(128)S(1)}, f32[4]{0:T(128)S(1)}, u32[]{:S(2)}, u32[]{:S(2)}) collective-permute-start(f32[4]{0:T(128)S(1)} %fusion.137), channel_id=1, source_target_pairs={{0,4},{1,5},{2,6},{3,7},{4,0},{5,1},{6,2},{7,3},{8,12},{9,13},{10,... | collective-permute-start | bytes 56 | tf_op jit(solution)/shard_map/ppermute | solution.py:98
  137.1 1.6 collective-permute-start.7
  139.8 3.3 collective-permute-start.8
  144.0 2.2 collective-permute-start.9
  147.1 2.6 collective-permute-start.10
  156.7 5.7 %fusion.9 = f32[32,128,256]{1,0,2:T(8,128)} fusion(bf16[32,128,256]{1,0,2:T(8,128)(2,1)S(1)} %copy.58, f32[]{:T(128)} %bitcast.25, f32[]{:T(128)} %bitcast.24, f32[]{:T(128)} %bitcast.23, f32[32,128,256]{1,0,2:T(8,128)} %multiply_reduce_fusion.7, f32[34,130,258]{1,0,2:T(8,128)S(1)} %pad_convert_fusion), kind=kLoop, calls=%fused_computation.28 | loop fusion | flops 6291456 | bytes 14680076 | tf_op jit(solution)/shard_map/sub | solution.py:172
  162.4 15.5 %multiply_reduce_fusion.6 = (f32[3,128,256]{1,2,0:T(8,128)S(1)}, f32[3,128,256]{1,2,0:T(8,128)S(1)}, f32[3,128,256]{1,2,0:T(8,128)S(1)}) fusion(f32[32,128,256]{1,0,2:T(8,128)} %fusion.9, f32[32]{0:T(128)S(1)} %copy-done.13, f32[1,32,128,256]{2,1,3,0:T(8,128)} %get-tuple-element.67, f32[1,32,128,256]{2,1,3,0:T(8,128)} %get-tuple-element.68, ...), kind=kLoop, calls=%fused_computation.7 | loop fusion | flops 28016640 | bytes 17957248 | tf_op jit(solution)/shard_map/reduce_sum | solution.py:77
  179.4 8.2 %collective-permute-start.12 = (f32[3,9,17]{2,1,0:T(8,128)S(1)}, f32[3,9,17]{2,1,0:T(8,128)S(1)}, u32[]{:S(2)}, u32[]{:S(2)}) collective-permute-start(f32[3,9,17]{2,1,0:T(8,128)S(1)} %get-tuple-element.42), channel_id=1, source_target_pairs={{1,0},{2,1},{3,2},{4,3},{5,4},{6,5},{7,6},{8,7},{9,8},{10,9},{11,1... | collective-permute-start | bytes 5516 | tf_op jit(solution)/shard_map/ppermute | solution.py:111
  187.6 2.6 collective-permute-start.11
  191.4 3.6 %collective-permute-start.13 = (f32[3,3,9]{2,1,0:T(4,128)S(1)}, f32[3,3,9]{2,1,0:T(4,128)S(1)}, u32[]{:S(2)}, u32[]{:S(2)}) collective-permute-start(f32[3,3,9]{2,1,0:T(4,128)S(1)} %get-tuple-element.21), channel_id=1, source_target_pairs={{0,32},{32,64},{64,96},{1,33},{33,65},{65,97},{2,34},{34,66},{66,9... | collective-permute-start | bytes 980 | tf_op jit(solution)/shard_map/ppermute | solution.py:110
  197.2 2.2 collective-permute-done.14
  202.5 11.5 %multiply_reduce_fusion.3 = f32[32,128,256]{1,0,2:T(8,128)S(1)} fusion(f32[3,128,256]{1,2,0:T(8,128)S(1)} %copy.75, f32[3,128,256]{1,2,0:T(8,128)} %copy.74, f32[3,128,256]{1,2,0:T(8,128)S(1)} %copy.73, f32[32]{0:T(128)S(1)} %copy-done.14, f32[32]{0:T(128)} %get-tuple-element.46, f32[32]{0:T(128)S(1)} %copy-done.13, ...), kind=kLoop, calls=%fused_computation.4 | loop fusion | flops 27262976 | bytes 17957248 | tf_op jit(solution)/shard_map/reduce_sum | solution.py:160
  214.0 2.0 fusion.124
  220.9 2.9 collective-permute-start.16
  226.2 3.9 %collective-permute-start.17 = (f32[2]{0:T(128)S(1)}, f32[2]{0:T(128)S(1)}, u32[]{:S(2)}, u32[]{:S(2)}) collective-permute-start(f32[2]{0:T(128)S(1)} %fusion.136), channel_id=1, source_target_pairs={{0,4},{1,5},{2,6},{3,7},{4,0},{5,1},{6,2},{7,3},{8,12},{9,13},{10,... | collective-permute-start | bytes 32 | tf_op jit(solution)/shard_map/ppermute | solution.py:98
  231.0 3.2 collective-permute-start.18
  235.2 3.6 %collective-permute-start.19 = (f32[2]{0:T(128)S(1)}, f32[2]{0:T(128)S(1)}, u32[]{:S(2)}, u32[]{:S(2)}) collective-permute-start(f32[2]{0:T(128)S(1)} %add.406), channel_id=1, source_target_pairs={{0,16},{1,17},{2,18},{3,19},{4,20},{5,21},{6,22},{7,23},{8,24},{9,... | collective-permute-start | bytes 32 | tf_op jit(solution)/shard_map/ppermute | solution.py:98
  240.5 1.7 collective-permute-done.20
  242.2 2.6 collective-permute-start.21
  249.4 6.5 %multiply_reduce_fusion.8 = (f32[]{:T(128)}, f32[32,128,256]{1,0,2:T(8,128)}) fusion(f32[]{:T(128)} %bitcast.46, f32[32,128,256]{1,0,2:T(8,128)} %copy-done.2, f32[34,130,258]{1,0,2:T(8,128)S(1)} %bitcast.126, f32[]{:T(128)} %bitcast.45, f32[]{:T(128)} %bitcast.23, bf16[32,128,256]{1,0,2:T(8,128)(2,1)S(1)} %copy-done.4), kind=kLoop, calls=%fused_computation.43 | loop fusion | flops 8388607 | bytes 14680080 | tf_op jit(solution)/shard_map/reduce_sum | solution.py:177
  255.9 15.3 %multiply_reduce_fusion.2 = (f32[3,128,256]{1,2,0:T(8,128)S(1)}, f32[3,128,256]{1,2,0:T(8,128)S(1)}, f32[3,128,256]{1,2,0:T(8,128)S(1)}) fusion(f32[32,128,256]{1,0,2:T(8,128)} %get-tuple-element.24, f32[32]{0:T(128)S(1)} %copy-done.13, f32[1,32,128,256]{2,1,3,0:T(8,128)} %get-tuple-element.67, f32[1,32,128,256]{2,1,3,0:T(8,128)} %get-tuple-element.68, ...), kind=kLoop, calls=%fused_computation.3 | loop fusion | flops 28016640 | bytes 17957248 | tf_op jit(solution)/shard_map/reduce_sum | solution.py:77
  271.2 5.2 %copy.81 = f32[32,128,256]{2,1,0:T(8,128)} copy(f32[32,128,256]{1,0,2:T(8,128)} %get-tuple-element.24) | data formatting | bytes 8388608
  278.9 43.1 %all_gather.3 = f32[128,2,689]{2,1,0:T(2,128)S(1)} all-gather(f32[1,2,689]{2,1,0:T(2,128)S(1)} %all_gather_reshape.3), channel_id=1, replica_groups=mesh['grp'=4,'dev'=32] {'grp','dev'}, dimensions={0}, use_global_device_ids=true | all-gather | bytes 711048 | tf_op jit(solution)/shard_map/all_gather | solution.py:179
  325.5 2.4 fusion.25
  327.9 2.2 fusion.29
  (160 shorter events, 45.4 us)
Async XLA Ops:
  2.8 21.7 %collective-permute-start.1 = (bf16[9,128,256]{2,1,0:T(8,128)(2,1)S(1)}, bf16[9,128,256]{2,1,0:T(8,128)(2,1)}, u32[]{:S(2)}, u32[]{:S(2)}) collective-permute-start(bf16[9,128,256]{2,1,0:T(8,128)(2,1)S(1)} %get-tuple-element.32), channel_id=1, source_target_pairs={{1,0},{2,1},{3,2},{4,3},{5,4},{6,5},{7,6},{8,7},{9,8},{10,9},{11,1... | collective-permute-start | bytes 1769480 | tf_op jit(solution)/shard_map/ppermute | solution.py:22
  6.1 20.3 %collective-permute-start = (bf16[9,128,256]{2,1,0:T(8,128)(2,1)}, bf16[9,128,256]{2,1,0:T(8,128)(2,1)}, u32[]{:S(2)}, u32[]{:S(2)}) collective-permute-start(bf16[9,128,256]{2,1,0:T(8,128)(2,1)} %get-tuple-element.31), channel_id=1, source_target_pairs={{0,1},{1,2},{2,3},{3,4},{4,5},{5,6},{6,7},{7,8},{8,9},{9,10},{10,1... | collective-permute-start | bytes 1769480 | tf_op jit(solution)/shard_map/ppermute | solution.py:21
  9.3 10.8 %copy-start.19 = (f32[128]{0:T(128)}, f32[128]{0:T(128)S(1)}, u32[]{:S(2)}) copy-start(f32[128]{0:T(128)S(1)} %get-tuple-element.63) | copy-start | bytes 1540
  9.3 10.8 %copy-start.22 = (f32[128]{0:T(128)}, f32[128]{0:T(128)S(1)}, u32[]{:S(2)}) copy-start(f32[128]{0:T(128)S(1)} %get-tuple-element.64) | copy-start | bytes 1540
  9.3 10.8 %copy-start.25 = (s32[128]{0:T(128)}, s32[128]{0:T(128)S(1)}, u32[]{:S(2)}) copy-start(s32[128]{0:T(128)S(1)} %get-tuple-element.57) | copy-start | bytes 1540
  9.3 10.8 %copy-start.28 = (s32[128]{0:T(128)}, s32[128]{0:T(128)S(1)}, u32[]{:S(2)}) copy-start(s32[128]{0:T(128)S(1)} %get-tuple-element.58) | copy-start | bytes 1540
  17.3 139.4 %copy-start.3 = (bf16[32,128,256]{1,0,2:T(8,128)(2,1)}, bf16[32,128,256]{1,0,2:T(8,128)(2,1)S(1)}, u32[]{:S(2)}) copy-start(bf16[32,128,256]{1,0,2:T(8,128)(2,1)S(1)} %copy.58) | copy-start | bytes 6291460
  30.3 12.0 %collective-permute-start.2 = (bf16[50,128,1]{1,0,2:T(8,128)(2,1)}, bf16[50,128,1]{1,0,2:T(8,128)(2,1)}, u32[]{:S(2)}, u32[]{:S(2)}) collective-permute-start(bf16[50,128,1]{1,0,2:T(8,128)(2,1)} %get-tuple-element.30), channel_id=1, source_target_pairs={{0,32},{32,64},{64,96},{1,33},{33,65},{65,97},{2,34},{34,66},{66,9... | collective-permute-start | bytes 38408 | tf_op jit(solution)/shard_map/ppermute | solution.py:21
  34.1 8.2 %collective-permute-start.3 = (bf16[50,128,1]{1,0,2:T(8,128)(2,1)}, bf16[50,128,1]{1,0,2:T(8,128)(2,1)}, u32[]{:S(2)}, u32[]{:S(2)}) collective-permute-start(bf16[50,128,1]{1,0,2:T(8,128)(2,1)} %get-tuple-element.29), channel_id=1, source_target_pairs={{32,0},{64,32},{96,64},{33,1},{65,33},{97,65},{34,2},{66,34},{98,6... | collective-permute-start | bytes 38408 | tf_op jit(solution)/shard_map/ppermute | solution.py:22
  49.9 106.8 %copy-start = (f32[34,130,258]{1,0,2:T(8,128)}, f32[34,130,258]{1,0,2:T(8,128)S(1)}, u32[]{:S(2)}) copy-start(f32[34,130,258]{1,0,2:T(8,128)S(1)} %pad_convert_fusion) | copy-start | bytes 13684324
  90.6 14.3 %copy-start.1 = (f32[1,32,128,256]{2,1,3,0:T(8,128)}, f32[1,32,128,256]{2,1,3,0:T(8,128)S(1)}, u32[]{:S(2)}) copy-start(f32[1,32,128,256]{2,1,3,0:T(8,128)S(1)} %fusion.18) | copy-start | bytes 12582916
  90.6 14.3 %copy-start.5 = (f32[3,128,256]{1,2,0:T(8,128)S(1)}, f32[3,128,256]{1,2,0:T(8,128)}, u32[]{:S(2)}) copy-start(f32[3,128,256]{1,2,0:T(8,128)} %copy.62) | copy-start | bytes 1179652
  90.6 14.3 %copy-start.6 = (f32[3,128,256]{1,2,0:T(8,128)S(1)}, f32[3,128,256]{1,2,0:T(8,128)}, u32[]{:S(2)}) copy-start(f32[3,128,256]{1,2,0:T(8,128)} %copy.61) | copy-start | bytes 1179652
  90.6 14.3 %copy-start.7 = (f32[3,128,256]{1,2,0:T(8,128)S(1)}, f32[3,128,256]{1,2,0:T(8,128)}, u32[]{:S(2)}) copy-start(f32[3,128,256]{1,2,0:T(8,128)} %copy.60) | copy-start | bytes 1179652
  90.6 14.3 %copy-start.13 = (f32[32]{0:T(128)S(1)}, f32[32]{0:T(128)}, u32[]{:S(2)}) copy-start(f32[32]{0:T(128)} %get-tuple-element.44) | copy-start | bytes 388
  90.6 14.3 %copy-start.14 = (f32[32]{0:T(128)S(1)}, f32[32]{0:T(128)}, u32[]{:S(2)}) copy-start(f32[32]{0:T(128)} %get-tuple-element.45) | copy-start | bytes 388
  90.7 14.3 %copy-start.15 = (f32[32]{0:T(128)S(1)}, f32[32]{0:T(128)}, u32[]{:S(2)}) copy-start(f32[32]{0:T(128)} %get-tuple-element.46) | copy-start | bytes 388
  123.3 1.3 collective-permute-start.4
  127.1 2.4 collective-permute-start.5
  132.0 5.1 %collective-permute-start.6 = (f32[4]{0:T(128)S(1)}, f32[4]{0:T(128)S(1)}, u32[]{:S(2)}, u32[]{:S(2)}) collective-permute-start(f32[4]{0:T(128)S(1)} %fusion.137), channel_id=1, source_target_pairs={{0,4},{1,5},{2,6},{3,7},{4,0},{5,1},{6,2},{7,3},{8,12},{9,13},{10,... | collective-permute-start | bytes 56 | tf_op jit(solution)/shard_map/ppermute | solution.py:98
  137.1 2.6 collective-permute-start.7
  139.8 4.2 %collective-permute-start.8 = (f32[4]{0:T(128)S(1)}, f32[4]{0:T(128)S(1)}, u32[]{:S(2)}, u32[]{:S(2)}) collective-permute-start(f32[4]{0:T(128)S(1)} %add.387), channel_id=1, source_target_pairs={{0,16},{1,17},{2,18},{3,19},{4,20},{5,21},{6,22},{7,23},{8,24},{9,... | collective-permute-start | bytes 56 | tf_op jit(solution)/shard_map/ppermute | solution.py:98
  144.0 3.1 collective-permute-start.9
  147.1 3.9 %collective-permute-start.10 = (f32[4]{0:T(128)S(1)}, f32[4]{0:T(128)S(1)}, u32[]{:S(2)}, u32[]{:S(2)}) collective-permute-start(f32[4]{0:T(128)S(1)} %add.389), channel_id=1, source_target_pairs={{0,64},{32,96},{64,0},{96,32},{1,65},{33,97},{65,1},{97,33},{2,66}... | collective-permute-start | bytes 56 | tf_op jit(solution)/shard_map/ppermute | solution.py:98
  162.4 16.0 %copy-start.20 = (f32[128]{0:T(128)S(1)}, f32[128]{0:T(128)}, u32[]{:S(2)}) copy-start(f32[128]{0:T(128)} %copy-done.19) | copy-start | bytes 1540
  162.4 16.0 %copy-start.23 = (f32[128]{0:T(128)S(1)}, f32[128]{0:T(128)}, u32[]{:S(2)}) copy-start(f32[128]{0:T(128)} %copy-done.22) | copy-start | bytes 1540
  162.4 16.0 %copy-start.26 = (s32[128]{0:T(128)S(1)}, s32[128]{0:T(128)}, u32[]{:S(2)}) copy-start(s32[128]{0:T(128)} %copy-done.25) | copy-start | bytes 1540
  162.4 16.0 %copy-start.29 = (s32[128]{0:T(128)S(1)}, s32[128]{0:T(128)}, u32[]{:S(2)}) copy-start(s32[128]{0:T(128)} %copy-done.28) | copy-start | bytes 1540
  177.9 21.7 %copy-start.11 = (f32[3,3,9,17]{3,1,2,0:T(4,128)S(1)}, f32[3,3,9,17]{3,1,2,0:T(4,128)}, u32[]{:S(2)}) copy-start(f32[3,3,9,17]{3,1,2,0:T(4,128)} %copy-done.10) | copy-start | bytes 16528
  177.9 21.7 %copy-start.12 = (f32[3,3,9,17]{3,1,2,0:T(4,128)S(1)}, f32[3,3,9,17]{3,1,2,0:T(4,128)}, u32[]{:S(2)}) copy-start(f32[3,3,9,17]{3,1,2,0:T(4,128)} %get-tuple-element.65) | copy-start | bytes 16528
  179.4 10.8 %collective-permute-start.12 = (f32[3,9,17]{2,1,0:T(8,128)S(1)}, f32[3,9,17]{2,1,0:T(8,128)S(1)}, u32[]{:S(2)}, u32[]{:S(2)}) collective-permute-start(f32[3,9,17]{2,1,0:T(8,128)S(1)} %get-tuple-element.42), channel_id=1, source_target_pairs={{1,0},{2,1},{3,2},{4,3},{5,4},{6,5},{7,6},{8,7},{9,8},{10,9},{11,1... | collective-permute-start | bytes 5516 | tf_op jit(solution)/shard_map/ppermute | solution.py:111
  187.6 3.5 %collective-permute-start.11 = (f32[3,9,17]{2,1,0:T(8,128)S(1)}, f32[3,9,17]{2,1,0:T(8,128)S(1)}, u32[]{:S(2)}, u32[]{:S(2)}) collective-permute-start(f32[3,9,17]{2,1,0:T(8,128)S(1)} %get-tuple-element.41), channel_id=1, source_target_pairs={{0,1},{1,2},{2,3},{3,4},{4,5},{5,6},{6,7},{7,8},{8,9},{9,10},{10,1... | collective-permute-start | bytes 5516 | tf_op jit(solution)/shard_map/ppermute | solution.py:110
  191.4 5.7 %collective-permute-start.13 = (f32[3,3,9]{2,1,0:T(4,128)S(1)}, f32[3,3,9]{2,1,0:T(4,128)S(1)}, u32[]{:S(2)}, u32[]{:S(2)}) collective-permute-start(f32[3,3,9]{2,1,0:T(4,128)S(1)} %get-tuple-element.21), channel_id=1, source_target_pairs={{0,32},{32,64},{64,96},{1,33},{33,65},{65,97},{2,34},{34,66},{66,9... | collective-permute-start | bytes 980 | tf_op jit(solution)/shard_map/ppermute | solution.py:110
  195.0 4.4 %collective-permute-start.14 = (f32[3,3,9]{2,1,0:T(4,128)S(1)}, f32[3,3,9]{2,1,0:T(4,128)S(1)}, u32[]{:S(2)}, u32[]{:S(2)}) collective-permute-start(f32[3,3,9]{2,1,0:T(4,128)S(1)} %get-tuple-element.22), channel_id=1, source_target_pairs={{32,0},{64,32},{96,64},{33,1},{65,33},{97,65},{34,2},{66,34},{98,6... | collective-permute-start | bytes 980 | tf_op jit(solution)/shard_map/ppermute | solution.py:111
  201.4 12.6 %slice-start = ((s8[10567680]{0:T(1024)(128)(4,1)}), s8[2179072]{0:T(1024)(128)(4,1)S(1)}, s32[]{:S(2)}) async-start(s8[10567680]{0:T(1024)(128)(4,1)} %bitcast.125), calls=%async_computation | async-start | bytes 4358144
  202.5 11.5 %slice-start.1 = ((s8[10567680]{0:T(1024)(128)(4,1)}), s8[4194304]{0:T(1024)(128)(4,1)S(1)}, s32[]{:S(2)}) async-start(s8[10567680]{0:T(1024)(128)(4,1)} %bitcast.125), calls=%async_computation.1 | async-start | bytes 8388608
  202.5 11.5 %slice-start.2 = ((s8[10567680]{0:T(1024)(128)(4,1)}), s8[4194304]{0:T(1024)(128)(4,1)S(1)}, s32[]{:S(2)}) async-start(s8[10567680]{0:T(1024)(128)(4,1)} %bitcast.125), calls=%async_computation.2 | async-start | bytes 8388608
  214.0 35.3 %copy-start.4 = (bf16[32,128,256]{1,0,2:T(8,128)(2,1)S(1)}, bf16[32,128,256]{1,0,2:T(8,128)(2,1)}, u32[]{:S(2)}) copy-start(bf16[32,128,256]{1,0,2:T(8,128)(2,1)} %copy-done.3) | copy-start | bytes 6291460
  217.6 2.0 collective-permute-start.15
  220.9 3.9 %collective-permute-start.16 = (f32[2]{0:T(128)S(1)}, f32[2]{0:T(128)S(1)}, u32[]{:S(2)}, u32[]{:S(2)}) collective-permute-start(f32[2]{0:T(128)S(1)} %fusion.134), channel_id=1, source_target_pairs={{0,2},{1,3},{2,0},{3,1},{4,6},{5,7},{6,4},{7,5},{8,10},{9,11},{10,... | collective-permute-start | bytes 32 | tf_op jit(solution)/shard_map/ppermute | solution.py:98
  226.2 4.8 %collective-permute-start.17 = (f32[2]{0:T(128)S(1)}, f32[2]{0:T(128)S(1)}, u32[]{:S(2)}, u32[]{:S(2)}) collective-permute-start(f32[2]{0:T(128)S(1)} %fusion.136), channel_id=1, source_target_pairs={{0,4},{1,5},{2,6},{3,7},{4,0},{5,1},{6,2},{7,3},{8,12},{9,13},{10,... | collective-permute-start | bytes 32 | tf_op jit(solution)/shard_map/ppermute | solution.py:98
  231.0 4.1 %collective-permute-start.18 = (f32[2]{0:T(128)S(1)}, f32[2]{0:T(128)S(1)}, u32[]{:S(2)}, u32[]{:S(2)}) collective-permute-start(f32[2]{0:T(128)S(1)} %add.405), channel_id=1, source_target_pairs={{0,8},{1,9},{2,10},{3,11},{4,12},{5,13},{6,14},{7,15},{8,0},{9,1},... | collective-permute-start | bytes 32 | tf_op jit(solution)/shard_map/ppermute | solution.py:98
  235.2 4.6 %collective-permute-start.19 = (f32[2]{0:T(128)S(1)}, f32[2]{0:T(128)S(1)}, u32[]{:S(2)}, u32[]{:S(2)}) collective-permute-start(f32[2]{0:T(128)S(1)} %add.406), channel_id=1, source_target_pairs={{0,16},{1,17},{2,18},{3,19},{4,20},{5,21},{6,22},{7,23},{8,24},{9,... | collective-permute-start | bytes 32 | tf_op jit(solution)/shard_map/ppermute | solution.py:98
  239.7 2.4 collective-permute-start.20
  242.2 3.9 %collective-permute-start.21 = (f32[2]{0:T(128)S(1)}, f32[2]{0:T(128)S(1)}, u32[]{:S(2)}, u32[]{:S(2)}) collective-permute-start(f32[2]{0:T(128)S(1)} %add.408), channel_id=1, source_target_pairs={{0,64},{32,96},{64,0},{96,32},{1,65},{33,97},{65,1},{97,33},{2,66}... | collective-permute-start | bytes 32 | tf_op jit(solution)/shard_map/ppermute | solution.py:98
  249.4 6.5 %copy-start.16 = (f32[32]{0:T(128)S(1)}, f32[32]{0:T(128)}, u32[]{:S(2)}) copy-start(f32[32]{0:T(128)} %get-tuple-element.46) | copy-start | bytes 388
  271.2 5.8 %copy-start.24 = (f32[128]{0:T(128)S(1)}, f32[128]{0:T(128)}, u32[]{:S(2)}) copy-start(f32[128]{0:T(128)} %copy-done.22) | copy-start | bytes 1540
  277.7 47.8 %copy-start.17 = (s32[32,3]{0,1:T(4,128)S(1)}, s32[32,3]{0,1:T(4,128)}, u32[]{:S(2)}) copy-start(s32[32,3]{0,1:T(4,128)} %iota_add_fusion.1) | copy-start | bytes 1156
  (8 other events, 30.1 us)
where the time goes:
time: 336 us; the launch traced here: 332 us
  other arithmetic  153 us (46%)
  starting transfers between devices  61.1 us (18%)
  blocking collectives  43.1 us (13%)
  local copies, waits for them, and re-layouts  34.6 us (10%)
  waiting for transfers between devices  18 us (5%)
  between operations  12 us (4%)
  matrix products  9.32 us (3%)
    all_gather x1, blocking collectives, local(): lax.all_gather(packed.reshape(2, -1), ('grp', 'dev'))  43.1 us
    div x3, other arithmetic, smooth(): return (lower + 4.0 * middle + upper) / 6.0  36.1 us
    ppermute x14, starting transfers between devices, allsum(): values = values + lax.ppermute(values, axis, pairs)  33.6 us
    reduce_sum x2, other arithmetic, restrict(): jnp.sum(terms * hat_x[None, :, i, None, None], axis=1)  30.8 us
    reduce_sum x2, other arithmetic, local(): warped = sample + jnp.sum(shift_field * slopes, axis=0)  23.3 us
    another operation x2, other arithmetic, gradients(): return jnp.stack([slope_x, slope_y, slope_z])  18.8 us
    ppermute x14, waiting for transfers between devices, allsum(): values = values + lax.ppermute(values, axis, pairs)  14.9 us
    unnamed x72, local copies, waits for them, and re-layouts  13.7 us
  transfers between devices with their start and end apart: 22, of which 16 were waited for; matrix products, arithmetic and copies ran while one was open for 7% of the time, Pallas kernels for 0%

commit v1 on v0

--- a/solution.py
+++ b/solution.py
@@ -56,7 +56,7 @@
     slope_x = differ(smooth(smooth_z, 1), 0)
     slope_y = smooth(differ(smooth_z, 1), 0)
     slope_z = smooth(smooth(differ(window, 2), 1), 0)
-    return jnp.stack([slope_x, slope_y, slope_z])
+    return (slope_x, slope_y, slope_z)
 
 
 def interpolate(local_nodes, hat_y, hat_z):
@@ -152,13 +152,16 @@
     local_nodes = lax.dynamic_slice(init_disp, corner, extent)
     local_precond = lax.dynamic_slice(precond, corner, extent)
     target_sums = jnp.stack([jnp.sum(target), jnp.sum(target * target)])
+    fixed_a = restrict(jnp.stack([s * target for s in slopes]), hat_x, hat_y, hat_z)
+    fixed_b = restrict(jnp.stack(slopes), hat_x, hat_y, hat_z)
     residual = target
     total_slab = None
     mean_ref = var_ref = None
     for iteration in range(ITERS):
         shift_field = expand_x(interpolate(local_nodes, hat_y, hat_z), hat_x)
-        warped = sample + jnp.sum(shift_field * slopes, axis=0)
+        warped = sample + sum(shift_field[c] * slopes[c] for c in range(3))
         image_sums = jnp.stack([jnp.sum(warped), jnp.sum(warped * warped)])
+        moving = restrict(jnp.stack([s * warped for s in slopes]), hat_x, hat_y, hat_z)
         if iteration == 0:
             sums = allsum(jnp.concatenate([target_sums, image_sums]))
             mean_ref = sums[0] / voxel_count
@@ -169,11 +172,12 @@
         mean_img = image_sums[0] / voxel_count
         var_img = image_sums[1] / voxel_count - mean_img * mean_img
         ratio = jnp.sqrt((var_ref + epsilon) / (var_img + epsilon))
-        residual = target - mean_ref - ratio * (warped - mean_img)
-        slab = restrict(slopes * residual[None], hat_x, hat_y, hat_z)
+        slab = fixed_a - mean_ref * fixed_b - ratio * (moving - mean_img * fixed_b)
         total_slab = slab if total_slab is None else total_slab + slab
         if iteration + 1 < ITERS:
             local_nodes = local_nodes + local_precond * share_nodes(slab)
+        else:
+            residual = target - mean_ref - ratio * (warped - mean_img)
     squares = jnp.sum(residual * residual)
     packed = jnp.concatenate([total_slab.reshape(-1), squares[None]])
     gathered = lax.all_gather(packed.reshape(2, -1), ("grp", "dev")).reshape(grp_count * dev_count, -1)

time: 336 us -> 396 us (1.18)
  other arithmetic: 153 us -> 203 us
  matrix products: 9.32 us -> 15.2 us
  local copies, waits for them, and re-layouts: 34.6 us -> 38.7 us
    another operation x2 -> x4, other arithmetic: 18.8 us -> 64.2 us  [local(): jnp.stack([s * warped for s in slopes])]
    reduce_sum x2, other arithmetic: 30.8 us -> 68 us  [restrict(): jnp.sum(terms * hat_x[None, :, i, None, None], axis=1)]
    div x3 -> x1, other arithmetic: 36.1 us -> 4.33 us  [smooth(): return (lower + 4.0 * middle + upper) / 6.0]
    reduce_sum x4 -> x0, other arithmetic: 31.5 us -> none  [the longest x2 23.3 us: local(): warped = sample + jnp.sum(shift_field * slopes, axis=0)]
    mul x0 -> x2, other arithmetic: none -> 23.3 us  [differ(): return 0.5 * (upper - lower)]
    add x0 -> x2, other arithmetic: none -> 14.1 us  [expand_x(): sum((hat_x[None, :, i, None, None] * partial_y[:, i, None] for i in range...]
    ppermute x2, starting transfers between devices: 9.5 us -> 3.42 us  [share_nodes(): after = lax.ppermute(first, axis, down)]
    reduce_sum x6 -> x12, local copies, waits for them, and re-layouts: 0.97 us -> 6.96 us  [restrict(): jnp.sum(terms * hat_x[None, :, i, None, None], axis=1)]
  transfers between devices with their start and end apart: 22 -> 22, of which waited for: 16 -> 15; matrix products, arithmetic and copies ran while one was open for 7% -> 22% of each run, Pallas kernels for 0% -> 0%
where the time goes in v1:
time: 396 us; the launch traced here: 392 us
  other arithmetic  203 us (51%)
  starting transfers between devices  60.9 us (15%)
  blocking collectives  43.2 us (11%)
  local copies, waits for them, and re-layouts  38.7 us (10%)
  waiting for transfers between devices  18.6 us (5%)
  matrix products  15.2 us (4%)
  between operations  12.6 us (3%)
    reduce_sum x2, other arithmetic, restrict(): jnp.sum(terms * hat_x[None, :, i, None, None], axis=1)  68 us
    another operation x4, other arithmetic, local(): jnp.stack([s * warped for s in slopes])  64.2 us
    all_gather x1, blocking collectives, local(): lax.all_gather(packed.reshape(2, -1), ('grp', 'dev'))  43.2 us
    ppermute x14, starting transfers between devices, allsum(): values = values + lax.ppermute(values, axis, pairs)  34.6 us
    mul x2, other arithmetic, differ(): return 0.5 * (upper - lower)  23.3 us
    unnamed x84, local copies, waits for them, and re-layouts  15 us
    add x2, other arithmetic, expand_x(): sum((hat_x[None, :, i, None, None] * partial_y[:, i, None] for i in range...  14.1 us
    ppermute x14, waiting for transfers between devices, allsum(): values = values + lax.ppermute(values, axis, pairs)  13.4 us
  transfers between devices with their start and end apart: 22, of which 15 were waited for; matrix products, arithmetic and copies ran while one was open for 22% of the time, Pallas kernels for 0%

profile of v1, /device:TPU:1, one launch (start us, length us, event | category | flops | bytes accessed | tf_op | source)
XLA Modules:
  0.0 391.8 jit_solution(2041699827348268665)
XLA Ops:
  0.6 2.4 fusion.197
  3.0 4.5 %collective-permute-start = (bf16[9,128,256]{2,1,0:T(8,128)(2,1)}, bf16[9,128,256]{2,1,0:T(8,128)(2,1)}, u32[]{:S(2)}, u32[]{:S(2)}) collective-permute-start(bf16[9,128,256]{2,1,0:T(8,128)(2,1)} %get-tuple-element.57), channel_id=1, source_target_pairs={{0,1},{1,2},{2,3},{3,4},{4,5},{5,6},{6,7},{7,8},{8,9},{9,10},{10,1... | collective-permute-start | bytes 1769480 | tf_op jit(solution)/shard_map/ppermute | solution.py:21
  7.5 1.9 collective-permute-start.1
  9.5 3.4 copy.56
  13.0 1.8 constant_dynamic-slice_fusion
  19.0 5.5 %multiply_add_fusion.1 = f32[3,32,128,256]{2,1,3,0:T(8,128)} fusion(f32[3,128,256]{1,2,0:T(8,128)S(1)} %copy.65, f32[3,128,256]{1,2,0:T(8,128)S(1)} %copy.64, f32[3,128,256]{1,2,0:T(8,128)S(1)} %copy.63, f32[32]{0:T(128)S(1)} %get-tuple-element.71, f32[32]{0:T(128)S(1)} %get-tuple-element.72, f32[32]{0:T(128)S(1)} %get-tuple-element.70), kind=kLoop, calls=%fused_computation.14 | loop fusion | flops 15728640 | bytes 13762944 | tf_op jit(solution)/shard_map/add | solution.py:69
  24.5 1.8 copy.55
  26.3 2.6 copy.57
  29.6 3.2 collective-permute-start.2
  32.8 1.8 collective-permute-start.3
  35.9 4.6 %copy.58 = bf16[32,128,256]{1,0,2:T(8,128)(2,1)} copy(bf16[32,128,256]{2,1,0:T(8,128)(2,1)} %param.5) | data formatting | bytes 4194304 | tf_op args[0]
  40.5 5.8 %fusion.33 = bf16[34,128,258]{1,0,2:T(8,128)(2,1)S(1)} fusion(s32[]{:T(128)S(6)} %select_n.120, bf16[50,128,1]{1,0,2:T(8,128)(2,1)S(1)} %collective-permute-done.2, bf16[9,128,256]{1,0,2:T(8,128)(2,1)S(1)} %copy.55, bf16[32,128,256]{1,0,2:T(8,128)(2,1)S(1)} %copy.56, bf16[9,128,256]{1,0,2:T(8,128)(2,1)} %copy.57, ...), kind=kLoop, calls=%fused_computation.89 | loop fusion | flops 11228160 | bytes 5548036 | tf_op jit(solution)/shard_map/concatenate | solution.py:23
  46.3 1.5 pad_convert_fusion
  47.7 9.2 %subtract_multiply_fusion = (f32[34,130,256]{1,0,2:T(8,128)}, f32[34,130,256]{1,0,2:T(8,128)}) fusion(f32[34,130,258]{1,0,2:T(8,128)S(1)} %pad_convert_fusion), kind=kLoop, calls=%fused_computation.22 | loop fusion | flops 6789120 | bytes 22630400 | tf_op jit(solution)/shard_map/mul | solution.py:51
  57.9 14.1 %subtract_multiply_fusion.1 = (f32[34,128,256]{1,0,2:T(8,128)}, f32[34,128,256]{1,0,2:T(8,128)}) fusion(f32[34,130,256]{1,0,2:T(8,128)} %get-tuple-element.39), kind=kLoop, calls=%fused_computation.38 | loop fusion | flops 6684672 | bytes 22282240 | tf_op jit(solution)/shard_map/mul | solution.py:51
  72.0 4.3 %fusion.3 = f32[34,128,256]{1,0,2:T(8,128)} fusion(f32[34,130,256]{1,0,2:T(8,128)S(1)} %copy-done.7), kind=kLoop, calls=%fused_computation.31 | loop fusion | flops 4456448 | bytes 17825792 | tf_op jit(solution)/shard_map/div | solution.py:44
  76.3 32.1 %multiply_bitcast_fusion.5 = (f32[1,32,128,256]{2,1,3,0:T(8,128)}, f32[32,128,256]{1,0,2:T(8,128)}, f32[32,128,256]{1,0,2:T(8,128)}, f32[32,128,256]{1,0,2:T(8,128)}, f32[32,128,256]{1,0,2:T(8,128)}) fusion(f32[3,32,128,256]{2,1,3,0:T(8,128)} %multiply_add_fusion.1, f32[34,130,258]{1,0,2:T(8,128)} %copy-done, f32[34,128,256]{1,0,2:T(8,128)} %get-tuple-element.41, ...), kind=kLoop, calls=%fused_computation.79 | loop fusion | flops 17825792 | bytes 71303168 | tf_op jit(solution)/shard_map/stack | solution.py:164
  108.5 14.8 %multiply_bitcast_fusion.4 = (f32[1,32,128,256]{2,1,3,0:T(8,128)}, f32[1,32,128,256]{2,1,3,0:T(8,128)}, f32[1,32,128,256]{2,1,3,0:T(8,128)}, f32[1,32,128,256]{2...) fusion(f32[32,128,256]{1,0,2:T(8,128)} %get-tuple-element.36, ...), kind=kLoop, calls=%fused_computation.78 | loop fusion | flops 12582908 | bytes 39845904 | tf_op jit(solution)/shard_map/stack | solution.py:164
  123.4 3.7 pad_maximum_fusion.9
  127.1 55.0 %multiply_reduce_fusion.5 = (f32[3,128,256]{1,2,0:T(8,128)S(1)}, f32[3,128,256]{1,2,0:T(8,128)S(1)}, f32[3,128,256]{1,2,0:T(8,128)S(1)}, f32[3,128,256]{1,2,0:T(...) fusion(f32[32]{0:T(128)S(1)} %copy-done.22, ...), kind=kLoop, calls=%fused_computation.10 | loop fusion | flops 74612736 | bytes 41288064 | tf_op jit(solution)/shard_map/reduce_sum | solution.py:77
  186.2 1.7 fusion.71
  191.4 3.1 fusion.208
  194.5 2.1 collective-permute-start.5
  197.5 3.1 fusion.210
  200.6 3.0 collective-permute-start.6
  204.6 4.0 %collective-permute-start.7 = (f32[4]{0:T(128)S(1)}, f32[4]{0:T(128)S(1)}, u32[]{:S(2)}, u32[]{:S(2)}) collective-permute-start(f32[4]{0:T(128)S(1)} %add.452), channel_id=1, source_target_pairs={{0,8},{1,9},{2,10},{3,11},{4,12},{5,13},{6,14},{7,15},{8,0},{9,1},... | collective-permute-start | bytes 56 | tf_op jit(solution)/shard_map/ppermute | solution.py:98
  209.5 3.4 collective-permute-start.8
  213.9 2.4 collective-permute-start.9
  217.3 3.1 collective-permute-start.10
  227.9 7.9 %collective-permute-start.11 = (f32[3,9,17]{2,1,0:T(8,128)S(1)}, f32[3,9,17]{2,1,0:T(8,128)S(1)}, u32[]{:S(2)}, u32[]{:S(2)}) collective-permute-start(f32[3,9,17]{2,1,0:T(8,128)S(1)} %get-tuple-element.67), channel_id=1, source_target_pairs={{0,1},{1,2},{2,3},{3,4},{4,5},{5,6},{6,7},{7,8},{8,9},{9,10},{10,1... | collective-permute-start | bytes 5516 | tf_op jit(solution)/shard_map/ppermute | solution.py:110
  235.8 2.1 collective-permute-start.12
  237.9 3.0 collective-permute-done.12
  241.1 3.6 collective-permute-start.13
  246.9 2.2 collective-permute-done.14
  253.0 8.6 %multiply_add_fusion = f32[3,32,128,256]{2,1,3,0:T(8,128)} fusion(f32[3,128,256]{1,2,0:T(8,128)} %copy.81, f32[3,128,256]{1,2,0:T(8,128)} %copy.80, f32[3,128,256]{1,2,0:T(8,128)S(1)} %copy.79, f32[32]{0:T(128)S(1)} %copy-done.26, f32[32]{0:T(128)} %copy-done.27, f32[32]{0:T(128)S(1)} %copy-done.23), kind=kLoop, calls=%fused_computation.7 | loop fusion | flops 15728640 | bytes 13762944 | tf_op jit(solution)/shard_map/add | solution.py:69
  261.6 12.2 %multiply_bitcast_fusion.2 = (f32[1,32,128,256]{2,1,3,0:T(8,128)}, f32[32,128,256]{1,0,2:T(8,128)}) fusion(f32[32,128,256]{1,0,2:T(8,128)S(1)} %copy-done.6, f32[32,128,256]{1,0,2:T(8,128)S(1)} %copy-done.4, f32[3,32,128,256]{2,1,3,0:T(8,128)} %multiply_add_fusion, f32[32,128,256]{1,0,2:T(8,128)S(1)} %copy-done.2, f32[34,130,258]{1,0,2:T(8,128)} %copy-done), kind=kLoop, calls=%fused_computation.75 | loop fusion | flops 7340032 | bytes 37748736 | tf_op jit(solution)/shard_map/stack | solution.py:164
  273.8 4.0 %fusion.189 = (f32[]{:T(128)}, f32[]{:T(128)}) fusion(f32[32,128,256]{1,0,2:T(8,128)} %get-tuple-element.30), kind=kLoop, calls=%fused_computation.302 | loop fusion | flops 3145726 | bytes 4194312 | tf_op jit(solution)/shard_map/reduce_sum | solution.py:163
  284.2 1.4 fusion.209
  285.6 5.8 %collective-permute-start.17 = (f32[2]{0:T(128)S(1)}, f32[2]{0:T(128)S(1)}, u32[]{:S(2)}, u32[]{:S(2)}) collective-permute-start(f32[2]{0:T(128)S(1)} %fusion.209), channel_id=1, source_target_pairs={{0,4},{1,5},{2,6},{3,7},{4,0},{5,1},{6,2},{7,3},{8,12},{9,13},{10,... | collective-permute-start | bytes 32 | tf_op jit(solution)/shard_map/ppermute | solution.py:98
  292.3 2.1 collective-permute-start.18
  295.3 3.5 collective-permute-start.19
  302.1 2.8 collective-permute-start.21
  309.6 5.1 %multiply_bitcast_fusion.1 = (f32[1,32,128,256]{2,1,3,0:T(8,128)S(1)}, f32[1,32,128,256]{2,1,3,0:T(8,128)S(1)}, f32[]{:T(128)}, f32[32,128,256]{1,0,2:T(8,128)}) fusion(f32[32,128,256]{1,0,2:T(8,128)S(1)} %copy-done.2, f32[32,128,256]{1,0,2:T(8,128)S(1)} %copy-done.8, f32[32,128,256]{1,0,2:T(8,128)S(1)} %copy-done.4, f32[]{:T(128)} %bitcast.73, f32[]{:T(128)} %bitcast.65, ...), kind=kLoop, calls=%fused_computation.74 | loop fusion | flops 9437183 | bytes 27262992 | tf_op jit(solution)/shard_map/stack | solution.py:164
  314.7 13.0 %multiply_reduce_fusion.2 = (f32[3,128,256]{1,2,0:T(8,128)}, f32[3,128,256]{1,2,0:T(8,128)}, f32[3,128,256]{1,2,0:T(8,128)S(1)}) fusion(f32[32]{0:T(128)S(1)} %copy-done.23, f32[1,32,128,256]{2,1,3,0:T(8,128)S(1)} %get-tuple-element.43, f32[1,32,128,256]{2,1,3,0:T(8,128)S(1)} %get-tuple-element.42, f32[1,32,128,256]{2,1,3,0:T(8,128)S(1)} %copy-done.10, ...), kind=kLoop, calls=%fused_computation.6 | loop fusion | flops 24870912 | bytes 13762944 | tf_op jit(solution)/shard_map/reduce_sum | solution.py:77
  333.6 43.2 %all_gather.3 = f32[128,2,689]{2,1,0:T(2,128)S(1)} all-gather(f32[1,2,689]{2,1,0:T(2,128)S(1)} %all_gather_reshape.3), channel_id=1, replica_groups=mesh['grp'=4,'dev'=32] {'grp','dev'}, dimensions={0}, use_global_device_ids=true | all-gather | bytes 711048 | tf_op jit(solution)/shard_map/all_gather | solution.py:183
  379.6 5.2 %copy.87 = f32[32,128,256]{2,1,0:T(8,128)} copy(f32[32,128,256]{1,0,2:T(8,128)} %get-tuple-element.45) | data formatting | bytes 8388608
  385.5 2.4 fusion.36
  387.9 2.2 fusion.40
  (179 shorter events, 49.3 us)
Async XLA Ops:
  3.0 21.5 %collective-permute-start = (bf16[9,128,256]{2,1,0:T(8,128)(2,1)}, bf16[9,128,256]{2,1,0:T(8,128)(2,1)}, u32[]{:S(2)}, u32[]{:S(2)}) collective-permute-start(bf16[9,128,256]{2,1,0:T(8,128)(2,1)} %get-tuple-element.57), channel_id=1, source_target_pairs={{0,1},{1,2},{2,3},{3,4},{4,5},{5,6},{6,7},{7,8},{8,9},{9,10},{10,1... | collective-permute-start | bytes 1769480 | tf_op jit(solution)/shard_map/ppermute | solution.py:21
  7.5 18.9 %collective-permute-start.1 = (bf16[9,128,256]{2,1,0:T(8,128)(2,1)}, bf16[9,128,256]{2,1,0:T(8,128)(2,1)}, u32[]{:S(2)}, u32[]{:S(2)}) collective-permute-start(bf16[9,128,256]{2,1,0:T(8,128)(2,1)} %get-tuple-element.58), channel_id=1, source_target_pairs={{1,0},{2,1},{3,2},{4,3},{5,4},{6,5},{7,6},{8,7},{9,8},{10,9},{11,1... | collective-permute-start | bytes 1769480 | tf_op jit(solution)/shard_map/ppermute | solution.py:22
  9.5 8.0 %copy-start.32 = (s32[128]{0:T(128)}, s32[128]{0:T(128)S(1)}, u32[]{:S(2)}) copy-start(s32[128]{0:T(128)S(1)} %get-tuple-element.89) | copy-start | bytes 1540
  9.5 7.9 %copy-start.34 = (s32[128]{0:T(128)}, s32[128]{0:T(128)S(1)}, u32[]{:S(2)}) copy-start(s32[128]{0:T(128)S(1)} %get-tuple-element.90) | copy-start | bytes 1540
  9.5 7.9 %copy-start.36 = (f32[128]{0:T(128)}, f32[128]{0:T(128)S(1)}, u32[]{:S(2)}) copy-start(f32[128]{0:T(128)S(1)} %get-tuple-element.95) | copy-start | bytes 1540
  29.6 10.8 %collective-permute-start.2 = (bf16[50,128,1]{1,0,2:T(8,128)(2,1)S(1)}, bf16[50,128,1]{1,0,2:T(8,128)(2,1)S(1)}, u32[]{:S(2)}, u32[]{:S(2)}) collective-permute-start(bf16[50,128,1]{1,0,2:T(8,128)(2,1)S(1)} %get-tuple-element.53), channel_id=1, source_target_pairs={{0,32},{32,64},{64,96},{1,33},{33,65},{65,97},{2,34},{34,66},{66,9... | collective-permute-start | bytes 38408 | tf_op jit(solution)/shard_map/ppermute | solution.py:21
  32.8 7.6 %collective-permute-start.3 = (bf16[50,128,1]{1,0,2:T(8,128)(2,1)S(1)}, bf16[50,128,1]{1,0,2:T(8,128)(2,1)S(1)}, u32[]{:S(2)}, u32[]{:S(2)}) collective-permute-start(bf16[50,128,1]{1,0,2:T(8,128)(2,1)S(1)} %get-tuple-element.52), channel_id=1, source_target_pairs={{32,0},{64,32},{96,64},{33,1},{65,33},{97,65},{34,2},{66,34},{98,6... | collective-permute-start | bytes 38408 | tf_op jit(solution)/shard_map/ppermute | solution.py:22
  47.7 10.2 %copy-start = (f32[34,130,258]{1,0,2:T(8,128)}, f32[34,130,258]{1,0,2:T(8,128)S(1)}, u32[]{:S(2)}) copy-start(f32[34,130,258]{1,0,2:T(8,128)S(1)} %pad_convert_fusion) | copy-start | bytes 13684324
  57.9 14.1 %copy-start.7 = (f32[34,130,256]{1,0,2:T(8,128)S(1)}, f32[34,130,256]{1,0,2:T(8,128)}, u32[]{:S(2)}) copy-start(f32[34,130,256]{1,0,2:T(8,128)} %get-tuple-element.38) | copy-start | bytes 13578244
  76.3 32.1 %copy-start.9 = (bf16[32,128,256]{1,0,2:T(8,128)(2,1)S(1)}, bf16[32,128,256]{1,0,2:T(8,128)(2,1)}, u32[]{:S(2)}) copy-start(bf16[32,128,256]{1,0,2:T(8,128)(2,1)} %copy.58) | copy-start | bytes 6291460
  108.5 18.6 %copy-start.1 = (f32[32,128,256]{1,0,2:T(8,128)S(1)}, f32[32,128,256]{1,0,2:T(8,128)}, u32[]{:S(2)}) copy-start(f32[32,128,256]{1,0,2:T(8,128)} %get-tuple-element.36) | copy-start | bytes 12582916
  108.5 18.6 %copy-start.3 = (f32[32,128,256]{1,0,2:T(8,128)S(1)}, f32[32,128,256]{1,0,2:T(8,128)}, u32[]{:S(2)}) copy-start(f32[32,128,256]{1,0,2:T(8,128)} %get-tuple-element.37) | copy-start | bytes 12582916
  108.5 18.6 %copy-start.5 = (f32[32,128,256]{1,0,2:T(8,128)S(1)}, f32[32,128,256]{1,0,2:T(8,128)}, u32[]{:S(2)}) copy-start(f32[32,128,256]{1,0,2:T(8,128)} %get-tuple-element.35) | copy-start | bytes 12582916
  108.5 18.6 %copy-start.22 = (f32[32]{0:T(128)S(1)}, f32[32]{0:T(128)}, u32[]{:S(2)}) copy-start(f32[32]{0:T(128)} %copy-done.21) | copy-start | bytes 388
  108.5 18.6 %copy-start.25 = (f32[32]{0:T(128)S(1)}, f32[32]{0:T(128)}, u32[]{:S(2)}) copy-start(f32[32]{0:T(128)} %copy-done.24) | copy-start | bytes 388
  108.5 18.6 %copy-start.28 = (f32[32]{0:T(128)S(1)}, f32[32]{0:T(128)}, u32[]{:S(2)}) copy-start(f32[32]{0:T(128)} %copy-done.27) | copy-start | bytes 388
  127.1 64.3 %collective-permute-start.4 = (f32[4]{0:T(128)}, f32[4]{0:T(128)}, u32[]{:S(2)}, u32[]{:S(2)}) collective-permute-start(f32[4]{0:T(128)} %pad_maximum_fusion.9), channel_id=1, source_target_pairs={{0,1},{1,0},{2,3},{3,2},{4,5},{5,4},{6,7},{7,6},{8,9},{9,8},{10,11... | collective-permute-start | bytes 56 | tf_op jit(solution)/shard_map/ppermute | solution.py:98
  186.2 63.1 %copy-start.15 = (f32[3,3,9,17]{3,1,2,0:T(4,128)S(1)}, f32[3,3,9,17]{3,1,2,0:T(4,128)}, u32[]{:S(2)}) copy-start(f32[3,3,9,17]{3,1,2,0:T(4,128)} %copy-done.14) | copy-start | bytes 16528
  187.9 61.5 %copy-start.20 = (f32[3,3,9,17]{3,1,2,0:T(4,128)S(1)}, f32[3,3,9,17]{3,1,2,0:T(4,128)}, u32[]{:S(2)}) copy-start(f32[3,3,9,17]{3,1,2,0:T(4,128)} %get-tuple-element.97) | copy-start | bytes 16528
  187.9 61.8 %copy-start.33 = (s32[128]{0:T(128)S(1)}, s32[128]{0:T(128)}, u32[]{:S(2)}) copy-start(s32[128]{0:T(128)} %copy-done.32) | copy-start | bytes 1540
  187.9 61.8 %copy-start.35 = (s32[128]{0:T(128)S(1)}, s32[128]{0:T(128)}, u32[]{:S(2)}) copy-start(s32[128]{0:T(128)} %copy-done.34) | copy-start | bytes 1540
  187.9 61.8 %copy-start.37 = (f32[128]{0:T(128)S(1)}, f32[128]{0:T(128)}, u32[]{:S(2)}) copy-start(f32[128]{0:T(128)} %copy-done.36) | copy-start | bytes 1540
  187.9 61.8 %copy-start.39 = (f32[128]{0:T(128)S(1)}, f32[128]{0:T(128)}, u32[]{:S(2)}) copy-start(f32[128]{0:T(128)} %copy-done.38) | copy-start | bytes 1540
  194.5 3.0 collective-permute-start.5
  200.6 4.0 %collective-permute-start.6 = (f32[4]{0:T(128)S(1)}, f32[4]{0:T(128)S(1)}, u32[]{:S(2)}, u32[]{:S(2)}) collective-permute-start(f32[4]{0:T(128)S(1)} %fusion.210), channel_id=1, source_target_pairs={{0,4},{1,5},{2,6},{3,7},{4,0},{5,1},{6,2},{7,3},{8,12},{9,13},{10,... | collective-permute-start | bytes 56 | tf_op jit(solution)/shard_map/ppermute | solution.py:98
  204.6 4.9 %collective-permute-start.7 = (f32[4]{0:T(128)S(1)}, f32[4]{0:T(128)S(1)}, u32[]{:S(2)}, u32[]{:S(2)}) collective-permute-start(f32[4]{0:T(128)S(1)} %add.452), channel_id=1, source_target_pairs={{0,8},{1,9},{2,10},{3,11},{4,12},{5,13},{6,14},{7,15},{8,0},{9,1},... | collective-permute-start | bytes 56 | tf_op jit(solution)/shard_map/ppermute | solution.py:98
  209.5 4.4 %collective-permute-start.8 = (f32[4]{0:T(128)S(1)}, f32[4]{0:T(128)S(1)}, u32[]{:S(2)}, u32[]{:S(2)}) collective-permute-start(f32[4]{0:T(128)S(1)} %add.453), channel_id=1, source_target_pairs={{0,16},{1,17},{2,18},{3,19},{4,20},{5,21},{6,22},{7,23},{8,24},{9,... | collective-permute-start | bytes 56 | tf_op jit(solution)/shard_map/ppermute | solution.py:98
  213.9 3.4 collective-permute-start.9
  217.3 4.0 %collective-permute-start.10 = (f32[4]{0:T(128)S(1)}, f32[4]{0:T(128)S(1)}, u32[]{:S(2)}, u32[]{:S(2)}) collective-permute-start(f32[4]{0:T(128)S(1)} %add.455), channel_id=1, source_target_pairs={{0,64},{32,96},{64,0},{96,32},{1,65},{33,97},{65,1},{97,33},{2,66}... | collective-permute-start | bytes 56 | tf_op jit(solution)/shard_map/ppermute | solution.py:98
  227.5 24.5 %copy-start.16 = (f32[3,3,9,17]{3,2,1,0:T(8,128)}, f32[3,3,9,17]{3,2,1,0:T(8,128)S(1)}, u32[]{:S(2)}) copy-start(f32[3,3,9,17]{3,2,1,0:T(8,128)S(1)} %convolution_subtract_fusion.2) | copy-start | bytes 16528
  227.6 25.4 %copy-start.23 = (f32[32]{0:T(128)S(1)}, f32[32]{0:T(128)}, u32[]{:S(2)}) copy-start(f32[32]{0:T(128)} %copy-done.21) | copy-start | bytes 388
  227.6 25.4 %copy-start.26 = (f32[32]{0:T(128)S(1)}, f32[32]{0:T(128)}, u32[]{:S(2)}) copy-start(f32[32]{0:T(128)} %copy-done.24) | copy-start | bytes 388
  227.9 13.1 %copy-start.13 = (f32[3,3,9,17]{3,2,1,0:T(8,128)}, f32[3,3,9,17]{3,2,1,0:T(8,128)S(1)}, u32[]{:S(2)}) copy-start(f32[3,3,9,17]{3,2,1,0:T(8,128)S(1)} %fusion.79) | copy-start | bytes 16528
  227.9 10.0 %collective-permute-start.11 = (f32[3,9,17]{2,1,0:T(8,128)S(1)}, f32[3,9,17]{2,1,0:T(8,128)S(1)}, u32[]{:S(2)}, u32[]{:S(2)}) collective-permute-start(f32[3,9,17]{2,1,0:T(8,128)S(1)} %get-tuple-element.67), channel_id=1, source_target_pairs={{0,1},{1,2},{2,3},{3,4},{4,5},{5,6},{6,7},{7,8},{8,9},{9,10},{10,1... | collective-permute-start | bytes 5516 | tf_op jit(solution)/shard_map/ppermute | solution.py:110
  235.8 5.1 %collective-permute-start.12 = (f32[3,9,17]{2,1,0:T(8,128)S(1)}, f32[3,9,17]{2,1,0:T(8,128)S(1)}, u32[]{:S(2)}, u32[]{:S(2)}) collective-permute-start(f32[3,9,17]{2,1,0:T(8,128)S(1)} %get-tuple-element.68), channel_id=1, source_target_pairs={{1,0},{2,1},{3,2},{4,3},{5,4},{6,5},{7,6},{8,7},{9,8},{10,9},{11,1... | collective-permute-start | bytes 5516 | tf_op jit(solution)/shard_map/ppermute | solution.py:111
  241.1 5.6 %collective-permute-start.13 = (f32[3,3,9]{2,1,0:T(4,128)S(1)}, f32[3,3,9]{2,1,0:T(4,128)S(1)}, u32[]{:S(2)}, u32[]{:S(2)}) collective-permute-start(f32[3,3,9]{2,1,0:T(4,128)S(1)} %get-tuple-element.27), channel_id=1, source_target_pairs={{0,32},{32,64},{64,96},{1,33},{33,65},{65,97},{2,34},{34,66},{66,9... | collective-permute-start | bytes 980 | tf_op jit(solution)/shard_map/ppermute | solution.py:110
  244.7 4.4 %collective-permute-start.14 = (f32[3,3,9]{2,1,0:T(4,128)S(1)}, f32[3,3,9]{2,1,0:T(4,128)S(1)}, u32[]{:S(2)}, u32[]{:S(2)}) collective-permute-start(f32[3,3,9]{2,1,0:T(4,128)S(1)} %get-tuple-element.28), channel_id=1, source_target_pairs={{32,0},{64,32},{96,64},{33,1},{65,33},{97,65},{34,2},{66,34},{98,6... | collective-permute-start | bytes 980 | tf_op jit(solution)/shard_map/ppermute | solution.py:111
  253.0 8.6 %copy-start.2 = (f32[32,128,256]{1,0,2:T(8,128)S(1)}, f32[32,128,256]{1,0,2:T(8,128)}, u32[]{:S(2)}) copy-start(f32[32,128,256]{1,0,2:T(8,128)} %get-tuple-element.36) | copy-start | bytes 12582916
  253.0 8.6 %copy-start.4 = (f32[32,128,256]{1,0,2:T(8,128)S(1)}, f32[32,128,256]{1,0,2:T(8,128)}, u32[]{:S(2)}) copy-start(f32[32,128,256]{1,0,2:T(8,128)} %get-tuple-element.37) | copy-start | bytes 12582916
  253.0 8.7 %copy-start.6 = (f32[32,128,256]{1,0,2:T(8,128)S(1)}, f32[32,128,256]{1,0,2:T(8,128)}, u32[]{:S(2)}) copy-start(f32[32,128,256]{1,0,2:T(8,128)} %get-tuple-element.35) | copy-start | bytes 12582916
  273.8 35.8 %copy-start.8 = (f32[32,128,256]{1,0,2:T(8,128)S(1)}, f32[32,128,256]{1,0,2:T(8,128)}, u32[]{:S(2)}) copy-start(f32[32,128,256]{1,0,2:T(8,128)} %get-tuple-element.30) | copy-start | bytes 12582916
  279.2 1.2 collective-permute-start.15
  281.7 2.4 collective-permute-start.16
  285.6 6.7 %collective-permute-start.17 = (f32[2]{0:T(128)S(1)}, f32[2]{0:T(128)S(1)}, u32[]{:S(2)}, u32[]{:S(2)}) collective-permute-start(f32[2]{0:T(128)S(1)} %fusion.209), channel_id=1, source_target_pairs={{0,4},{1,5},{2,6},{3,7},{4,0},{5,1},{6,2},{7,3},{8,12},{9,13},{10,... | collective-permute-start | bytes 32 | tf_op jit(solution)/shard_map/ppermute | solution.py:98
  292.3 3.0 collective-permute-start.18
  295.3 4.4 %collective-permute-start.19 = (f32[2]{0:T(128)S(1)}, f32[2]{0:T(128)S(1)}, u32[]{:S(2)}, u32[]{:S(2)}) collective-permute-start(f32[2]{0:T(128)S(1)} %add.474), channel_id=1, source_target_pairs={{0,16},{1,17},{2,18},{3,19},{4,20},{5,21},{6,22},{7,23},{8,24},{9,... | collective-permute-start | bytes 32 | tf_op jit(solution)/shard_map/ppermute | solution.py:98
  299.7 2.4 collective-permute-start.20
  302.1 4.2 %collective-permute-start.21 = (f32[2]{0:T(128)S(1)}, f32[2]{0:T(128)S(1)}, u32[]{:S(2)}, u32[]{:S(2)}) collective-permute-start(f32[2]{0:T(128)S(1)} %add.476), channel_id=1, source_target_pairs={{0,64},{32,96},{64,0},{96,32},{1,65},{33,97},{65,1},{97,33},{2,66}... | collective-permute-start | bytes 32 | tf_op jit(solution)/shard_map/ppermute | solution.py:98
  (14 other events, 61.3 us)

commit v2 on v0

--- a/solution.py
+++ b/solution.py
@@ -2,6 +2,8 @@
 import jax.numpy as jnp
 from jax import lax
 from jax.sharding import PartitionSpec as P
+from jax.experimental import pallas as pl
+from jax.experimental.pallas import tpu as pltpu
 
 E = 16
 SMAX = 8
@@ -22,6 +24,73 @@
         after = lax.ppermute(initial, axis, down)
         shard = jnp.concatenate([before, shard, after], axis=dim)
     return shard
+
+
+from jax.experimental import pallas as pl
+from jax.experimental.pallas import tpu as pltpu
+
+PLANES = 8
+
+
+def _native_kernel(offset_ref, w_ref, lo_ref, hi_ref, sl_ref, sm_ref):
+    step = pl.program_id(0)
+    _, wy, wz = w_ref.shape
+    row = lax.broadcasted_iota(jnp.int32, (wy, wz), 0)
+    lane = lax.broadcasted_iota(jnp.int32, (wy, wz), 1)
+    sixth = 1.0 / 6.0
+    base = offset_ref[0] + SMAX + step * PLANES
+
+    def planes(t):
+        p = base + t
+        w = w_ref[p].astype(jnp.float32)
+        below = jnp.where(lane == 0, lo_ref[p].astype(jnp.float32), pltpu.roll(w, 1, 1))
+        above = jnp.where(lane == wz - 1, hi_ref[p].astype(jnp.float32), pltpu.roll(w, wz - 1, 1))
+        smooth_z = (below + 4.0 * w + above) * sixth
+        differ_z = 0.5 * (above - below)
+        s_lo = jnp.where(row == 0, 0.0, pltpu.roll(smooth_z, 1, 0))
+        s_hi = jnp.where(row == wy - 1, 0.0, pltpu.roll(smooth_z, wy - 1, 0))
+        d_lo = jnp.where(row == 0, 0.0, pltpu.roll(differ_z, 1, 0))
+        d_hi = jnp.where(row == wy - 1, 0.0, pltpu.roll(differ_z, wy - 1, 0))
+        return (
+            (s_lo + 4.0 * smooth_z + s_hi) * sixth,
+            0.5 * (s_hi - s_lo),
+            (d_lo + 4.0 * differ_z + d_hi) * sixth,
+            w,
+        )
+
+    window = [planes(0), planes(1)]
+    for k in range(PLANES):
+        window.append(planes(k + 2))
+        prev, mid, nxt = window[k], window[k + 1], window[k + 2]
+        sl_ref[0, k] = 0.5 * (nxt[0] - prev[0])
+        sl_ref[1, k] = (prev[1] + 4.0 * mid[1] + nxt[1]) * sixth
+        sl_ref[2, k] = (prev[2] + 4.0 * mid[2] + nxt[2]) * sixth
+        sm_ref[k] = mid[3]
+
+
+def native_slopes(offset, widened, below, above, width_x, interpret=False):
+    _, wy, wz = widened.shape
+    assert width_x % PLANES == 0
+    whole = pl.BlockSpec(widened.shape, lambda i, o: (0, 0, 0))
+    face = pl.BlockSpec(below.shape, lambda i, o: (0, 0, 0))
+    spec = pltpu.PrefetchScalarGridSpec(
+        num_scalar_prefetch=1,
+        grid=(width_x // PLANES,),
+        in_specs=[whole, face, face],
+        out_specs=[
+            pl.BlockSpec((3, PLANES, wy, wz), lambda i, o: (0, i, 0, 0)),
+            pl.BlockSpec((PLANES, wy, wz), lambda i, o: (i, 0, 0)),
+        ],
+    )
+    return pl.pallas_call(
+        _native_kernel,
+        grid_spec=spec,
+        out_shape=[
+            jax.ShapeDtypeStruct((3, width_x, wy, wz), jnp.float32),
+            jax.ShapeDtypeStruct((width_x, wy, wz), jnp.float32),
+        ],
+        interpret=interpret,
+    )(offset, widened, below, above)
 
 
 def hat_matrix(voxels, nodes):
@@ -135,11 +204,11 @@
     margin = SMAX + 1
     offset = shifts[0, 0]
     widened = with_halo(def_volume, (("dev", 0),), margin)
-    framed = with_halo(widened, (("grp", 2),), 1)
-    window = lax.dynamic_slice_in_dim(framed, offset + margin - 1, width_x + 2, 0)
-    window = jnp.pad(window, ((0, 0), (1, 1), (0, 0))).astype(jnp.float32)
-    slopes = gradients(window)
-    sample = window[1:-1, 1:-1, 1:-1]
+    up = [(i, i + 1) for i in range(grp_count - 1)]
+    down = [(j, i) for i, j in up]
+    below = lax.ppermute(widened[:, :, -1:], "grp", up)
+    above = lax.ppermute(widened[:, :, :1], "grp", down)
+    slopes, sample = native_slopes(offset.reshape(1), widened, below, above, width_x)
     target = ref_volume.astype(jnp.float32)
     elements_x = width_x // E
     elements_z = depth_z // E

time: 336 us -> 231 us (0.69); the launches traced: 332 us -> 230 us
  other arithmetic: 153 us -> 46.7 us
  Pallas kernels: 0 us -> 13.1 us
  local copies, waits for them, and re-layouts: 34.6 us -> 23.7 us
  waiting for transfers between devices: 18 us -> 26.4 us
  starting transfers between devices: 61.1 us -> 56.6 us
    div x3 -> x0, other arithmetic: 36.1 us -> none  [smooth(): return (lower + 4.0 * middle + upper) / 6.0]
    reduce_sum x2, other arithmetic: 30.8 us -> 7.3 us  [restrict(): jnp.sum(terms * hat_x[None, :, i, None, None], axis=1)]
    another operation x2 -> x0, other arithmetic: 18.8 us -> none  [gradients(): return jnp.stack([slope_x, slope_y, slope_z])]
    pallas_call x0 -> x1, Pallas kernels: none -> 13.1 us  [native_slopes(): pl.pallas_call(_native_kernel, grid_spec=spec, out_shape=[jax.ShapeDtypeS...]
    unnamed x72 -> x31, local copies, waits for them, and re-layouts: 13.7 us -> 4.88 us
    mul x9 -> x3, local copies, waits for them, and re-layouts: 7.74 us -> 0.2 us  [expand_x(): hat_x[None, :, i, None, None] * partial_y[:, i, None]]
    concatenate x2 -> x0, other arithmetic: 7.44 us -> none  [with_halo(): shard = jnp.concatenate([before, shard, after], axis=dim)]
    slice x1 -> x4, local copies, waits for them, and re-layouts: 2.15 us -> 9.07 us  [the longest x2 4.57 us: local(): above = lax.ppermute(widened[:, :, :1], 'grp', down)]
  transfers between devices with their start and end apart: 22 -> 22, of which waited for: 16 -> 19; matrix products, arithmetic and copies ran while one was open for 7% -> 4% of each run, Pallas kernels for 0% -> 0%
where the time goes in v2:
time: 231 us; the launch traced here: 230 us
  starting transfers between devices  56.6 us (25%)
  other arithmetic  46.7 us (20%)
  blocking collectives  42.6 us (18%)
  waiting for transfers between devices  26.4 us (11%)
  local copies, waits for them, and re-layouts  23.7 us (10%)
  Pallas kernels  13.1 us (6%)
  between operations  11.5 us (5%)
  matrix products  9.32 us (4%)
    all_gather x1, blocking collectives, local(): lax.all_gather(packed.reshape(2, -1), ('grp', 'dev'))  42.6 us
    ppermute x14, starting transfers between devices, allsum(): values = values + lax.ppermute(values, axis, pairs)  30.6 us
    reduce_sum x2, other arithmetic, local(): warped = sample + jnp.sum(shift_field * slopes, axis=0)  16.4 us
    ppermute x14, waiting for transfers between devices, allsum(): values = values + lax.ppermute(values, axis, pairs)  16.2 us
    pallas_call x1, Pallas kernels, native_slopes(): pl.pallas_call(_native_kernel, grid_spec=spec, out_shape=[jax.ShapeDtypeS...  13.1 us
    ppermute x2, starting transfers between devices, share_nodes(): before = lax.ppermute(last, axis, up)  11.9 us
    add x14, other arithmetic, allsum(): values = values + lax.ppermute(values, axis, pairs)  8.07 us
    reduce_sum x2, other arithmetic, restrict(): jnp.sum(terms * hat_x[None, :, i, None, None], axis=1)  7.3 us
  transfers between devices with their start and end apart: 22, of which 19 were waited for; matrix products, arithmetic and copies ran while one was open for 4% of the time, Pallas kernels for 0%

profile of v2, /device:TPU:1, one launch (start us, length us, event | category | flops | bytes accessed | tf_op | source)
XLA Modules:
  0.0 230.0 jit_solution(15458566595629994423)
XLA Ops:
  0.6 2.5 %fusion.107 = (bf16[9,128,256]{2,1,0:T(8,128)(2,1)}, bf16[9,128,256]{2,1,0:T(8,128)(2,1)}) fusion(bf16[32,128,256]{2,1,0:T(8,128)(2,1)} %param.6), kind=kLoop, calls=%fused_computation.181 | loop fusion | bytes 2359296 | tf_op jit(solution)/shard_map/slice | solution.py:22
  3.1 4.5 %collective-permute-start = (bf16[9,128,256]{2,1,0:T(8,128)(2,1)}, bf16[9,128,256]{2,1,0:T(8,128)(2,1)}, u32[]{:S(2)}, u32[]{:S(2)}) collective-permute-start(bf16[9,128,256]{2,1,0:T(8,128)(2,1)} %get-tuple-element.28), channel_id=1, source_target_pairs={{0,1},{1,2},{2,3},{3,4},{4,5},{5,6},{6,7},{7,8},{8,9},{9,10},{10,1... | collective-permute-start | bytes 1769480 | tf_op jit(solution)/shard_map/ppermute | solution.py:23
  7.6 1.9 collective-permute-start.1
  9.7 1.3 constant_dynamic-slice_fusion
  12.6 1.8 convert_reduce_fusion
  16.0 3.1 %collective-permute-done.1 = bf16[9,128,256]{2,1,0:T(8,128)(2,1)} collective-permute-done((bf16[9,128,256]{2,1,0:T(8,128)(2,1)}, bf16[9,128,256]{2,1,0:T(8,128)(2,1)}, u32[]{:S(2)}, u32[]{:S(2)}) %collective-permute-start.1) | collective-permute-done | bytes 589856 | tf_op jit(solution)/shard_map/ppermute | solution.py:24
  20.3 1.7 copy-done.4
  21.9 2.6 %fusion.106 = (bf16[50,128,1]{2,1,0:T(8,128)(2,1)}, bf16[50,128,1]{2,1,0:T(8,128)(2,1)}) fusion(bf16[50,128,256]{2,1,0:T(8,128)(2,1)S(1)} %constant_dynamic-update-slice_fusion.w_ref), kind=kLoop, calls=%fused_computation.180 | loop fusion | bytes 51200 | tf_op jit(solution)/shard_map/slice | solution.py:210
  24.5 2.0 copy.34
  26.5 3.2 %collective-permute-start.2 = (bf16[50,128,1]{1,0,2:T(8,128)(2,1)S(1)}, bf16[50,128,1]{1,0,2:T(8,128)(2,1)S(1)}, u32[]{:S(2)}, u32[]{:S(2)}) collective-permute-start(bf16[50,128,1]{1,0,2:T(8,128)(2,1)S(1)} %copy.34), channel_id=1, source_target_pairs={{0,32},{32,64},{64,96},{1,33},{33,65},{65,97},{2,34},{34,66},{66,9... | collective-permute-start | bytes 38408 | tf_op jit(solution)/shard_map/ppermute | solution.py:209
  29.7 2.0 copy.35
  33.7 1.7 copy.36.lo_ref
  36.2 1.7 copy.37.hi_ref
  37.9 13.1 %shard_map.76 = (f32[3,32,128,256]{3,2,1,0:T(8,128)}, f32[32,128,256]{2,1,0:T(8,128)}) custom-call(s32[1]{0:T(128)} %bitcast.118.offset_ref, bf16[50,128,256]{2,1,0:T(8,128)(2,1)} %copy-done.4, bf16[50,128,1]{2,1,0:T(8,128)(2,1)} %copy.36.lo_ref, bf16[50,128,1]{2,1,0:T(8,128)(2,1)} %copy.37.hi_ref), custom_call_target="tpu_custom_call" | custom-call | tf_op jit(solution)/shard_map/pallas_call | solution.py:85
  51.0 8.2 %multiply_reduce_fusion.7 = f32[32,128,256]{2,1,0:T(8,128)S(1)} fusion(f32[3,32,128,256]{3,2,1,0:T(8,128)} %get-tuple-element.5, f32[3,128,256]{2,1,0:T(8,128)S(1)} %get-tuple-element.33, f32[32]{0:T(128)S(1)} %get-tuple-element.41, f32[3,128,256]{2,1,0:T(8,128)S(1)} %get-tuple-element.34, f32[32]{0:T(128)S(1)} %get-tuple-element.42, ...), kind=kLoop, calls=%fused_computation.7 | loop fusion | flops 20971520 | bytes 17957248 | tf_op jit(solution)/shard_map/reduce_sum | solution.py:229
  59.2 2.2 fusion.104
  61.4 2.9 %pad_maximum_fusion.2 = f32[4]{0:T(128)S(1)} fusion(f32[1]{0:T(128)} %bitcast.18, f32[1]{0:T(128)} %bitcast.17, f32[1]{0:T(128)} %bitcast.6, f32[1]{0:T(128)} %bitcast.5), kind=kLoop, calls=%fused_computation.150 | loop fusion | flops 12 | bytes 32 | tf_op jit(solution)/shard_map/concatenate | solution.py:232
  65.5 2.7 %fusion.116 = f32[4]{0:T(128)S(1)} fusion(f32[4]{0:T(128)S(1)} %collective-permute-done.4, f32[1]{0:T(128)} %bitcast.18, f32[1]{0:T(128)} %bitcast.17, f32[1]{0:T(128)} %bitcast.6, f32[1]{0:T(128)} %bitcast.5), kind=kLoop, calls=%fused_computation.185 | loop fusion | flops 16 | bytes 48 | tf_op jit(solution)/shard_map/add | solution.py:167
  70.6 2.7 %fusion.118 = f32[4]{0:T(128)S(1)} fusion(f32[4]{0:T(128)S(1)} %collective-permute-done.5, f32[4]{0:T(128)S(1)} %collective-permute-done.4, f32[1]{0:T(128)} %bitcast.18, f32[1]{0:T(128)} %bitcast.17, f32[1]{0:T(128)} %bitcast.6, f32[1]{0:T(128)} %bitcast.5), kind=kLoop, calls=%fused_computation.187 | loop fusion | flops 20 | bytes 64 | tf_op jit(solution)/shard_map/add | solution.py:167
  73.2 4.7 %collective-permute-start.6 = (f32[4]{0:T(128)S(1)}, f32[4]{0:T(128)S(1)}, u32[]{:S(2)}, u32[]{:S(2)}) collective-permute-start(f32[4]{0:T(128)S(1)} %fusion.118), channel_id=1, source_target_pairs={{0,4},{1,5},{2,6},{3,7},{4,0},{5,1},{6,2},{7,3},{8,12},{9,13},{10,... | collective-permute-start | bytes 56 | tf_op jit(solution)/shard_map/ppermute | solution.py:167
  78.9 1.9 collective-permute-start.7
  81.7 3.4 %collective-permute-start.8 = (f32[4]{0:T(128)S(1)}, f32[4]{0:T(128)S(1)}, u32[]{:S(2)}, u32[]{:S(2)}) collective-permute-start(f32[4]{0:T(128)S(1)} %add.330), channel_id=1, source_target_pairs={{0,16},{1,17},{2,18},{3,19},{4,20},{5,21},{6,22},{7,23},{8,24},{9,... | collective-permute-start | bytes 56 | tf_op jit(solution)/shard_map/ppermute | solution.py:167
  86.1 1.3 collective-permute-start.9
  88.5 2.6 %collective-permute-start.10 = (f32[4]{0:T(128)S(1)}, f32[4]{0:T(128)S(1)}, u32[]{:S(2)}, u32[]{:S(2)}) collective-permute-start(f32[4]{0:T(128)S(1)} %add.332), channel_id=1, source_target_pairs={{0,64},{32,96},{64,0},{96,32},{1,65},{33,97},{65,1},{97,33},{2,66}... | collective-permute-start | bytes 56 | tf_op jit(solution)/shard_map/ppermute | solution.py:167
  91.2 1.3 collective-permute-done.10
  100.4 3.6 %multiply_reduce_fusion.6 = (f32[3,128,256]{2,1,0:T(8,128)S(1)}, f32[3,128,256]{2,1,0:T(8,128)S(1)}, f32[3,128,256]{2,1,0:T(8,128)S(1)}) fusion(f32[3,32,128,256]{3,2,1,0:T(8,128)S(1)} %bitcast.120, f32[32,128,256]{2,1,0:T(8,128)S(1)} %fusion.1, f32[32]{0:T(128)S(1)} %get-tuple-element.40, f32[32]{0:T(128)S(1)} %get-tuple-element.42, f32[32]{0:T(128)S(1)} %get-tuple-element.41), kind=kLoop, calls=%fused_computation.6 | loop fusion | flops 21725184 | bytes 17957248 | tf_op jit(solution)/shard_map/reduce_sum | solution.py:146
  104.9 8.6 %collective-permute-start.11 = (f32[3,9,17]{2,1,0:T(8,128)S(1)}, f32[3,9,17]{2,1,0:T(8,128)S(1)}, u32[]{:S(2)}, u32[]{:S(2)}) collective-permute-start(f32[3,9,17]{2,1,0:T(8,128)S(1)} %get-tuple-element.37), channel_id=1, source_target_pairs={{0,1},{1,2},{2,3},{3,4},{4,5},{5,6},{6,7},{7,8},{8,9},{9,10},{10,1... | collective-permute-start | bytes 5516 | tf_op jit(solution)/shard_map/ppermute | solution.py:179
  113.5 1.9 collective-permute-start.12
  115.5 3.2 %collective-permute-done.12 = f32[3,9,17]{2,1,0:T(8,128)S(1)} collective-permute-done((f32[3,9,17]{2,1,0:T(8,128)S(1)}, f32[3,9,17]{2,1,0:T(8,128)S(1)}, u32[]{:S(2)}, u32[]{:S(2)}) %collective-permute-start.12) | collective-permute-done | bytes 1868 | tf_op jit(solution)/shard_map/ppermute | solution.py:180
  118.9 3.2 %collective-permute-start.13 = (f32[3,3,9]{2,1,0:T(4,128)S(1)}, f32[3,3,9]{2,1,0:T(4,128)S(1)}, u32[]{:S(2)}, u32[]{:S(2)}) collective-permute-start(f32[3,3,9]{2,1,0:T(4,128)S(1)} %get-tuple-element.19), channel_id=1, source_target_pairs={{0,32},{32,64},{64,96},{1,33},{33,65},{65,97},{2,34},{34,66},{66,9... | collective-permute-start | bytes 980 | tf_op jit(solution)/shard_map/ppermute | solution.py:179
  123.7 2.8 %collective-permute-done.14 = f32[3,3,9]{2,1,0:T(4,128)S(1)} collective-permute-done((f32[3,3,9]{2,1,0:T(4,128)S(1)}, f32[3,3,9]{2,1,0:T(4,128)S(1)}, u32[]{:S(2)}, u32[]{:S(2)}) %collective-permute-start.14) | collective-permute-done | bytes 356 | tf_op jit(solution)/shard_map/ppermute | solution.py:180
  128.3 8.2 %multiply_reduce_fusion.3 = f32[32,128,256]{2,1,0:T(8,128)S(1)} fusion(f32[3,32,128,256]{3,2,1,0:T(8,128)} %get-tuple-element.5, f32[3,128,256]{2,1,0:T(8,128)S(1)} %get-tuple-element.30, f32[3,128,256]{2,1,0:T(8,128)S(1)} %get-tuple-element.31, f32[3,128,256]{2,1,0:T(8,128)S(1)} %get-tuple-element.29, f32[32]{0:T(128)S(1)} %get-tuple-element.41, ...), kind=kLoop, calls=%fused_computation.3 | loop fusion | flops 20971520 | bytes 17957248 | tf_op jit(solution)/shard_map/reduce_sum | solution.py:229
  136.6 2.2 fusion.103
  138.8 1.6 pad_maximum_fusion.3
  141.6 1.4 fusion.115
  142.9 1.8 collective-permute-start.16
  145.7 1.4 fusion.117
  147.1 5.3 %collective-permute-start.17 = (f32[2]{0:T(128)S(1)}, f32[2]{0:T(128)S(1)}, u32[]{:S(2)}, u32[]{:S(2)}) collective-permute-start(f32[2]{0:T(128)S(1)} %fusion.117), channel_id=1, source_target_pairs={{0,4},{1,5},{2,6},{3,7},{4,0},{5,1},{6,2},{7,3},{8,12},{9,13},{10,... | collective-permute-start | bytes 32 | tf_op jit(solution)/shard_map/ppermute | solution.py:167
  153.3 2.1 collective-permute-start.18
  156.4 3.4 %collective-permute-start.19 = (f32[2]{0:T(128)S(1)}, f32[2]{0:T(128)S(1)}, u32[]{:S(2)}, u32[]{:S(2)}) collective-permute-start(f32[2]{0:T(128)S(1)} %add.349), channel_id=1, source_target_pairs={{0,16},{1,17},{2,18},{3,19},{4,20},{5,21},{6,22},{7,23},{8,24},{9,... | collective-permute-start | bytes 32 | tf_op jit(solution)/shard_map/ppermute | solution.py:167
  161.8 1.4 collective-permute-done.20
  163.2 1.8 collective-permute-start.21
  165.0 2.1 collective-permute-done.21
  170.4 1.8 multiply_reduce_fusion.8
  172.6 3.7 %multiply_reduce_fusion.2 = (f32[3,128,256]{2,1,0:T(8,128)S(1)}, f32[3,128,256]{2,1,0:T(8,128)S(1)}, f32[3,128,256]{2,1,0:T(8,128)S(1)}) fusion(f32[3,32,128,256]{3,2,1,0:T(8,128)S(1)} %bitcast.122, f32[32,128,256]{2,1,0:T(8,128)S(1)} %get-tuple-element.22, f32[32]{0:T(128)S(1)} %get-tuple-element.40, f32[32]{0:T(128)S(1)} %get-tuple-element.42, ...), kind=kLoop, calls=%fused_computation.2 | loop fusion | flops 21725184 | bytes 17957248 | tf_op jit(solution)/shard_map/reduce_sum | solution.py:146
  178.1 42.6 %all_gather.3 = f32[128,2,689]{2,1,0:T(2,128)S(1)} all-gather(f32[1,2,689]{2,1,0:T(2,128)S(1)} %all_gather_reshape.3), channel_id=1, replica_groups=mesh['grp'=4,'dev'=32] {'grp','dev'}, dimensions={0}, use_global_device_ids=true | all-gather | bytes 711048 | tf_op jit(solution)/shard_map/all_gather | solution.py:248
  224.2 2.4 %fusion.5 = f32[4,3,65,9,17]{2,4,0,3,1:T(8,128)S(1)} fusion(f32[4,32,3,3,9,17]{1,0,5,4,3,2:T(4,128)S(1)} %reshape.189, s32[32,3]{0,1:T(4,128)S(1)} %iota_add_fusion.1), kind=kOutput, calls=%fused_computation.19 | convolution fusion | flops 137485920 | bytes 1182768 | tf_op jit(solution)/shard_map/pqcijk,qix->pcxjk/dot_general | solution.py:193
  226.6 2.2 fusion.9
  (105 shorter events, 32.9 us)
Async XLA Ops:
  0.6 11.9 %copy-start = (bf16[32,128,256]{2,1,0:T(8,128)(2,1)S(1)}, bf16[32,128,256]{2,1,0:T(8,128)(2,1)}, u32[]{:S(2)}) copy-start(bf16[32,128,256]{2,1,0:T(8,128)(2,1)} %param.5) | copy-start | bytes 6291460
  3.1 11.6 %collective-permute-start = (bf16[9,128,256]{2,1,0:T(8,128)(2,1)}, bf16[9,128,256]{2,1,0:T(8,128)(2,1)}, u32[]{:S(2)}, u32[]{:S(2)}) collective-permute-start(bf16[9,128,256]{2,1,0:T(8,128)(2,1)} %get-tuple-element.28), channel_id=1, source_target_pairs={{0,1},{1,2},{2,3},{3,4},{4,5},{5,6},{6,7},{7,8},{8,9},{9,10},{10,1... | collective-permute-start | bytes 1769480 | tf_op jit(solution)/shard_map/ppermute | solution.py:23
  7.6 11.5 %collective-permute-start.1 = (bf16[9,128,256]{2,1,0:T(8,128)(2,1)}, bf16[9,128,256]{2,1,0:T(8,128)(2,1)}, u32[]{:S(2)}, u32[]{:S(2)}) collective-permute-start(bf16[9,128,256]{2,1,0:T(8,128)(2,1)} %get-tuple-element.27), channel_id=1, source_target_pairs={{1,0},{2,1},{3,2},{4,3},{5,4},{6,5},{7,6},{8,7},{9,8},{10,9},{11,1... | collective-permute-start | bytes 1769480 | tf_op jit(solution)/shard_map/ppermute | solution.py:24
  9.6 6.2 %copy-start.5 = (bf16[32,128,256]{2,1,0:T(8,128)(2,1)S(1)}, bf16[32,128,256]{2,1,0:T(8,128)(2,1)}, u32[]{:S(2)}) copy-start(bf16[32,128,256]{2,1,0:T(8,128)(2,1)} %param.6) | copy-start | bytes 6291460
  20.3 1.7 copy-start.4
  26.5 7.2 %collective-permute-start.2 = (bf16[50,128,1]{1,0,2:T(8,128)(2,1)S(1)}, bf16[50,128,1]{1,0,2:T(8,128)(2,1)S(1)}, u32[]{:S(2)}, u32[]{:S(2)}) collective-permute-start(bf16[50,128,1]{1,0,2:T(8,128)(2,1)S(1)} %copy.34), channel_id=1, source_target_pairs={{0,32},{32,64},{64,96},{1,33},{33,65},{65,97},{2,34},{34,66},{66,9... | collective-permute-start | bytes 38408 | tf_op jit(solution)/shard_map/ppermute | solution.py:209
  31.7 4.5 %collective-permute-start.3 = (bf16[50,128,1]{1,0,2:T(8,128)(2,1)S(1)}, bf16[50,128,1]{1,0,2:T(8,128)(2,1)S(1)}, u32[]{:S(2)}, u32[]{:S(2)}) collective-permute-start(bf16[50,128,1]{1,0,2:T(8,128)(2,1)S(1)} %copy.35), channel_id=1, source_target_pairs={{32,0},{64,32},{96,64},{33,1},{65,33},{97,65},{34,2},{66,34},{98,6... | collective-permute-start | bytes 38408 | tf_op jit(solution)/shard_map/ppermute | solution.py:210
  51.0 8.2 %copy-start.1 = (f32[32,128,256]{2,1,0:T(8,128)S(1)}, f32[32,128,256]{2,1,0:T(8,128)}, u32[]{:S(2)}) copy-start(f32[32,128,256]{2,1,0:T(8,128)} %get-tuple-element.6) | copy-start | bytes 12582916
  59.2 39.9 %slice-start = ((s8[12582912]{0:T(1024)(128)(4,1)}), s8[4194304]{0:T(1024)(128)(4,1)S(1)}, s32[]{:S(2)}) async-start(s8[12582912]{0:T(1024)(128)(4,1)} %bitcast.119), calls=%async_computation | async-start | bytes 8388608
  59.2 39.9 %slice-start.1 = ((s8[12582912]{0:T(1024)(128)(4,1)}), s8[4194304]{0:T(1024)(128)(4,1)S(1)}, s32[]{:S(2)}) async-start(s8[12582912]{0:T(1024)(128)(4,1)} %bitcast.119), calls=%async_computation.1 | async-start | bytes 8388608
  64.3 1.2 collective-permute-start.4
  68.1 2.4 %collective-permute-start.5 = (f32[4]{0:T(128)S(1)}, f32[4]{0:T(128)S(1)}, u32[]{:S(2)}, u32[]{:S(2)}) collective-permute-start(f32[4]{0:T(128)S(1)} %fusion.116), channel_id=1, source_target_pairs={{0,2},{1,3},{2,0},{3,1},{4,6},{5,7},{6,4},{7,5},{8,10},{9,11},{10,... | collective-permute-start | bytes 56 | tf_op jit(solution)/shard_map/ppermute | solution.py:167
  73.2 5.6 %collective-permute-start.6 = (f32[4]{0:T(128)S(1)}, f32[4]{0:T(128)S(1)}, u32[]{:S(2)}, u32[]{:S(2)}) collective-permute-start(f32[4]{0:T(128)S(1)} %fusion.118), channel_id=1, source_target_pairs={{0,4},{1,5},{2,6},{3,7},{4,0},{5,1},{6,2},{7,3},{8,12},{9,13},{10,... | collective-permute-start | bytes 56 | tf_op jit(solution)/shard_map/ppermute | solution.py:167
  78.9 2.8 %collective-permute-start.7 = (f32[4]{0:T(128)S(1)}, f32[4]{0:T(128)S(1)}, u32[]{:S(2)}, u32[]{:S(2)}) collective-permute-start(f32[4]{0:T(128)S(1)} %add.329), channel_id=1, source_target_pairs={{0,8},{1,9},{2,10},{3,11},{4,12},{5,13},{6,14},{7,15},{8,0},{9,1},... | collective-permute-start | bytes 56 | tf_op jit(solution)/shard_map/ppermute | solution.py:167
  81.7 4.4 %collective-permute-start.8 = (f32[4]{0:T(128)S(1)}, f32[4]{0:T(128)S(1)}, u32[]{:S(2)}, u32[]{:S(2)}) collective-permute-start(f32[4]{0:T(128)S(1)} %add.330), channel_id=1, source_target_pairs={{0,16},{1,17},{2,18},{3,19},{4,20},{5,21},{6,22},{7,23},{8,24},{9,... | collective-permute-start | bytes 56 | tf_op jit(solution)/shard_map/ppermute | solution.py:167
  86.1 2.4 %collective-permute-start.9 = (f32[4]{0:T(128)S(1)}, f32[4]{0:T(128)S(1)}, u32[]{:S(2)}, u32[]{:S(2)}) collective-permute-start(f32[4]{0:T(128)S(1)} %add.331), channel_id=1, source_target_pairs={{0,32},{32,0},{64,96},{96,64},{1,33},{33,1},{65,97},{97,65},{2,34}... | collective-permute-start | bytes 56 | tf_op jit(solution)/shard_map/ppermute | solution.py:167
  88.5 3.9 %collective-permute-start.10 = (f32[4]{0:T(128)S(1)}, f32[4]{0:T(128)S(1)}, u32[]{:S(2)}, u32[]{:S(2)}) collective-permute-start(f32[4]{0:T(128)S(1)} %add.332), channel_id=1, source_target_pairs={{0,64},{32,96},{64,0},{96,32},{1,65},{33,97},{65,1},{97,33},{2,66}... | collective-permute-start | bytes 56 | tf_op jit(solution)/shard_map/ppermute | solution.py:167
  98.2 2.2 slice-start.2
  104.9 10.6 %collective-permute-start.11 = (f32[3,9,17]{2,1,0:T(8,128)S(1)}, f32[3,9,17]{2,1,0:T(8,128)S(1)}, u32[]{:S(2)}, u32[]{:S(2)}) collective-permute-start(f32[3,9,17]{2,1,0:T(8,128)S(1)} %get-tuple-element.37), channel_id=1, source_target_pairs={{0,1},{1,2},{2,3},{3,4},{4,5},{5,6},{6,7},{7,8},{8,9},{9,10},{10,1... | collective-permute-start | bytes 5516 | tf_op jit(solution)/shard_map/ppermute | solution.py:179
  113.5 5.1 %collective-permute-start.12 = (f32[3,9,17]{2,1,0:T(8,128)S(1)}, f32[3,9,17]{2,1,0:T(8,128)S(1)}, u32[]{:S(2)}, u32[]{:S(2)}) collective-permute-start(f32[3,9,17]{2,1,0:T(8,128)S(1)} %get-tuple-element.38), channel_id=1, source_target_pairs={{1,0},{2,1},{3,2},{4,3},{5,4},{6,5},{7,6},{8,7},{9,8},{10,9},{11,1... | collective-permute-start | bytes 5516 | tf_op jit(solution)/shard_map/ppermute | solution.py:180
  118.9 4.7 %collective-permute-start.13 = (f32[3,3,9]{2,1,0:T(4,128)S(1)}, f32[3,3,9]{2,1,0:T(4,128)S(1)}, u32[]{:S(2)}, u32[]{:S(2)}) collective-permute-start(f32[3,3,9]{2,1,0:T(4,128)S(1)} %get-tuple-element.19), channel_id=1, source_target_pairs={{0,32},{32,64},{64,96},{1,33},{33,65},{65,97},{2,34},{34,66},{66,9... | collective-permute-start | bytes 980 | tf_op jit(solution)/shard_map/ppermute | solution.py:179
  122.1 4.4 %collective-permute-start.14 = (f32[3,3,9]{2,1,0:T(4,128)S(1)}, f32[3,3,9]{2,1,0:T(4,128)S(1)}, u32[]{:S(2)}, u32[]{:S(2)}) collective-permute-start(f32[3,3,9]{2,1,0:T(4,128)S(1)} %get-tuple-element.20), channel_id=1, source_target_pairs={{32,0},{64,32},{96,64},{33,1},{65,33},{97,65},{34,2},{66,34},{98,6... | collective-permute-start | bytes 980 | tf_op jit(solution)/shard_map/ppermute | solution.py:180
  128.3 8.2 %copy-start.2 = (f32[32,128,256]{2,1,0:T(8,128)S(1)}, f32[32,128,256]{2,1,0:T(8,128)}, u32[]{:S(2)}) copy-start(f32[32,128,256]{2,1,0:T(8,128)} %get-tuple-element.6) | copy-start | bytes 12582916
  136.6 35.6 %slice-start.3 = ((s8[12582912]{0:T(1024)(128)(4,1)}), s8[4194304]{0:T(1024)(128)(4,1)S(1)}, s32[]{:S(2)}) async-start(s8[12582912]{0:T(1024)(128)(4,1)} %bitcast.121), calls=%async_computation.3 | async-start | bytes 8388608
  136.6 35.6 %slice-start.4 = ((s8[12582912]{0:T(1024)(128)(4,1)}), s8[4194304]{0:T(1024)(128)(4,1)S(1)}, s32[]{:S(2)}) async-start(s8[12582912]{0:T(1024)(128)(4,1)} %bitcast.121), calls=%async_computation.4 | async-start | bytes 8388608
  140.4 1.2 collective-permute-start.15
  142.9 2.8 %collective-permute-start.16 = (f32[2]{0:T(128)S(1)}, f32[2]{0:T(128)S(1)}, u32[]{:S(2)}, u32[]{:S(2)}) collective-permute-start(f32[2]{0:T(128)S(1)} %fusion.115), channel_id=1, source_target_pairs={{0,2},{1,3},{2,0},{3,1},{4,6},{5,7},{6,4},{7,5},{8,10},{9,11},{10,... | collective-permute-start | bytes 32 | tf_op jit(solution)/shard_map/ppermute | solution.py:167
  147.1 6.3 %collective-permute-start.17 = (f32[2]{0:T(128)S(1)}, f32[2]{0:T(128)S(1)}, u32[]{:S(2)}, u32[]{:S(2)}) collective-permute-start(f32[2]{0:T(128)S(1)} %fusion.117), channel_id=1, source_target_pairs={{0,4},{1,5},{2,6},{3,7},{4,0},{5,1},{6,2},{7,3},{8,12},{9,13},{10,... | collective-permute-start | bytes 32 | tf_op jit(solution)/shard_map/ppermute | solution.py:167
  153.3 3.0 %collective-permute-start.18 = (f32[2]{0:T(128)S(1)}, f32[2]{0:T(128)S(1)}, u32[]{:S(2)}, u32[]{:S(2)}) collective-permute-start(f32[2]{0:T(128)S(1)} %add.348), channel_id=1, source_target_pairs={{0,8},{1,9},{2,10},{3,11},{4,12},{5,13},{6,14},{7,15},{8,0},{9,1},... | collective-permute-start | bytes 32 | tf_op jit(solution)/shard_map/ppermute | solution.py:167
  156.4 4.4 %collective-permute-start.19 = (f32[2]{0:T(128)S(1)}, f32[2]{0:T(128)S(1)}, u32[]{:S(2)}, u32[]{:S(2)}) collective-permute-start(f32[2]{0:T(128)S(1)} %add.349), channel_id=1, source_target_pairs={{0,16},{1,17},{2,18},{3,19},{4,20},{5,21},{6,22},{7,23},{8,24},{9,... | collective-permute-start | bytes 32 | tf_op jit(solution)/shard_map/ppermute | solution.py:167
  160.8 2.4 %collective-permute-start.20 = (f32[2]{0:T(128)S(1)}, f32[2]{0:T(128)S(1)}, u32[]{:S(2)}, u32[]{:S(2)}) collective-permute-start(f32[2]{0:T(128)S(1)} %add.350), channel_id=1, source_target_pairs={{0,32},{32,0},{64,96},{96,64},{1,33},{33,1},{65,97},{97,65},{2,34}... | collective-permute-start | bytes 32 | tf_op jit(solution)/shard_map/ppermute | solution.py:167
  163.2 3.9 %collective-permute-start.21 = (f32[2]{0:T(128)S(1)}, f32[2]{0:T(128)S(1)}, u32[]{:S(2)}, u32[]{:S(2)}) collective-permute-start(f32[2]{0:T(128)S(1)} %add.351), channel_id=1, source_target_pairs={{0,64},{32,96},{64,0},{96,32},{1,65},{33,97},{65,1},{97,33},{2,66}... | collective-permute-start | bytes 32 | tf_op jit(solution)/shard_map/ppermute | solution.py:167
  170.4 2.2 slice-start.5
  172.2 4.1 %copy-start.3 = (f32[32,128,256]{2,1,0:T(8,128)}, f32[32,128,256]{2,1,0:T(8,128)S(1)}, u32[]{:S(2)}) copy-start(f32[32,128,256]{2,1,0:T(8,128)S(1)} %get-tuple-element.22) | copy-start | bytes 12582916
  224.2 2.4 %copy-start.6 = (f32[3,65,9,65]{3,1,2,0:T(8,128)S(1)}, f32[3,65,9,65]{3,1,2,0:T(8,128)}, u32[]{:S(2)}) copy-start(f32[3,65,9,65]{3,1,2,0:T(8,128)} %param.8) | copy-start | bytes 1368904
  224.2 2.4 %copy-start.7 = (f32[3,65,9,65]{3,1,2,0:T(8,128)S(1)}, f32[3,65,9,65]{3,1,2,0:T(8,128)}, u32[]{:S(2)}) copy-start(f32[3,65,9,65]{3,1,2,0:T(8,128)} %param.9) | copy-start | bytes 1368904

commit v3 on v2

--- a/solution.py
+++ b/solution.py
@@ -32,7 +32,7 @@
 PLANES = 8
 
 
-def _native_kernel(offset_ref, w_ref, lo_ref, hi_ref, sl_ref, sm_ref):
+def _native_kernel(offset_ref, w_ref, lo_ref, hi_ref, sl_ref, sm_ref, keep_ref):
     step = pl.program_id(0)
     _, wy, wz = w_ref.shape
     row = lax.broadcasted_iota(jnp.int32, (wy, wz), 0)
@@ -58,7 +58,13 @@
             w,
         )
 
-    window = [planes(0), planes(1)]
+    @pl.when(step == 0)
+    def _():
+        for t in range(2):
+            for n, value in enumerate(planes(t)):
+                keep_ref[t, n] = value
+
+    window = [tuple(keep_ref[t, n] for n in range(4)) for t in range(2)]
     for k in range(PLANES):
         window.append(planes(k + 2))
         prev, mid, nxt = window[k], window[k + 1], window[k + 2]
@@ -66,6 +72,9 @@
         sl_ref[1, k] = (prev[1] + 4.0 * mid[1] + nxt[1]) * sixth
         sl_ref[2, k] = (prev[2] + 4.0 * mid[2] + nxt[2]) * sixth
         sm_ref[k] = mid[3]
+    for t in range(2):
+        for n, value in enumerate(window[PLANES + t]):
+            keep_ref[t, n] = value
 
 
 def native_slopes(offset, widened, below, above, width_x, interpret=False):
@@ -77,6 +86,7 @@
         num_scalar_prefetch=1,
         grid=(width_x // PLANES,),
         in_specs=[whole, face, face],
+        scratch_shapes=[pltpu.VMEM((2, 4, wy, wz), jnp.float32)],
         out_specs=[
             pl.BlockSpec((3, PLANES, wy, wz), lambda i, o: (0, i, 0, 0)),
             pl.BlockSpec((PLANES, wy, wz), lambda i, o: (i, 0, 0)),

time: 231 us -> 230 us (level)
  no operation moved by 1% of the time
where the time goes in v3:
time: 230 us; the launch traced here: 229 us
  starting transfers between devices  56.6 us (25%)
  other arithmetic  46.7 us (20%)
  blocking collectives  42.6 us (19%)
  waiting for transfers between devices  26.4 us (11%)
  local copies, waits for them, and re-layouts  23.7 us (10%)
  Pallas kernels  12.4 us (5%)
  between operations  11.5 us (5%)
  matrix products  9.32 us (4%)
    all_gather x1, blocking collectives, local(): lax.all_gather(packed.reshape(2, -1), ('grp', 'dev'))  42.6 us
    ppermute x14, starting transfers between devices, allsum(): values = values + lax.ppermute(values, axis, pairs)  30.6 us
    reduce_sum x2, other arithmetic, local(): warped = sample + jnp.sum(shift_field * slopes, axis=0)  16.4 us
    ppermute x14, waiting for transfers between devices, allsum(): values = values + lax.ppermute(values, axis, pairs)  16.2 us
    pallas_call x1, Pallas kernels, native_slopes(): pl.pallas_call(_native_kernel, grid_spec=spec, out_shape=[jax.ShapeDtypeS...  12.4 us
    ppermute x2, starting transfers between devices, share_nodes(): before = lax.ppermute(last, axis, up)  11.9 us
    add x14, other arithmetic, allsum(): values = values + lax.ppermute(values, axis, pairs)  8.07 us
    reduce_sum x2, other arithmetic, restrict(): jnp.sum(terms * hat_x[None, :, i, None, None], axis=1)  7.3 us
  transfers between devices with their start and end apart: 22, of which 19 were waited for; matrix products, arithmetic and copies ran while one was open for 4% of the time, Pallas kernels for 0%

profile of v3, /device:TPU:1, one launch (start us, length us, event | category | flops | bytes accessed | tf_op | source)
XLA Modules:
  0.0 229.3 jit_solution(15185637926401378492)
XLA Ops:
  0.6 2.5 %fusion.107 = (bf16[9,128,256]{2,1,0:T(8,128)(2,1)}, bf16[9,128,256]{2,1,0:T(8,128)(2,1)}) fusion(bf16[32,128,256]{2,1,0:T(8,128)(2,1)} %param.6), kind=kLoop, calls=%fused_computation.181 | loop fusion | bytes 2359296 | tf_op jit(solution)/shard_map/slice | solution.py:22
  3.1 4.5 %collective-permute-start = (bf16[9,128,256]{2,1,0:T(8,128)(2,1)}, bf16[9,128,256]{2,1,0:T(8,128)(2,1)}, u32[]{:S(2)}, u32[]{:S(2)}) collective-permute-start(bf16[9,128,256]{2,1,0:T(8,128)(2,1)} %get-tuple-element.28), channel_id=1, source_target_pairs={{0,1},{1,2},{2,3},{3,4},{4,5},{5,6},{6,7},{7,8},{8,9},{9,10},{10,1... | collective-permute-start | bytes 1769480 | tf_op jit(solution)/shard_map/ppermute | solution.py:23
  7.6 1.9 collective-permute-start.1
  9.7 1.3 constant_dynamic-slice_fusion
  12.6 1.8 convert_reduce_fusion
  16.0 3.1 %collective-permute-done.1 = bf16[9,128,256]{2,1,0:T(8,128)(2,1)} collective-permute-done((bf16[9,128,256]{2,1,0:T(8,128)(2,1)}, bf16[9,128,256]{2,1,0:T(8,128)(2,1)}, u32[]{:S(2)}, u32[]{:S(2)}) %collective-permute-start.1) | collective-permute-done | bytes 589856 | tf_op jit(solution)/shard_map/ppermute | solution.py:24
  20.3 1.7 copy-done.4
  21.9 2.6 %fusion.106 = (bf16[50,128,1]{2,1,0:T(8,128)(2,1)}, bf16[50,128,1]{2,1,0:T(8,128)(2,1)}) fusion(bf16[50,128,256]{2,1,0:T(8,128)(2,1)S(1)} %constant_dynamic-update-slice_fusion.w_ref), kind=kLoop, calls=%fused_computation.180 | loop fusion | bytes 51200 | tf_op jit(solution)/shard_map/slice | solution.py:220
  24.5 2.0 copy.34
  26.5 3.2 %collective-permute-start.2 = (bf16[50,128,1]{1,0,2:T(8,128)(2,1)S(1)}, bf16[50,128,1]{1,0,2:T(8,128)(2,1)S(1)}, u32[]{:S(2)}, u32[]{:S(2)}) collective-permute-start(bf16[50,128,1]{1,0,2:T(8,128)(2,1)S(1)} %copy.34), channel_id=1, source_target_pairs={{0,32},{32,64},{64,96},{1,33},{33,65},{65,97},{2,34},{34,66},{66,9... | collective-permute-start | bytes 38408 | tf_op jit(solution)/shard_map/ppermute | solution.py:219
  29.7 2.0 copy.35
  33.7 1.7 copy.36.lo_ref
  36.2 1.7 copy.37.hi_ref
  37.9 12.4 %shard_map.76 = (f32[3,32,128,256]{3,2,1,0:T(8,128)}, f32[32,128,256]{2,1,0:T(8,128)}) custom-call(s32[1]{0:T(128)} %bitcast.118.offset_ref, bf16[50,128,256]{2,1,0:T(8,128)(2,1)} %copy-done.4, bf16[50,128,1]{2,1,0:T(8,128)(2,1)} %copy.36.lo_ref, bf16[50,128,1]{2,1,0:T(8,128)(2,1)} %copy.37.hi_ref), custom_call_target="tpu_custom_call" | custom-call | tf_op jit(solution)/shard_map/pallas_call | solution.py:95
  50.3 8.2 %multiply_reduce_fusion.7 = f32[32,128,256]{2,1,0:T(8,128)S(1)} fusion(f32[3,32,128,256]{3,2,1,0:T(8,128)} %get-tuple-element.5, f32[3,128,256]{2,1,0:T(8,128)S(1)} %get-tuple-element.33, f32[32]{0:T(128)S(1)} %get-tuple-element.41, f32[3,128,256]{2,1,0:T(8,128)S(1)} %get-tuple-element.34, f32[32]{0:T(128)S(1)} %get-tuple-element.42, ...), kind=kLoop, calls=%fused_computation.7 | loop fusion | flops 20971520 | bytes 17957248 | tf_op jit(solution)/shard_map/reduce_sum | solution.py:239
  58.5 2.2 fusion.104
  60.7 2.9 %pad_maximum_fusion.2 = f32[4]{0:T(128)S(1)} fusion(f32[1]{0:T(128)} %bitcast.18, f32[1]{0:T(128)} %bitcast.17, f32[1]{0:T(128)} %bitcast.6, f32[1]{0:T(128)} %bitcast.5), kind=kLoop, calls=%fused_computation.150 | loop fusion | flops 12 | bytes 32 | tf_op jit(solution)/shard_map/concatenate | solution.py:242
  64.8 2.7 %fusion.116 = f32[4]{0:T(128)S(1)} fusion(f32[4]{0:T(128)S(1)} %collective-permute-done.4, f32[1]{0:T(128)} %bitcast.18, f32[1]{0:T(128)} %bitcast.17, f32[1]{0:T(128)} %bitcast.6, f32[1]{0:T(128)} %bitcast.5), kind=kLoop, calls=%fused_computation.185 | loop fusion | flops 16 | bytes 48 | tf_op jit(solution)/shard_map/add | solution.py:177
  69.9 2.7 %fusion.118 = f32[4]{0:T(128)S(1)} fusion(f32[4]{0:T(128)S(1)} %collective-permute-done.5, f32[4]{0:T(128)S(1)} %collective-permute-done.4, f32[1]{0:T(128)} %bitcast.18, f32[1]{0:T(128)} %bitcast.17, f32[1]{0:T(128)} %bitcast.6, f32[1]{0:T(128)} %bitcast.5), kind=kLoop, calls=%fused_computation.187 | loop fusion | flops 20 | bytes 64 | tf_op jit(solution)/shard_map/add | solution.py:177
  72.6 4.7 %collective-permute-start.6 = (f32[4]{0:T(128)S(1)}, f32[4]{0:T(128)S(1)}, u32[]{:S(2)}, u32[]{:S(2)}) collective-permute-start(f32[4]{0:T(128)S(1)} %fusion.118), channel_id=1, source_target_pairs={{0,4},{1,5},{2,6},{3,7},{4,0},{5,1},{6,2},{7,3},{8,12},{9,13},{10,... | collective-permute-start | bytes 56 | tf_op jit(solution)/shard_map/ppermute | solution.py:177
  78.2 1.9 collective-permute-start.7
  81.0 3.4 %collective-permute-start.8 = (f32[4]{0:T(128)S(1)}, f32[4]{0:T(128)S(1)}, u32[]{:S(2)}, u32[]{:S(2)}) collective-permute-start(f32[4]{0:T(128)S(1)} %add.330), channel_id=1, source_target_pairs={{0,16},{1,17},{2,18},{3,19},{4,20},{5,21},{6,22},{7,23},{8,24},{9,... | collective-permute-start | bytes 56 | tf_op jit(solution)/shard_map/ppermute | solution.py:177
  85.4 1.3 collective-permute-start.9
  87.8 2.6 %collective-permute-start.10 = (f32[4]{0:T(128)S(1)}, f32[4]{0:T(128)S(1)}, u32[]{:S(2)}, u32[]{:S(2)}) collective-permute-start(f32[4]{0:T(128)S(1)} %add.332), channel_id=1, source_target_pairs={{0,64},{32,96},{64,0},{96,32},{1,65},{33,97},{65,1},{97,33},{2,66}... | collective-permute-start | bytes 56 | tf_op jit(solution)/shard_map/ppermute | solution.py:177
  90.5 1.3 collective-permute-done.10
  99.7 3.6 %multiply_reduce_fusion.6 = (f32[3,128,256]{2,1,0:T(8,128)S(1)}, f32[3,128,256]{2,1,0:T(8,128)S(1)}, f32[3,128,256]{2,1,0:T(8,128)S(1)}) fusion(f32[3,32,128,256]{3,2,1,0:T(8,128)S(1)} %bitcast.120, f32[32,128,256]{2,1,0:T(8,128)S(1)} %fusion.1, f32[32]{0:T(128)S(1)} %get-tuple-element.40, f32[32]{0:T(128)S(1)} %get-tuple-element.42, f32[32]{0:T(128)S(1)} %get-tuple-element.41), kind=kLoop, calls=%fused_computation.6 | loop fusion | flops 21725184 | bytes 17957248 | tf_op jit(solution)/shard_map/reduce_sum | solution.py:156
  104.2 8.6 %collective-permute-start.11 = (f32[3,9,17]{2,1,0:T(8,128)S(1)}, f32[3,9,17]{2,1,0:T(8,128)S(1)}, u32[]{:S(2)}, u32[]{:S(2)}) collective-permute-start(f32[3,9,17]{2,1,0:T(8,128)S(1)} %get-tuple-element.37), channel_id=1, source_target_pairs={{0,1},{1,2},{2,3},{3,4},{4,5},{5,6},{6,7},{7,8},{8,9},{9,10},{10,1... | collective-permute-start | bytes 5516 | tf_op jit(solution)/shard_map/ppermute | solution.py:189
  112.8 1.9 collective-permute-start.12
  114.8 3.2 %collective-permute-done.12 = f32[3,9,17]{2,1,0:T(8,128)S(1)} collective-permute-done((f32[3,9,17]{2,1,0:T(8,128)S(1)}, f32[3,9,17]{2,1,0:T(8,128)S(1)}, u32[]{:S(2)}, u32[]{:S(2)}) %collective-permute-start.12) | collective-permute-done | bytes 1868 | tf_op jit(solution)/shard_map/ppermute | solution.py:190
  118.2 3.2 %collective-permute-start.13 = (f32[3,3,9]{2,1,0:T(4,128)S(1)}, f32[3,3,9]{2,1,0:T(4,128)S(1)}, u32[]{:S(2)}, u32[]{:S(2)}) collective-permute-start(f32[3,3,9]{2,1,0:T(4,128)S(1)} %get-tuple-element.19), channel_id=1, source_target_pairs={{0,32},{32,64},{64,96},{1,33},{33,65},{65,97},{2,34},{34,66},{66,9... | collective-permute-start | bytes 980 | tf_op jit(solution)/shard_map/ppermute | solution.py:189
  123.1 2.8 %collective-permute-done.14 = f32[3,3,9]{2,1,0:T(4,128)S(1)} collective-permute-done((f32[3,3,9]{2,1,0:T(4,128)S(1)}, f32[3,3,9]{2,1,0:T(4,128)S(1)}, u32[]{:S(2)}, u32[]{:S(2)}) %collective-permute-start.14) | collective-permute-done | bytes 356 | tf_op jit(solution)/shard_map/ppermute | solution.py:190
  127.6 8.2 %multiply_reduce_fusion.3 = f32[32,128,256]{2,1,0:T(8,128)S(1)} fusion(f32[3,32,128,256]{3,2,1,0:T(8,128)} %get-tuple-element.5, f32[3,128,256]{2,1,0:T(8,128)S(1)} %get-tuple-element.30, f32[3,128,256]{2,1,0:T(8,128)S(1)} %get-tuple-element.31, f32[3,128,256]{2,1,0:T(8,128)S(1)} %get-tuple-element.29, f32[32]{0:T(128)S(1)} %get-tuple-element.41, ...), kind=kLoop, calls=%fused_computation.3 | loop fusion | flops 20971520 | bytes 17957248 | tf_op jit(solution)/shard_map/reduce_sum | solution.py:239
  135.9 2.2 fusion.103
  138.1 1.6 pad_maximum_fusion.3
  140.9 1.4 fusion.115
  142.2 1.8 collective-permute-start.16
  145.0 1.4 fusion.117
  146.4 5.3 %collective-permute-start.17 = (f32[2]{0:T(128)S(1)}, f32[2]{0:T(128)S(1)}, u32[]{:S(2)}, u32[]{:S(2)}) collective-permute-start(f32[2]{0:T(128)S(1)} %fusion.117), channel_id=1, source_target_pairs={{0,4},{1,5},{2,6},{3,7},{4,0},{5,1},{6,2},{7,3},{8,12},{9,13},{10,... | collective-permute-start | bytes 32 | tf_op jit(solution)/shard_map/ppermute | solution.py:177
  152.7 2.1 collective-permute-start.18
  155.7 3.4 %collective-permute-start.19 = (f32[2]{0:T(128)S(1)}, f32[2]{0:T(128)S(1)}, u32[]{:S(2)}, u32[]{:S(2)}) collective-permute-start(f32[2]{0:T(128)S(1)} %add.349), channel_id=1, source_target_pairs={{0,16},{1,17},{2,18},{3,19},{4,20},{5,21},{6,22},{7,23},{8,24},{9,... | collective-permute-start | bytes 32 | tf_op jit(solution)/shard_map/ppermute | solution.py:177
  161.1 1.4 collective-permute-done.20
  162.5 1.8 collective-permute-start.21
  164.3 2.1 collective-permute-done.21
  169.7 1.8 multiply_reduce_fusion.8
  171.9 3.7 %multiply_reduce_fusion.2 = (f32[3,128,256]{2,1,0:T(8,128)S(1)}, f32[3,128,256]{2,1,0:T(8,128)S(1)}, f32[3,128,256]{2,1,0:T(8,128)S(1)}) fusion(f32[3,32,128,256]{3,2,1,0:T(8,128)S(1)} %bitcast.122, f32[32,128,256]{2,1,0:T(8,128)S(1)} %get-tuple-element.22, f32[32]{0:T(128)S(1)} %get-tuple-element.40, f32[32]{0:T(128)S(1)} %get-tuple-element.42, ...), kind=kLoop, calls=%fused_computation.2 | loop fusion | flops 21725184 | bytes 17957248 | tf_op jit(solution)/shard_map/reduce_sum | solution.py:156
  177.4 42.6 %all_gather.3 = f32[128,2,689]{2,1,0:T(2,128)S(1)} all-gather(f32[1,2,689]{2,1,0:T(2,128)S(1)} %all_gather_reshape.3), channel_id=1, replica_groups=mesh['grp'=4,'dev'=32] {'grp','dev'}, dimensions={0}, use_global_device_ids=true | all-gather | bytes 711048 | tf_op jit(solution)/shard_map/all_gather | solution.py:258
  223.5 2.4 %fusion.5 = f32[4,3,65,9,17]{2,4,0,3,1:T(8,128)S(1)} fusion(f32[4,32,3,3,9,17]{1,0,5,4,3,2:T(4,128)S(1)} %reshape.189, s32[32,3]{0,1:T(4,128)S(1)} %iota_add_fusion.1), kind=kOutput, calls=%fused_computation.19 | convolution fusion | flops 137485920 | bytes 1182768 | tf_op jit(solution)/shard_map/pqcijk,qix->pcxjk/dot_general | solution.py:203
  225.9 2.2 fusion.9
  (105 shorter events, 32.9 us)
Async XLA Ops:
  0.6 11.9 %copy-start = (bf16[32,128,256]{2,1,0:T(8,128)(2,1)S(1)}, bf16[32,128,256]{2,1,0:T(8,128)(2,1)}, u32[]{:S(2)}) copy-start(bf16[32,128,256]{2,1,0:T(8,128)(2,1)} %param.5) | copy-start | bytes 6291460
  3.1 11.6 %collective-permute-start = (bf16[9,128,256]{2,1,0:T(8,128)(2,1)}, bf16[9,128,256]{2,1,0:T(8,128)(2,1)}, u32[]{:S(2)}, u32[]{:S(2)}) collective-permute-start(bf16[9,128,256]{2,1,0:T(8,128)(2,1)} %get-tuple-element.28), channel_id=1, source_target_pairs={{0,1},{1,2},{2,3},{3,4},{4,5},{5,6},{6,7},{7,8},{8,9},{9,10},{10,1... | collective-permute-start | bytes 1769480 | tf_op jit(solution)/shard_map/ppermute | solution.py:23
  7.6 11.5 %collective-permute-start.1 = (bf16[9,128,256]{2,1,0:T(8,128)(2,1)}, bf16[9,128,256]{2,1,0:T(8,128)(2,1)}, u32[]{:S(2)}, u32[]{:S(2)}) collective-permute-start(bf16[9,128,256]{2,1,0:T(8,128)(2,1)} %get-tuple-element.27), channel_id=1, source_target_pairs={{1,0},{2,1},{3,2},{4,3},{5,4},{6,5},{7,6},{8,7},{9,8},{10,9},{11,1... | collective-permute-start | bytes 1769480 | tf_op jit(solution)/shard_map/ppermute | solution.py:24
  9.6 6.2 %copy-start.5 = (bf16[32,128,256]{2,1,0:T(8,128)(2,1)S(1)}, bf16[32,128,256]{2,1,0:T(8,128)(2,1)}, u32[]{:S(2)}) copy-start(bf16[32,128,256]{2,1,0:T(8,128)(2,1)} %param.6) | copy-start | bytes 6291460
  20.3 1.7 copy-start.4
  26.5 7.2 %collective-permute-start.2 = (bf16[50,128,1]{1,0,2:T(8,128)(2,1)S(1)}, bf16[50,128,1]{1,0,2:T(8,128)(2,1)S(1)}, u32[]{:S(2)}, u32[]{:S(2)}) collective-permute-start(bf16[50,128,1]{1,0,2:T(8,128)(2,1)S(1)} %copy.34), channel_id=1, source_target_pairs={{0,32},{32,64},{64,96},{1,33},{33,65},{65,97},{2,34},{34,66},{66,9... | collective-permute-start | bytes 38408 | tf_op jit(solution)/shard_map/ppermute | solution.py:219
  31.7 4.5 %collective-permute-start.3 = (bf16[50,128,1]{1,0,2:T(8,128)(2,1)S(1)}, bf16[50,128,1]{1,0,2:T(8,128)(2,1)S(1)}, u32[]{:S(2)}, u32[]{:S(2)}) collective-permute-start(bf16[50,128,1]{1,0,2:T(8,128)(2,1)S(1)} %copy.35), channel_id=1, source_target_pairs={{32,0},{64,32},{96,64},{33,1},{65,33},{97,65},{34,2},{66,34},{98,6... | collective-permute-start | bytes 38408 | tf_op jit(solution)/shard_map/ppermute | solution.py:220
  50.3 8.2 %copy-start.1 = (f32[32,128,256]{2,1,0:T(8,128)S(1)}, f32[32,128,256]{2,1,0:T(8,128)}, u32[]{:S(2)}) copy-start(f32[32,128,256]{2,1,0:T(8,128)} %get-tuple-element.6) | copy-start | bytes 12582916
  58.5 39.9 %slice-start = ((s8[12582912]{0:T(1024)(128)(4,1)}), s8[4194304]{0:T(1024)(128)(4,1)S(1)}, s32[]{:S(2)}) async-start(s8[12582912]{0:T(1024)(128)(4,1)} %bitcast.119), calls=%async_computation | async-start | bytes 8388608
  58.5 39.9 %slice-start.1 = ((s8[12582912]{0:T(1024)(128)(4,1)}), s8[4194304]{0:T(1024)(128)(4,1)S(1)}, s32[]{:S(2)}) async-start(s8[12582912]{0:T(1024)(128)(4,1)} %bitcast.119), calls=%async_computation.1 | async-start | bytes 8388608
  63.6 1.2 collective-permute-start.4
  67.5 2.4 %collective-permute-start.5 = (f32[4]{0:T(128)S(1)}, f32[4]{0:T(128)S(1)}, u32[]{:S(2)}, u32[]{:S(2)}) collective-permute-start(f32[4]{0:T(128)S(1)} %fusion.116), channel_id=1, source_target_pairs={{0,2},{1,3},{2,0},{3,1},{4,6},{5,7},{6,4},{7,5},{8,10},{9,11},{10,... | collective-permute-start | bytes 56 | tf_op jit(solution)/shard_map/ppermute | solution.py:177
  72.6 5.6 %collective-permute-start.6 = (f32[4]{0:T(128)S(1)}, f32[4]{0:T(128)S(1)}, u32[]{:S(2)}, u32[]{:S(2)}) collective-permute-start(f32[4]{0:T(128)S(1)} %fusion.118), channel_id=1, source_target_pairs={{0,4},{1,5},{2,6},{3,7},{4,0},{5,1},{6,2},{7,3},{8,12},{9,13},{10,... | collective-permute-start | bytes 56 | tf_op jit(solution)/shard_map/ppermute | solution.py:177
  78.2 2.8 %collective-permute-start.7 = (f32[4]{0:T(128)S(1)}, f32[4]{0:T(128)S(1)}, u32[]{:S(2)}, u32[]{:S(2)}) collective-permute-start(f32[4]{0:T(128)S(1)} %add.329), channel_id=1, source_target_pairs={{0,8},{1,9},{2,10},{3,11},{4,12},{5,13},{6,14},{7,15},{8,0},{9,1},... | collective-permute-start | bytes 56 | tf_op jit(solution)/shard_map/ppermute | solution.py:177
  81.0 4.4 %collective-permute-start.8 = (f32[4]{0:T(128)S(1)}, f32[4]{0:T(128)S(1)}, u32[]{:S(2)}, u32[]{:S(2)}) collective-permute-start(f32[4]{0:T(128)S(1)} %add.330), channel_id=1, source_target_pairs={{0,16},{1,17},{2,18},{3,19},{4,20},{5,21},{6,22},{7,23},{8,24},{9,... | collective-permute-start | bytes 56 | tf_op jit(solution)/shard_map/ppermute | solution.py:177
  85.4 2.4 %collective-permute-start.9 = (f32[4]{0:T(128)S(1)}, f32[4]{0:T(128)S(1)}, u32[]{:S(2)}, u32[]{:S(2)}) collective-permute-start(f32[4]{0:T(128)S(1)} %add.331), channel_id=1, source_target_pairs={{0,32},{32,0},{64,96},{96,64},{1,33},{33,1},{65,97},{97,65},{2,34}... | collective-permute-start | bytes 56 | tf_op jit(solution)/shard_map/ppermute | solution.py:177
  87.8 3.9 %collective-permute-start.10 = (f32[4]{0:T(128)S(1)}, f32[4]{0:T(128)S(1)}, u32[]{:S(2)}, u32[]{:S(2)}) collective-permute-start(f32[4]{0:T(128)S(1)} %add.332), channel_id=1, source_target_pairs={{0,64},{32,96},{64,0},{96,32},{1,65},{33,97},{65,1},{97,33},{2,66}... | collective-permute-start | bytes 56 | tf_op jit(solution)/shard_map/ppermute | solution.py:177
  97.5 2.2 slice-start.2
  104.2 10.6 %collective-permute-start.11 = (f32[3,9,17]{2,1,0:T(8,128)S(1)}, f32[3,9,17]{2,1,0:T(8,128)S(1)}, u32[]{:S(2)}, u32[]{:S(2)}) collective-permute-start(f32[3,9,17]{2,1,0:T(8,128)S(1)} %get-tuple-element.37), channel_id=1, source_target_pairs={{0,1},{1,2},{2,3},{3,4},{4,5},{5,6},{6,7},{7,8},{8,9},{9,10},{10,1... | collective-permute-start | bytes 5516 | tf_op jit(solution)/shard_map/ppermute | solution.py:189
  112.8 5.1 %collective-permute-start.12 = (f32[3,9,17]{2,1,0:T(8,128)S(1)}, f32[3,9,17]{2,1,0:T(8,128)S(1)}, u32[]{:S(2)}, u32[]{:S(2)}) collective-permute-start(f32[3,9,17]{2,1,0:T(8,128)S(1)} %get-tuple-element.38), channel_id=1, source_target_pairs={{1,0},{2,1},{3,2},{4,3},{5,4},{6,5},{7,6},{8,7},{9,8},{10,9},{11,1... | collective-permute-start | bytes 5516 | tf_op jit(solution)/shard_map/ppermute | solution.py:190
  118.2 4.7 %collective-permute-start.13 = (f32[3,3,9]{2,1,0:T(4,128)S(1)}, f32[3,3,9]{2,1,0:T(4,128)S(1)}, u32[]{:S(2)}, u32[]{:S(2)}) collective-permute-start(f32[3,3,9]{2,1,0:T(4,128)S(1)} %get-tuple-element.19), channel_id=1, source_target_pairs={{0,32},{32,64},{64,96},{1,33},{33,65},{65,97},{2,34},{34,66},{66,9... | collective-permute-start | bytes 980 | tf_op jit(solution)/shard_map/ppermute | solution.py:189
  121.4 4.4 %collective-permute-start.14 = (f32[3,3,9]{2,1,0:T(4,128)S(1)}, f32[3,3,9]{2,1,0:T(4,128)S(1)}, u32[]{:S(2)}, u32[]{:S(2)}) collective-permute-start(f32[3,3,9]{2,1,0:T(4,128)S(1)} %get-tuple-element.20), channel_id=1, source_target_pairs={{32,0},{64,32},{96,64},{33,1},{65,33},{97,65},{34,2},{66,34},{98,6... | collective-permute-start | bytes 980 | tf_op jit(solution)/shard_map/ppermute | solution.py:190
  127.6 8.2 %copy-start.2 = (f32[32,128,256]{2,1,0:T(8,128)S(1)}, f32[32,128,256]{2,1,0:T(8,128)}, u32[]{:S(2)}) copy-start(f32[32,128,256]{2,1,0:T(8,128)} %get-tuple-element.6) | copy-start | bytes 12582916
  135.9 35.6 %slice-start.3 = ((s8[12582912]{0:T(1024)(128)(4,1)}), s8[4194304]{0:T(1024)(128)(4,1)S(1)}, s32[]{:S(2)}) async-start(s8[12582912]{0:T(1024)(128)(4,1)} %bitcast.121), calls=%async_computation.3 | async-start | bytes 8388608
  135.9 35.6 %slice-start.4 = ((s8[12582912]{0:T(1024)(128)(4,1)}), s8[4194304]{0:T(1024)(128)(4,1)S(1)}, s32[]{:S(2)}) async-start(s8[12582912]{0:T(1024)(128)(4,1)} %bitcast.121), calls=%async_computation.4 | async-start | bytes 8388608
  139.7 1.2 collective-permute-start.15
  142.2 2.8 %collective-permute-start.16 = (f32[2]{0:T(128)S(1)}, f32[2]{0:T(128)S(1)}, u32[]{:S(2)}, u32[]{:S(2)}) collective-permute-start(f32[2]{0:T(128)S(1)} %fusion.115), channel_id=1, source_target_pairs={{0,2},{1,3},{2,0},{3,1},{4,6},{5,7},{6,4},{7,5},{8,10},{9,11},{10,... | collective-permute-start | bytes 32 | tf_op jit(solution)/shard_map/ppermute | solution.py:177
  146.4 6.3 %collective-permute-start.17 = (f32[2]{0:T(128)S(1)}, f32[2]{0:T(128)S(1)}, u32[]{:S(2)}, u32[]{:S(2)}) collective-permute-start(f32[2]{0:T(128)S(1)} %fusion.117), channel_id=1, source_target_pairs={{0,4},{1,5},{2,6},{3,7},{4,0},{5,1},{6,2},{7,3},{8,12},{9,13},{10,... | collective-permute-start | bytes 32 | tf_op jit(solution)/shard_map/ppermute | solution.py:177
  152.7 3.0 %collective-permute-start.18 = (f32[2]{0:T(128)S(1)}, f32[2]{0:T(128)S(1)}, u32[]{:S(2)}, u32[]{:S(2)}) collective-permute-start(f32[2]{0:T(128)S(1)} %add.348), channel_id=1, source_target_pairs={{0,8},{1,9},{2,10},{3,11},{4,12},{5,13},{6,14},{7,15},{8,0},{9,1},... | collective-permute-start | bytes 32 | tf_op jit(solution)/shard_map/ppermute | solution.py:177
  155.7 4.4 %collective-permute-start.19 = (f32[2]{0:T(128)S(1)}, f32[2]{0:T(128)S(1)}, u32[]{:S(2)}, u32[]{:S(2)}) collective-permute-start(f32[2]{0:T(128)S(1)} %add.349), channel_id=1, source_target_pairs={{0,16},{1,17},{2,18},{3,19},{4,20},{5,21},{6,22},{7,23},{8,24},{9,... | collective-permute-start | bytes 32 | tf_op jit(solution)/shard_map/ppermute | solution.py:177
  160.1 2.4 %collective-permute-start.20 = (f32[2]{0:T(128)S(1)}, f32[2]{0:T(128)S(1)}, u32[]{:S(2)}, u32[]{:S(2)}) collective-permute-start(f32[2]{0:T(128)S(1)} %add.350), channel_id=1, source_target_pairs={{0,32},{32,0},{64,96},{96,64},{1,33},{33,1},{65,97},{97,65},{2,34}... | collective-permute-start | bytes 32 | tf_op jit(solution)/shard_map/ppermute | solution.py:177
  162.5 3.9 %collective-permute-start.21 = (f32[2]{0:T(128)S(1)}, f32[2]{0:T(128)S(1)}, u32[]{:S(2)}, u32[]{:S(2)}) collective-permute-start(f32[2]{0:T(128)S(1)} %add.351), channel_id=1, source_target_pairs={{0,64},{32,96},{64,0},{96,32},{1,65},{33,97},{65,1},{97,33},{2,66}... | collective-permute-start | bytes 32 | tf_op jit(solution)/shard_map/ppermute | solution.py:177
  169.7 2.2 slice-start.5
  171.5 4.1 %copy-start.3 = (f32[32,128,256]{2,1,0:T(8,128)}, f32[32,128,256]{2,1,0:T(8,128)S(1)}, u32[]{:S(2)}) copy-start(f32[32,128,256]{2,1,0:T(8,128)S(1)} %get-tuple-element.22) | copy-start | bytes 12582916
  223.5 2.4 %copy-start.6 = (f32[3,65,9,65]{3,1,2,0:T(8,128)S(1)}, f32[3,65,9,65]{3,1,2,0:T(8,128)}, u32[]{:S(2)}) copy-start(f32[3,65,9,65]{3,1,2,0:T(8,128)} %param.8) | copy-start | bytes 1368904
  223.5 2.4 %copy-start.7 = (f32[3,65,9,65]{3,1,2,0:T(8,128)S(1)}, f32[3,65,9,65]{3,1,2,0:T(8,128)}, u32[]{:S(2)}) copy-start(f32[3,65,9,65]{3,1,2,0:T(8,128)} %param.9) | copy-start | bytes 1368904

commit v4 on v3

--- a/solution.py
+++ b/solution.py
@@ -32,7 +32,7 @@
 PLANES = 8
 
 
-def _native_kernel(offset_ref, w_ref, lo_ref, hi_ref, sl_ref, sm_ref, keep_ref):
+def _native_kernel(offset_ref, w_ref, lo_ref, hi_ref, q_ref, sl_ref, wp_ref, mo_ref, keep_ref):
     step = pl.program_id(0)
     _, wy, wz = w_ref.shape
     row = lax.broadcasted_iota(jnp.int32, (wy, wz), 0)
@@ -60,24 +60,42 @@
 
     @pl.when(step == 0)
     def _():
+        mo_ref[...] = jnp.zeros(mo_ref.shape, jnp.float32)
         for t in range(2):
             for n, value in enumerate(planes(t)):
                 keep_ref[t, n] = value
 
     window = [tuple(keep_ref[t, n] for n in range(4)) for t in range(2)]
+    total, square = mo_ref[0], mo_ref[1]
     for k in range(PLANES):
         window.append(planes(k + 2))
         prev, mid, nxt = window[k], window[k + 1], window[k + 2]
-        sl_ref[0, k] = 0.5 * (nxt[0] - prev[0])
-        sl_ref[1, k] = (prev[1] + 4.0 * mid[1] + nxt[1]) * sixth
-        sl_ref[2, k] = (prev[2] + 4.0 * mid[2] + nxt[2]) * sixth
-        sm_ref[k] = mid[3]
+        slopes = (
+            0.5 * (nxt[0] - prev[0]),
+            (prev[1] + 4.0 * mid[1] + nxt[1]) * sixth,
+            (prev[2] + 4.0 * mid[2] + nxt[2]) * sixth,
+        )
+        x = step * PLANES + k
+        node = x // E
+        part = (x - node * E).astype(jnp.float32) / E
+        warped = mid[3]
+        moved = None
+        for c in range(3):
+            sl_ref[c, k] = slopes[c]
+            field = (1.0 - part) * q_ref[c, node] + part * q_ref[c, node + 1]
+            moved = field * slopes[c] if moved is None else moved + field * slopes[c]
+        warped = warped + moved
+        wp_ref[k] = warped
+        total = total + warped
+        square = square + warped * warped
+    mo_ref[0] = total
+    mo_ref[1] = square
     for t in range(2):
         for n, value in enumerate(window[PLANES + t]):
             keep_ref[t, n] = value
 
 
-def native_slopes(offset, widened, below, above, width_x, interpret=False):
+def native_slopes(offset, widened, below, above, partial, width_x, interpret=False):
     _, wy, wz = widened.shape
     assert width_x % PLANES == 0
     whole = pl.BlockSpec(widened.shape, lambda i, o: (0, 0, 0))
@@ -85,11 +103,12 @@
     spec = pltpu.PrefetchScalarGridSpec(
         num_scalar_prefetch=1,
         grid=(width_x // PLANES,),
-        in_specs=[whole, face, face],
+        in_specs=[whole, face, face, pl.BlockSpec(partial.shape, lambda i, o: (0, 0, 0, 0))],
         scratch_shapes=[pltpu.VMEM((2, 4, wy, wz), jnp.float32)],
         out_specs=[
             pl.BlockSpec((3, PLANES, wy, wz), lambda i, o: (0, i, 0, 0)),
             pl.BlockSpec((PLANES, wy, wz), lambda i, o: (i, 0, 0)),
+            pl.BlockSpec((2, wy, wz), lambda i, o: (0, 0, 0)),
         ],
     )
     return pl.pallas_call(
@@ -98,9 +117,10 @@
         out_shape=[
             jax.ShapeDtypeStruct((3, width_x, wy, wz), jnp.float32),
             jax.ShapeDtypeStruct((width_x, wy, wz), jnp.float32),
+            jax.ShapeDtypeStruct((2, wy, wz), jnp.float32),
         ],
         interpret=interpret,
-    )(offset, widened, below, above)
+    )(offset, widened, below, above, partial)
 
 
 def hat_matrix(voxels, nodes):
@@ -218,7 +238,6 @@
     down = [(j, i) for i, j in up]
     below = lax.ppermute(widened[:, :, -1:], "grp", up)
     above = lax.ppermute(widened[:, :, :1], "grp", down)
-    slopes, sample = native_slopes(offset.reshape(1), widened, below, above, width_x)
     target = ref_volume.astype(jnp.float32)
     elements_x = width_x // E
     elements_z = depth_z // E
@@ -231,13 +250,22 @@
     local_nodes = lax.dynamic_slice(init_disp, corner, extent)
     local_precond = lax.dynamic_slice(precond, corner, extent)
     target_sums = jnp.stack([jnp.sum(target), jnp.sum(target * target)])
+    partial = interpolate(local_nodes, hat_y, hat_z)
+    slopes, warped, moments = native_slopes(
+        offset.reshape(1), widened, below, above, partial, width_x
+    )
     residual = target
     total_slab = None
     mean_ref = var_ref = None
     for iteration in range(ITERS):
-        shift_field = expand_x(interpolate(local_nodes, hat_y, hat_z), hat_x)
-        warped = sample + jnp.sum(shift_field * slopes, axis=0)
-        image_sums = jnp.stack([jnp.sum(warped), jnp.sum(warped * warped)])
+        if iteration == 0:
+            image_sums = jnp.sum(moments, axis=(1, 2))
+        else:
+            moved = interpolate(local_nodes, hat_y, hat_z)
+            shift_field = expand_x(moved - partial, hat_x)
+            warped = warped + jnp.sum(shift_field * slopes, axis=0)
+            partial = moved
+            image_sums = jnp.stack([jnp.sum(warped), jnp.sum(warped * warped)])
         if iteration == 0:
             sums = allsum(jnp.concatenate([target_sums, image_sums]))
             mean_ref = sums[0] / voxel_count

time: 230 us -> 233 us (1.013)
  waiting for transfers between devices: 26.4 us -> 19.6 us
  other arithmetic: 46.7 us -> 40.3 us
  matrix products: 9.32 us -> 15.5 us
  Pallas kernels: 12.4 us -> 15.1 us
  blocking collectives: 42.6 us -> 45.2 us
  local copies, waits for them, and re-layouts: 23.7 us -> 26.2 us
    reduce_sum x2, other arithmetic: 16.4 us -> 9.36 us  [the longest x1 8.27 us: local(): warped = warped + jnp.sum(shift_field * slopes, axis=0)]
    add x14, other arithmetic: 8.07 us -> 4.01 us  [allsum(): values = values + lax.ppermute(values, axis, pairs)]
    reduce_sum x2, other arithmetic: 7.3 us -> 10.6 us  [restrict(): jnp.sum(terms * hat_x[None, :, i, None, None], axis=1)]
    ppermute x2, waiting for transfers between devices: 5.96 us -> 3.2 us  [share_nodes(): after = lax.ppermute(first, axis, down)]
    pallas_call x1, Pallas kernels: 12.4 us -> 15.1 us  [native_slopes(): pl.pallas_call(_native_kernel, grid_spec=spec, out_shape=[jax.ShapeDtypeS...]
    all_gather x1, blocking collectives: 42.6 us -> 45.2 us  [local(): lax.all_gather(packed.reshape(2, -1), ('grp', 'dev'))]
    dot_general x2, matrix products: 2.26 us -> 4.63 us  [interpolate(): return jnp.einsum('cijz,yj->ciyz', partial_z, hat_y, precision=highest)]
    unnamed x31 -> x57, local copies, waits for them, and re-layouts: 4.88 us -> 3.12 us
  transfers between devices with their start and end apart: 22 -> 22, of which waited for: 19 -> 17; matrix products, arithmetic and copies ran while one was open for 4% -> 6% of each run, Pallas kernels for 0% -> 0%
where the time goes in v4:
time: 233 us; the launch traced here: 232 us
  starting transfers between devices  58.4 us (25%)
  blocking collectives  45.2 us (19%)
  other arithmetic  40.3 us (17%)
  local copies, waits for them, and re-layouts  26.2 us (11%)
  waiting for transfers between devices  19.6 us (8%)
  matrix products  15.5 us (7%)
  Pallas kernels  15.1 us (6%)
  between operations  11.4 us (5%)
    all_gather x1, blocking collectives, local(): lax.all_gather(packed.reshape(2, -1), ('grp', 'dev'))  45.2 us
    ppermute x14, starting transfers between devices, allsum(): values = values + lax.ppermute(values, axis, pairs)  31.9 us
    pallas_call x1, Pallas kernels, native_slopes(): pl.pallas_call(_native_kernel, grid_spec=spec, out_shape=[jax.ShapeDtypeS...  15.1 us
    ppermute x14, waiting for transfers between devices, allsum(): values = values + lax.ppermute(values, axis, pairs)  14.4 us
    ppermute x2, starting transfers between devices, share_nodes(): before = lax.ppermute(last, axis, up)  12.3 us
    reduce_sum x2, other arithmetic, restrict(): jnp.sum(terms * hat_x[None, :, i, None, None], axis=1)  10.6 us
    reduce_sum x1, other arithmetic, local(): warped = warped + jnp.sum(shift_field * slopes, axis=0)  8.27 us
  transfers between devices with their start and end apart: 22, of which 17 were waited for; matrix products, arithmetic and copies ran while one was open for 6% of the time, Pallas kernels for 0%

profile of v4, /device:TPU:1, one launch (start us, length us, event | category | flops | bytes accessed | tf_op | source)
XLA Modules:
  0.0 231.8 jit_solution(9657638700375672969)
XLA Ops:
  0.6 2.5 %fusion.107 = (bf16[9,128,256]{2,1,0:T(8,128)(2,1)}, bf16[9,128,256]{2,1,0:T(8,128)(2,1)}) fusion(bf16[32,128,256]{2,1,0:T(8,128)(2,1)} %param.6), kind=kLoop, calls=%fused_computation.176 | loop fusion | bytes 2359296 | tf_op jit(solution)/shard_map/slice | solution.py:22
  3.1 4.5 %collective-permute-start = (bf16[9,128,256]{2,1,0:T(8,128)(2,1)}, bf16[9,128,256]{2,1,0:T(8,128)(2,1)S(1)}, u32[]{:S(2)}, u32[]{:S(2)}) collective-permute-start(bf16[9,128,256]{2,1,0:T(8,128)(2,1)} %get-tuple-element.27), channel_id=1, source_target_pairs={{0,1},{1,2},{2,3},{3,4},{4,5},{5,6},{6,7},{7,8},{8,9},{9,10},{10,1... | collective-permute-start | bytes 1769480 | tf_op jit(solution)/shard_map/ppermute | solution.py:23
  7.6 1.9 collective-permute-start.1
  10.7 1.3 constant_dynamic-slice_fusion
  12.4 2.8 %convolution_bitcast_fusion.1.q_ref = f32[3,3,128,256]{3,2,1,0:T(8,128)} fusion(f32[3,3,9,256]{3,2,1,0:T(8,128)S(1)} %fusion.29, f32[128]{0:T(128)} %get-tuple-element.51, s32[128]{0:T(128)} %get-tuple-element.48, f32[128]{0:T(128)} %get-tuple-element.52, s32[128]{0:T(128)} %get-tuple-element.47), kind=kOutput, calls=%fused_computation.20 | convolution fusion | flops 31856256 | bytes 1264640 | tf_op jit(solution)/shard_map/cijz,yj->ciyz/dot_general | solution.py:164
  15.2 1.7 convert_reduce_fusion
  17.2 1.9 collective-permute-done.1
  19.1 1.7 copy-done.3
  20.8 2.6 %fusion.106 = (bf16[50,128,1]{2,1,0:T(8,128)(2,1)}, bf16[50,128,1]{2,1,0:T(8,128)(2,1)}) fusion(bf16[50,128,256]{2,1,0:T(8,128)(2,1)S(1)} %constant_dynamic-update-slice_fusion.w_ref), kind=kLoop, calls=%fused_computation.175 | loop fusion | bytes 51200 | tf_op jit(solution)/shard_map/slice | solution.py:240
  23.3 2.0 copy.34
  25.4 3.2 %collective-permute-start.2 = (bf16[50,128,1]{1,0,2:T(8,128)(2,1)S(1)}, bf16[50,128,1]{1,0,2:T(8,128)(2,1)S(1)}, u32[]{:S(2)}, u32[]{:S(2)}) collective-permute-start(bf16[50,128,1]{1,0,2:T(8,128)(2,1)S(1)} %copy.34), channel_id=1, source_target_pairs={{0,32},{32,64},{64,96},{1,33},{33,65},{65,97},{2,34},{34,66},{66,9... | collective-permute-start | bytes 38408 | tf_op jit(solution)/shard_map/ppermute | solution.py:239
  28.6 2.0 copy.35
  30.6 1.3 collective-permute-start.3
  33.1 1.7 copy.37.lo_ref
  35.0 1.7 copy.38.hi_ref
  36.7 15.1 %shard_map.76 = (f32[3,32,128,256]{3,2,1,0:T(8,128)}, f32[32,128,256]{2,1,0:T(8,128)}, f32[2,128,256]{2,1,0:T(8,128)}) custom-call(s32[1]{0:T(128)} %bitcast.112.offset_ref, bf16[50,128,256]{2,1,0:T(8,128)(2,1)} %copy-done.3, bf16[50,128,1]{2,1,0:T(8,128)(2,1)} %copy.37.lo_ref, bf16[50,128,1]{2,1,0:T(8,128)(2,1)} %copy.38.hi_ref, ...), custom_call_target="tpu_custom_call" | custom-call | tf_op jit(solution)/shard_map/pallas_call | solution.py:114
  59.0 4.7 %collective-permute-start.6 = (f32[4]{0:T(128)S(1)}, f32[4]{0:T(128)S(1)}, u32[]{:S(2)}, u32[]{:S(2)}) collective-permute-start(f32[4]{0:T(128)S(1)} %add.295), channel_id=1, source_target_pairs={{0,4},{1,5},{2,6},{3,7},{4,0},{5,1},{6,2},{7,3},{8,12},{9,13},{10,... | collective-permute-start | bytes 56 | tf_op jit(solution)/shard_map/ppermute | solution.py:197
  64.6 2.0 collective-permute-start.7
  67.6 3.4 %collective-permute-start.8 = (f32[4]{0:T(128)S(1)}, f32[4]{0:T(128)S(1)}, u32[]{:S(2)}, u32[]{:S(2)}) collective-permute-start(f32[4]{0:T(128)S(1)} %add.297), channel_id=1, source_target_pairs={{0,16},{1,17},{2,18},{3,19},{4,20},{5,21},{6,22},{7,23},{8,24},{9,... | collective-permute-start | bytes 56 | tf_op jit(solution)/shard_map/ppermute | solution.py:197
  72.0 1.3 collective-permute-start.9
  74.4 2.9 %collective-permute-start.10 = (f32[4]{0:T(128)S(1)}, f32[4]{0:T(128)S(1)}, u32[]{:S(2)}, u32[]{:S(2)}) collective-permute-start(f32[4]{0:T(128)S(1)} %add.299), channel_id=1, source_target_pairs={{0,64},{32,96},{64,0},{96,32},{1,65},{33,97},{65,1},{97,33},{2,66}... | collective-permute-start | bytes 56 | tf_op jit(solution)/shard_map/ppermute | solution.py:197
  83.9 2.9 %fusion.1 = f32[32,128,256]{2,1,0:T(8,128)S(1)} fusion(bf16[32,128,256]{2,1,0:T(8,128)(2,1)S(1)} %copy-done, f32[32,128,256]{2,1,0:T(8,128)} %get-tuple-element.8, f32[]{:T(128)} %bitcast.13, f32[]{:T(128)} %bitcast.12, f32[]{:T(128)} %bitcast.11), kind=kLoop, calls=%fused_computation.11 | loop fusion | flops 5242880 | bytes 10485772 | tf_op jit(solution)/shard_map/sub | solution.py:279
  86.9 6.9 %multiply_reduce_fusion.6 = (f32[3,128,256]{2,1,0:T(8,128)S(1)}, f32[3,128,256]{2,1,0:T(8,128)S(1)}, f32[3,128,256]{2,1,0:T(8,128)S(1)}) fusion(f32[3,32,128,256]{3,2,1,0:T(8,128)} %get-tuple-element.6, f32[32]{0:T(128)S(1)} %get-tuple-element.38, f32[32,128,256]{2,1,0:T(8,128)S(1)} %fusion.1, f32[32]{0:T(128)S(1)} %get-tuple-element.37, ...), kind=kLoop, calls=%fused_computation.6 | loop fusion | flops 21725184 | bytes 17957248 | tf_op jit(solution)/shard_map/reduce_sum | solution.py:176
  94.8 8.8 %collective-permute-start.11 = (f32[3,9,17]{2,1,0:T(8,128)S(1)}, f32[3,9,17]{2,1,0:T(8,128)S(1)}, u32[]{:S(2)}, u32[]{:S(2)}) collective-permute-start(f32[3,9,17]{2,1,0:T(8,128)S(1)} %get-tuple-element.33), channel_id=1, source_target_pairs={{0,1},{1,2},{2,3},{3,4},{4,5},{5,6},{6,7},{7,8},{8,9},{9,10},{10,1... | collective-permute-start | bytes 5516 | tf_op jit(solution)/shard_map/ppermute | solution.py:209
  103.6 1.9 collective-permute-start.12
  105.5 3.2 %collective-permute-done.12 = f32[3,9,17]{2,1,0:T(8,128)S(1)} collective-permute-done((f32[3,9,17]{2,1,0:T(8,128)S(1)}, f32[3,9,17]{2,1,0:T(8,128)S(1)}, u32[]{:S(2)}, u32[]{:S(2)}) %collective-permute-start.12) | collective-permute-done | bytes 1868 | tf_op jit(solution)/shard_map/ppermute | solution.py:210
  109.5 3.5 %collective-permute-start.13 = (f32[3,3,9]{2,1,0:T(4,128)S(1)}, f32[3,3,9]{2,1,0:T(4,128)S(1)}, u32[]{:S(2)}, u32[]{:S(2)}) collective-permute-start(f32[3,3,9]{2,1,0:T(4,128)S(1)} %get-tuple-element.19), channel_id=1, source_target_pairs={{0,32},{32,64},{64,96},{1,33},{33,65},{65,97},{2,34},{34,66},{66,9... | collective-permute-start | bytes 980 | tf_op jit(solution)/shard_map/ppermute | solution.py:209
  113.0 1.3 collective-permute-start.14
  116.3 1.5 copy.44
  117.7 1.5 copy.45
  121.4 1.8 fusion.8
  123.4 8.3 %multiply_reduce_fusion.3 = f32[32,128,256]{2,1,0:T(8,128)S(1)} fusion(f32[3,32,128,256]{3,2,1,0:T(8,128)} %get-tuple-element.6, f32[3,128,256]{2,1,0:T(8,128)S(1)} %get-tuple-element.29, f32[3,128,256]{2,1,0:T(8,128)S(1)} %get-tuple-element.30, f32[3,128,256]{2,1,0:T(8,128)S(1)} %get-tuple-element.28, f32[32]{0:T(128)} %copy-done.8, f32[32]{0:T(128)} %copy-done.10, ...), kind=kLoop, calls=%fused_computation.3 | loop fusion | flops 20971520 | bytes 17957248 | tf_op jit(solution)/shard_map/reduce_sum | solution.py:266
  131.7 2.2 fusion.104
  133.9 1.6 pad_maximum_fusion.3
  136.7 1.4 fusion.115
  138.0 1.8 collective-permute-start.16
  140.8 1.4 fusion.117
  142.2 4.8 %collective-permute-start.17 = (f32[2]{0:T(128)S(1)}, f32[2]{0:T(128)S(1)}, u32[]{:S(2)}, u32[]{:S(2)}) collective-permute-start(f32[2]{0:T(128)S(1)} %fusion.117), channel_id=1, source_target_pairs={{0,4},{1,5},{2,6},{3,7},{4,0},{5,1},{6,2},{7,3},{8,12},{9,13},{10,... | collective-permute-start | bytes 32 | tf_op jit(solution)/shard_map/ppermute | solution.py:197
  148.0 2.0 collective-permute-start.18
  151.0 3.4 %collective-permute-start.19 = (f32[2]{0:T(128)S(1)}, f32[2]{0:T(128)S(1)}, u32[]{:S(2)}, u32[]{:S(2)}) collective-permute-start(f32[2]{0:T(128)S(1)} %add.319), channel_id=1, source_target_pairs={{0,16},{1,17},{2,18},{3,19},{4,20},{5,21},{6,22},{7,23},{8,24},{9,... | collective-permute-start | bytes 32 | tf_op jit(solution)/shard_map/ppermute | solution.py:197
  155.3 1.4 collective-permute-start.20
  157.8 2.9 %collective-permute-start.21 = (f32[2]{0:T(128)S(1)}, f32[2]{0:T(128)S(1)}, u32[]{:S(2)}, u32[]{:S(2)}) collective-permute-start(f32[2]{0:T(128)S(1)} %add.321), channel_id=1, source_target_pairs={{0,64},{32,96},{64,0},{96,32},{1,65},{33,97},{65,1},{97,33},{2,66}... | collective-permute-start | bytes 32 | tf_op jit(solution)/shard_map/ppermute | solution.py:197
  165.0 1.8 multiply_reduce_fusion.7
  167.2 3.7 %multiply_reduce_fusion.2 = (f32[3,128,256]{2,1,0:T(8,128)S(1)}, f32[3,128,256]{2,1,0:T(8,128)S(1)}, f32[3,128,256]{2,1,0:T(8,128)S(1)}) fusion(f32[3,32,128,256]{3,2,1,0:T(8,128)S(1)} %bitcast.114, f32[32,128,256]{2,1,0:T(8,128)S(1)} %get-tuple-element.22, f32[32]{0:T(128)S(1)} %copy-done.13, f32[32]{0:T(128)S(1)} %copy-done.11, f32[32]{0:T(128)S(1)} %copy-done.9), kind=kLoop, calls=%fused_computation.2 | loop fusion | flops 21725184 | bytes 17957248 | tf_op jit(solution)/shard_map/reduce_sum | solution.py:176
  172.8 45.2 %all_gather.3 = f32[128,2,689]{2,1,0:T(2,128)S(1)} all-gather(f32[1,2,689]{2,1,0:T(2,128)S(1)} %all_gather_reshape.3), channel_id=1, replica_groups=mesh['grp'=4,'dev'=32] {'grp','dev'}, dimensions={0}, use_global_device_ids=true | all-gather | bytes 711048 | tf_op jit(solution)/shard_map/all_gather | solution.py:286
  219.6 2.8 %reshape.189 = f32[4,32,3,3,9,17]{1,0,5,4,3,2:T(4,128)} reshape(f32[128,1377]{0,1:T(8,128)S(1)} %copy.59) | data formatting | bytes 1410048 | tf_op jit(solution)/shard_map/reshape | solution.py:287
  223.1 4.1 %fusion.5 = f32[4,3,65,9,17]{2,4,0,3,1:T(8,128)S(1)} fusion(f32[4,32,3,3,9,17]{1,0,5,4,3,2:T(4,128)} %reshape.189, s32[32,3]{0,1:T(4,128)S(1)} %copy-done.7), kind=kOutput, calls=%fused_computation.17 | convolution fusion | flops 137485920 | bytes 1182768 | tf_op jit(solution)/shard_map/pqcijk,qix->pcxjk/dot_general | solution.py:223
  227.2 3.4 %fusion.10 = f32[3,65,9,65]{3,1,2,0:T(8,128)} fusion(f32[3,65,9,65]{3,1,2,0:T(8,128)S(1)} %copy-done.6, f32[3,65,9,65]{3,1,2,0:T(8,128)} %param.9, f32[4,3,65,9,17]{2,4,0,3,1:T(8,128)S(1)} %fusion.5, s32[4,17]{1,0:T(4,128)S(1)} %copy-done.14), kind=kOutput, calls=%fused_computation.23 | convolution fusion | flops 93317768 | bytes 1846532 | tf_op jit(solution)/shard_map/pcxjk,pkz->cxjz/dot_general | solution.py:224
  (128 shorter events, 32.7 us)
Async XLA Ops:
  0.6 14.6 %copy-start = (bf16[32,128,256]{2,1,0:T(8,128)(2,1)S(1)}, bf16[32,128,256]{2,1,0:T(8,128)(2,1)}, u32[]{:S(2)}) copy-start(bf16[32,128,256]{2,1,0:T(8,128)(2,1)} %param.5) | copy-start | bytes 6291460
  3.1 13.8 %collective-permute-start = (bf16[9,128,256]{2,1,0:T(8,128)(2,1)}, bf16[9,128,256]{2,1,0:T(8,128)(2,1)S(1)}, u32[]{:S(2)}, u32[]{:S(2)}) collective-permute-start(bf16[9,128,256]{2,1,0:T(8,128)(2,1)} %get-tuple-element.27), channel_id=1, source_target_pairs={{0,1},{1,2},{2,3},{3,4},{4,5},{5,6},{6,7},{7,8},{8,9},{9,10},{10,1... | collective-permute-start | bytes 1769480 | tf_op jit(solution)/shard_map/ppermute | solution.py:23
  7.6 11.4 %collective-permute-start.1 = (bf16[9,128,256]{2,1,0:T(8,128)(2,1)}, bf16[9,128,256]{2,1,0:T(8,128)(2,1)S(1)}, u32[]{:S(2)}, u32[]{:S(2)}) collective-permute-start(bf16[9,128,256]{2,1,0:T(8,128)(2,1)} %get-tuple-element.26), channel_id=1, source_target_pairs={{1,0},{2,1},{3,2},{4,3},{5,4},{6,5},{7,6},{8,7},{9,8},{10,9},{11,1... | collective-permute-start | bytes 1769480 | tf_op jit(solution)/shard_map/ppermute | solution.py:24
  10.7 6.3 %copy-start.5 = (bf16[32,128,256]{2,1,0:T(8,128)(2,1)S(1)}, bf16[32,128,256]{2,1,0:T(8,128)(2,1)}, u32[]{:S(2)}) copy-start(bf16[32,128,256]{2,1,0:T(8,128)(2,1)} %param.6) | copy-start | bytes 6291460
  15.2 71.6 %copy-start.8 = (f32[32]{0:T(128)}, f32[32]{0:T(128)S(1)}, u32[]{:S(2)}) copy-start(f32[32]{0:T(128)S(1)} %get-tuple-element.36) | copy-start | bytes 388
  15.2 71.6 %copy-start.10 = (f32[32]{0:T(128)}, f32[32]{0:T(128)S(1)}, u32[]{:S(2)}) copy-start(f32[32]{0:T(128)S(1)} %get-tuple-element.37) | copy-start | bytes 388
  15.2 71.6 %copy-start.12 = (f32[32]{0:T(128)}, f32[32]{0:T(128)S(1)}, u32[]{:S(2)}) copy-start(f32[32]{0:T(128)S(1)} %get-tuple-element.38) | copy-start | bytes 388
  19.1 1.7 copy-start.3
  25.4 7.8 %collective-permute-start.2 = (bf16[50,128,1]{1,0,2:T(8,128)(2,1)S(1)}, bf16[50,128,1]{1,0,2:T(8,128)(2,1)S(1)}, u32[]{:S(2)}, u32[]{:S(2)}) collective-permute-start(bf16[50,128,1]{1,0,2:T(8,128)(2,1)S(1)} %copy.34), channel_id=1, source_target_pairs={{0,32},{32,64},{64,96},{1,33},{33,65},{65,97},{2,34},{34,66},{66,9... | collective-permute-start | bytes 38408 | tf_op jit(solution)/shard_map/ppermute | solution.py:239
  30.6 4.5 %collective-permute-start.3 = (bf16[50,128,1]{1,0,2:T(8,128)(2,1)S(1)}, bf16[50,128,1]{1,0,2:T(8,128)(2,1)S(1)}, u32[]{:S(2)}, u32[]{:S(2)}) collective-permute-start(bf16[50,128,1]{1,0,2:T(8,128)(2,1)S(1)} %copy.35), channel_id=1, source_target_pairs={{32,0},{64,32},{96,64},{33,1},{65,33},{97,65},{34,2},{66,34},{98,6... | collective-permute-start | bytes 38408 | tf_op jit(solution)/shard_map/ppermute | solution.py:240
  54.1 1.2 collective-permute-start.4
  56.6 2.4 %collective-permute-start.5 = (f32[4]{0:T(128)S(1)}, f32[4]{0:T(128)S(1)}, u32[]{:S(2)}, u32[]{:S(2)}) collective-permute-start(f32[4]{0:T(128)S(1)} %fusion.116), channel_id=1, source_target_pairs={{0,2},{1,3},{2,0},{3,1},{4,6},{5,7},{6,4},{7,5},{8,10},{9,11},{10,... | collective-permute-start | bytes 56 | tf_op jit(solution)/shard_map/ppermute | solution.py:197
  59.0 5.6 %collective-permute-start.6 = (f32[4]{0:T(128)S(1)}, f32[4]{0:T(128)S(1)}, u32[]{:S(2)}, u32[]{:S(2)}) collective-permute-start(f32[4]{0:T(128)S(1)} %add.295), channel_id=1, source_target_pairs={{0,4},{1,5},{2,6},{3,7},{4,0},{5,1},{6,2},{7,3},{8,12},{9,13},{10,... | collective-permute-start | bytes 56 | tf_op jit(solution)/shard_map/ppermute | solution.py:197
  64.6 3.0 %collective-permute-start.7 = (f32[4]{0:T(128)S(1)}, f32[4]{0:T(128)S(1)}, u32[]{:S(2)}, u32[]{:S(2)}) collective-permute-start(f32[4]{0:T(128)S(1)} %add.296), channel_id=1, source_target_pairs={{0,8},{1,9},{2,10},{3,11},{4,12},{5,13},{6,14},{7,15},{8,0},{9,1},... | collective-permute-start | bytes 56 | tf_op jit(solution)/shard_map/ppermute | solution.py:197
  67.6 4.4 %collective-permute-start.8 = (f32[4]{0:T(128)S(1)}, f32[4]{0:T(128)S(1)}, u32[]{:S(2)}, u32[]{:S(2)}) collective-permute-start(f32[4]{0:T(128)S(1)} %add.297), channel_id=1, source_target_pairs={{0,16},{1,17},{2,18},{3,19},{4,20},{5,21},{6,22},{7,23},{8,24},{9,... | collective-permute-start | bytes 56 | tf_op jit(solution)/shard_map/ppermute | solution.py:197
  72.0 2.4 %collective-permute-start.9 = (f32[4]{0:T(128)S(1)}, f32[4]{0:T(128)S(1)}, u32[]{:S(2)}, u32[]{:S(2)}) collective-permute-start(f32[4]{0:T(128)S(1)} %add.298), channel_id=1, source_target_pairs={{0,32},{32,0},{64,96},{96,64},{1,33},{33,1},{65,97},{97,65},{2,34}... | collective-permute-start | bytes 56 | tf_op jit(solution)/shard_map/ppermute | solution.py:197
  74.4 3.9 %collective-permute-start.10 = (f32[4]{0:T(128)S(1)}, f32[4]{0:T(128)S(1)}, u32[]{:S(2)}, u32[]{:S(2)}) collective-permute-start(f32[4]{0:T(128)S(1)} %add.299), channel_id=1, source_target_pairs={{0,64},{32,96},{64,0},{96,32},{1,65},{33,97},{65,1},{97,33},{2,66}... | collective-permute-start | bytes 56 | tf_op jit(solution)/shard_map/ppermute | solution.py:197
  86.8 6.9 %copy-start.16 = (s32[128]{0:T(128)S(1)}, s32[128]{0:T(128)}, u32[]{:S(2)}) copy-start(s32[128]{0:T(128)} %get-tuple-element.47) | copy-start | bytes 1540
  86.9 6.9 %copy-start.18 = (s32[128]{0:T(128)S(1)}, s32[128]{0:T(128)}, u32[]{:S(2)}) copy-start(s32[128]{0:T(128)} %get-tuple-element.48) | copy-start | bytes 1540
  86.9 6.9 %copy-start.20 = (f32[128]{0:T(128)S(1)}, f32[128]{0:T(128)}, u32[]{:S(2)}) copy-start(f32[128]{0:T(128)} %get-tuple-element.51) | copy-start | bytes 1540
  86.9 6.9 %copy-start.22 = (f32[128]{0:T(128)S(1)}, f32[128]{0:T(128)}, u32[]{:S(2)}) copy-start(f32[128]{0:T(128)} %get-tuple-element.52) | copy-start | bytes 1540
  93.8 27.7 %copy-start.4 = (f32[3,3,128,256]{3,2,1,0:T(8,128)S(1)}, f32[3,3,128,256]{3,2,1,0:T(8,128)}, u32[]{:S(2)}) copy-start(f32[3,3,128,256]{3,2,1,0:T(8,128)} %convolution_bitcast_fusion.1.q_ref) | copy-start | bytes 3538948
  94.8 10.7 %collective-permute-start.11 = (f32[3,9,17]{2,1,0:T(8,128)S(1)}, f32[3,9,17]{2,1,0:T(8,128)S(1)}, u32[]{:S(2)}, u32[]{:S(2)}) collective-permute-start(f32[3,9,17]{2,1,0:T(8,128)S(1)} %get-tuple-element.33), channel_id=1, source_target_pairs={{0,1},{1,2},{2,3},{3,4},{4,5},{5,6},{6,7},{7,8},{8,9},{9,10},{10,1... | collective-permute-start | bytes 5516 | tf_op jit(solution)/shard_map/ppermute | solution.py:209
  103.6 5.1 %collective-permute-start.12 = (f32[3,9,17]{2,1,0:T(8,128)S(1)}, f32[3,9,17]{2,1,0:T(8,128)S(1)}, u32[]{:S(2)}, u32[]{:S(2)}) collective-permute-start(f32[3,9,17]{2,1,0:T(8,128)S(1)} %get-tuple-element.34), channel_id=1, source_target_pairs={{1,0},{2,1},{3,2},{4,3},{5,4},{6,5},{7,6},{8,7},{9,8},{10,9},{11,1... | collective-permute-start | bytes 5516 | tf_op jit(solution)/shard_map/ppermute | solution.py:210
  109.5 6.2 %collective-permute-start.13 = (f32[3,3,9]{2,1,0:T(4,128)S(1)}, f32[3,3,9]{2,1,0:T(4,128)S(1)}, u32[]{:S(2)}, u32[]{:S(2)}) collective-permute-start(f32[3,3,9]{2,1,0:T(4,128)S(1)} %get-tuple-element.19), channel_id=1, source_target_pairs={{0,32},{32,64},{64,96},{1,33},{33,65},{65,97},{2,34},{34,66},{66,9... | collective-permute-start | bytes 980 | tf_op jit(solution)/shard_map/ppermute | solution.py:209
  113.0 4.7 %collective-permute-start.14 = (f32[3,3,9]{2,1,0:T(4,128)}, f32[3,3,9]{2,1,0:T(4,128)}, u32[]{:S(2)}, u32[]{:S(2)}) collective-permute-start(f32[3,3,9]{2,1,0:T(4,128)} %get-tuple-element.20), channel_id=1, source_target_pairs={{32,0},{64,32},{96,64},{33,1},{65,33},{97,65},{34,2},{66,34},{98,6... | collective-permute-start | bytes 980 | tf_op jit(solution)/shard_map/ppermute | solution.py:210
  123.4 8.3 %copy-start.1 = (f32[32,128,256]{2,1,0:T(8,128)S(1)}, f32[32,128,256]{2,1,0:T(8,128)}, u32[]{:S(2)}) copy-start(f32[32,128,256]{2,1,0:T(8,128)} %get-tuple-element.8) | copy-start | bytes 12582916
  131.7 35.1 %slice-start = ((s8[12582912]{0:T(1024)(128)(4,1)}), s8[4194304]{0:T(1024)(128)(4,1)S(1)}, s32[]{:S(2)}) async-start(s8[12582912]{0:T(1024)(128)(4,1)} %bitcast.113), calls=%async_computation | async-start | bytes 8388608
  131.7 35.1 %slice-start.1 = ((s8[12582912]{0:T(1024)(128)(4,1)}), s8[4194304]{0:T(1024)(128)(4,1)S(1)}, s32[]{:S(2)}) async-start(s8[12582912]{0:T(1024)(128)(4,1)} %bitcast.113), calls=%async_computation.1 | async-start | bytes 8388608
  135.5 1.2 collective-permute-start.15
  138.0 2.8 %collective-permute-start.16 = (f32[2]{0:T(128)S(1)}, f32[2]{0:T(128)S(1)}, u32[]{:S(2)}, u32[]{:S(2)}) collective-permute-start(f32[2]{0:T(128)S(1)} %fusion.115), channel_id=1, source_target_pairs={{0,2},{1,3},{2,0},{3,1},{4,6},{5,7},{6,4},{7,5},{8,10},{9,11},{10,... | collective-permute-start | bytes 32 | tf_op jit(solution)/shard_map/ppermute | solution.py:197
  142.2 5.8 %collective-permute-start.17 = (f32[2]{0:T(128)S(1)}, f32[2]{0:T(128)S(1)}, u32[]{:S(2)}, u32[]{:S(2)}) collective-permute-start(f32[2]{0:T(128)S(1)} %fusion.117), channel_id=1, source_target_pairs={{0,4},{1,5},{2,6},{3,7},{4,0},{5,1},{6,2},{7,3},{8,12},{9,13},{10,... | collective-permute-start | bytes 32 | tf_op jit(solution)/shard_map/ppermute | solution.py:197
  148.0 3.0 %collective-permute-start.18 = (f32[2]{0:T(128)S(1)}, f32[2]{0:T(128)S(1)}, u32[]{:S(2)}, u32[]{:S(2)}) collective-permute-start(f32[2]{0:T(128)S(1)} %add.318), channel_id=1, source_target_pairs={{0,8},{1,9},{2,10},{3,11},{4,12},{5,13},{6,14},{7,15},{8,0},{9,1},... | collective-permute-start | bytes 32 | tf_op jit(solution)/shard_map/ppermute | solution.py:197
  151.0 4.4 %collective-permute-start.19 = (f32[2]{0:T(128)S(1)}, f32[2]{0:T(128)S(1)}, u32[]{:S(2)}, u32[]{:S(2)}) collective-permute-start(f32[2]{0:T(128)S(1)} %add.319), channel_id=1, source_target_pairs={{0,16},{1,17},{2,18},{3,19},{4,20},{5,21},{6,22},{7,23},{8,24},{9,... | collective-permute-start | bytes 32 | tf_op jit(solution)/shard_map/ppermute | solution.py:197
  155.3 2.4 %collective-permute-start.20 = (f32[2]{0:T(128)S(1)}, f32[2]{0:T(128)S(1)}, u32[]{:S(2)}, u32[]{:S(2)}) collective-permute-start(f32[2]{0:T(128)S(1)} %add.320), channel_id=1, source_target_pairs={{0,32},{32,0},{64,96},{96,64},{1,33},{33,1},{65,97},{97,65},{2,34}... | collective-permute-start | bytes 32 | tf_op jit(solution)/shard_map/ppermute | solution.py:197
  157.8 3.9 %collective-permute-start.21 = (f32[2]{0:T(128)S(1)}, f32[2]{0:T(128)S(1)}, u32[]{:S(2)}, u32[]{:S(2)}) collective-permute-start(f32[2]{0:T(128)S(1)} %add.321), channel_id=1, source_target_pairs={{0,64},{32,96},{64,0},{96,32},{1,65},{33,97},{65,1},{97,33},{2,66}... | collective-permute-start | bytes 32 | tf_op jit(solution)/shard_map/ppermute | solution.py:197
  164.9 2.2 slice-start.2
  165.0 2.2 copy-start.9
  165.0 2.2 copy-start.11
  165.0 2.2 copy-start.13
  166.8 4.1 %copy-start.2 = (f32[32,128,256]{2,1,0:T(8,128)}, f32[32,128,256]{2,1,0:T(8,128)S(1)}, u32[]{:S(2)}) copy-start(f32[32,128,256]{2,1,0:T(8,128)S(1)} %get-tuple-element.22) | copy-start | bytes 12582916
  167.1 3.8 %copy-start.17 = (s32[128]{0:T(128)S(1)}, s32[128]{0:T(128)}, u32[]{:S(2)}) copy-start(s32[128]{0:T(128)} %get-tuple-element.47) | copy-start | bytes 1540
  167.2 3.8 %copy-start.19 = (s32[128]{0:T(128)S(1)}, s32[128]{0:T(128)}, u32[]{:S(2)}) copy-start(s32[128]{0:T(128)} %get-tuple-element.48) | copy-start | bytes 1540
  167.2 3.8 %copy-start.21 = (f32[128]{0:T(128)S(1)}, f32[128]{0:T(128)}, u32[]{:S(2)}) copy-start(f32[128]{0:T(128)} %get-tuple-element.51) | copy-start | bytes 1540
  167.2 3.8 %copy-start.23 = (f32[128]{0:T(128)S(1)}, f32[128]{0:T(128)}, u32[]{:S(2)}) copy-start(f32[128]{0:T(128)} %get-tuple-element.52) | copy-start | bytes 1540
  171.6 51.5 %copy-start.7 = (s32[32,3]{0,1:T(4,128)S(1)}, s32[32,3]{0,1:T(4,128)}, u32[]{:S(2)}) copy-start(s32[32,3]{0,1:T(4,128)} %iota_add_fusion.1) | copy-start | bytes 1156
  219.6 7.6 %copy-start.6 = (f32[3,65,9,65]{3,1,2,0:T(8,128)S(1)}, f32[3,65,9,65]{3,1,2,0:T(8,128)}, u32[]{:S(2)}) copy-start(f32[3,65,9,65]{3,1,2,0:T(8,128)} %param.8) | copy-start | bytes 1368904
  219.6 7.6 %copy-start.14 = (s32[4,17]{1,0:T(4,128)S(1)}, s32[4,17]{1,0:T(4,128)}, u32[]{:S(2)}) copy-start(s32[4,17]{1,0:T(4,128)} %iota_add_fusion) | copy-start | bytes 820
  (1 other events, 0.6 us)

commit v5 on v3

--- a/solution.py
+++ b/solution.py
@@ -29,7 +29,7 @@
 from jax.experimental import pallas as pl
 from jax.experimental.pallas import tpu as pltpu
 
-PLANES = 8
+PLANES = 4
 
 
 def _native_kernel(offset_ref, w_ref, lo_ref, hi_ref, sl_ref, sm_ref, keep_ref):

time: 230 us -> 231 us (level)
  no operation moved by 1% of the time
where the time goes in v5:
time: 231 us; the launch traced here: 230 us
  starting transfers between devices  56.6 us (25%)
  other arithmetic  46.7 us (20%)
  blocking collectives  42.6 us (18%)
  waiting for transfers between devices  26.4 us (11%)
  local copies, waits for them, and re-layouts  23.7 us (10%)
  Pallas kernels  12.8 us (6%)
  between operations  11.5 us (5%)
  matrix products  9.33 us (4%)
    all_gather x1, blocking collectives, local(): lax.all_gather(packed.reshape(2, -1), ('grp', 'dev'))  42.6 us
    ppermute x14, starting transfers between devices, allsum(): values = values + lax.ppermute(values, axis, pairs)  30.6 us
    reduce_sum x2, other arithmetic, local(): warped = sample + jnp.sum(shift_field * slopes, axis=0)  16.4 us
    ppermute x14, waiting for transfers between devices, allsum(): values = values + lax.ppermute(values, axis, pairs)  16.2 us
    pallas_call x1, Pallas kernels, native_slopes(): pl.pallas_call(_native_kernel, grid_spec=spec, out_shape=[jax.ShapeDtypeS...  12.8 us
    ppermute x2, starting transfers between devices, share_nodes(): before = lax.ppermute(last, axis, up)  11.9 us
    add x14, other arithmetic, allsum(): values = values + lax.ppermute(values, axis, pairs)  8.07 us
    reduce_sum x2, other arithmetic, restrict(): jnp.sum(terms * hat_x[None, :, i, None, None], axis=1)  7.3 us
  transfers between devices with their start and end apart: 22, of which 19 were waited for; matrix products, arithmetic and copies ran while one was open for 4% of the time, Pallas kernels for 0%

profile of v5, /device:TPU:1, one launch (start us, length us, event | category | flops | bytes accessed | tf_op | source)
XLA Modules:
  0.0 229.6 jit_solution(17075176448269318157)
XLA Ops:
  0.6 2.5 %fusion.107 = (bf16[9,128,256]{2,1,0:T(8,128)(2,1)}, bf16[9,128,256]{2,1,0:T(8,128)(2,1)}) fusion(bf16[32,128,256]{2,1,0:T(8,128)(2,1)} %param.6), kind=kLoop, calls=%fused_computation.181 | loop fusion | bytes 2359296 | tf_op jit(solution)/shard_map/slice | solution.py:22
  3.1 4.5 %collective-permute-start = (bf16[9,128,256]{2,1,0:T(8,128)(2,1)}, bf16[9,128,256]{2,1,0:T(8,128)(2,1)}, u32[]{:S(2)}, u32[]{:S(2)}) collective-permute-start(bf16[9,128,256]{2,1,0:T(8,128)(2,1)} %get-tuple-element.28), channel_id=1, source_target_pairs={{0,1},{1,2},{2,3},{3,4},{4,5},{5,6},{6,7},{7,8},{8,9},{9,10},{10,1... | collective-permute-start | bytes 1769480 | tf_op jit(solution)/shard_map/ppermute | solution.py:23
  7.6 1.9 collective-permute-start.1
  9.7 1.3 constant_dynamic-slice_fusion
  12.6 1.8 convert_reduce_fusion
  16.0 3.1 %collective-permute-done.1 = bf16[9,128,256]{2,1,0:T(8,128)(2,1)} collective-permute-done((bf16[9,128,256]{2,1,0:T(8,128)(2,1)}, bf16[9,128,256]{2,1,0:T(8,128)(2,1)}, u32[]{:S(2)}, u32[]{:S(2)}) %collective-permute-start.1) | collective-permute-done | bytes 589856 | tf_op jit(solution)/shard_map/ppermute | solution.py:24
  20.3 1.7 copy-done.4
  21.9 2.6 %fusion.106 = (bf16[50,128,1]{2,1,0:T(8,128)(2,1)}, bf16[50,128,1]{2,1,0:T(8,128)(2,1)}) fusion(bf16[50,128,256]{2,1,0:T(8,128)(2,1)S(1)} %constant_dynamic-update-slice_fusion.w_ref), kind=kLoop, calls=%fused_computation.180 | loop fusion | bytes 51200 | tf_op jit(solution)/shard_map/slice | solution.py:220
  24.5 2.0 copy.34
  26.5 3.2 %collective-permute-start.2 = (bf16[50,128,1]{1,0,2:T(8,128)(2,1)S(1)}, bf16[50,128,1]{1,0,2:T(8,128)(2,1)S(1)}, u32[]{:S(2)}, u32[]{:S(2)}) collective-permute-start(bf16[50,128,1]{1,0,2:T(8,128)(2,1)S(1)} %copy.34), channel_id=1, source_target_pairs={{0,32},{32,64},{64,96},{1,33},{33,65},{65,97},{2,34},{34,66},{66,9... | collective-permute-start | bytes 38408 | tf_op jit(solution)/shard_map/ppermute | solution.py:219
  29.7 2.0 copy.35
  33.7 1.7 copy.36.lo_ref
  36.2 1.7 copy.37.hi_ref
  37.9 12.8 %shard_map.76 = (f32[3,32,128,256]{3,2,1,0:T(8,128)}, f32[32,128,256]{2,1,0:T(8,128)}) custom-call(s32[1]{0:T(128)} %bitcast.118.offset_ref, bf16[50,128,256]{2,1,0:T(8,128)(2,1)} %copy-done.4, bf16[50,128,1]{2,1,0:T(8,128)(2,1)} %copy.36.lo_ref, bf16[50,128,1]{2,1,0:T(8,128)(2,1)} %copy.37.hi_ref), custom_call_target="tpu_custom_call" | custom-call | tf_op jit(solution)/shard_map/pallas_call | solution.py:95
  50.6 8.2 %multiply_reduce_fusion.7 = f32[32,128,256]{2,1,0:T(8,128)S(1)} fusion(f32[3,32,128,256]{3,2,1,0:T(8,128)} %get-tuple-element.5, f32[3,128,256]{2,1,0:T(8,128)S(1)} %get-tuple-element.33, f32[32]{0:T(128)S(1)} %get-tuple-element.41, f32[3,128,256]{2,1,0:T(8,128)S(1)} %get-tuple-element.34, f32[32]{0:T(128)S(1)} %get-tuple-element.42, ...), kind=kLoop, calls=%fused_computation.7 | loop fusion | flops 20971520 | bytes 17957248 | tf_op jit(solution)/shard_map/reduce_sum | solution.py:239
  58.9 2.2 fusion.104
  61.1 2.9 %pad_maximum_fusion.2 = f32[4]{0:T(128)S(1)} fusion(f32[1]{0:T(128)} %bitcast.18, f32[1]{0:T(128)} %bitcast.17, f32[1]{0:T(128)} %bitcast.6, f32[1]{0:T(128)} %bitcast.5), kind=kLoop, calls=%fused_computation.150 | loop fusion | flops 12 | bytes 32 | tf_op jit(solution)/shard_map/concatenate | solution.py:242
  65.2 2.7 %fusion.116 = f32[4]{0:T(128)S(1)} fusion(f32[4]{0:T(128)S(1)} %collective-permute-done.4, f32[1]{0:T(128)} %bitcast.18, f32[1]{0:T(128)} %bitcast.17, f32[1]{0:T(128)} %bitcast.6, f32[1]{0:T(128)} %bitcast.5), kind=kLoop, calls=%fused_computation.185 | loop fusion | flops 16 | bytes 48 | tf_op jit(solution)/shard_map/add | solution.py:177
  70.3 2.7 %fusion.118 = f32[4]{0:T(128)S(1)} fusion(f32[4]{0:T(128)S(1)} %collective-permute-done.5, f32[4]{0:T(128)S(1)} %collective-permute-done.4, f32[1]{0:T(128)} %bitcast.18, f32[1]{0:T(128)} %bitcast.17, f32[1]{0:T(128)} %bitcast.6, f32[1]{0:T(128)} %bitcast.5), kind=kLoop, calls=%fused_computation.187 | loop fusion | flops 20 | bytes 64 | tf_op jit(solution)/shard_map/add | solution.py:177
  72.9 4.7 %collective-permute-start.6 = (f32[4]{0:T(128)S(1)}, f32[4]{0:T(128)S(1)}, u32[]{:S(2)}, u32[]{:S(2)}) collective-permute-start(f32[4]{0:T(128)S(1)} %fusion.118), channel_id=1, source_target_pairs={{0,4},{1,5},{2,6},{3,7},{4,0},{5,1},{6,2},{7,3},{8,12},{9,13},{10,... | collective-permute-start | bytes 56 | tf_op jit(solution)/shard_map/ppermute | solution.py:177
  78.5 1.9 collective-permute-start.7
  81.4 3.4 %collective-permute-start.8 = (f32[4]{0:T(128)S(1)}, f32[4]{0:T(128)S(1)}, u32[]{:S(2)}, u32[]{:S(2)}) collective-permute-start(f32[4]{0:T(128)S(1)} %add.330), channel_id=1, source_target_pairs={{0,16},{1,17},{2,18},{3,19},{4,20},{5,21},{6,22},{7,23},{8,24},{9,... | collective-permute-start | bytes 56 | tf_op jit(solution)/shard_map/ppermute | solution.py:177
  85.8 1.3 collective-permute-start.9
  88.2 2.6 %collective-permute-start.10 = (f32[4]{0:T(128)S(1)}, f32[4]{0:T(128)S(1)}, u32[]{:S(2)}, u32[]{:S(2)}) collective-permute-start(f32[4]{0:T(128)S(1)} %add.332), channel_id=1, source_target_pairs={{0,64},{32,96},{64,0},{96,32},{1,65},{33,97},{65,1},{97,33},{2,66}... | collective-permute-start | bytes 56 | tf_op jit(solution)/shard_map/ppermute | solution.py:177
  90.8 1.3 collective-permute-done.10
  100.0 3.6 %multiply_reduce_fusion.6 = (f32[3,128,256]{2,1,0:T(8,128)S(1)}, f32[3,128,256]{2,1,0:T(8,128)S(1)}, f32[3,128,256]{2,1,0:T(8,128)S(1)}) fusion(f32[3,32,128,256]{3,2,1,0:T(8,128)S(1)} %bitcast.120, f32[32,128,256]{2,1,0:T(8,128)S(1)} %fusion.1, f32[32]{0:T(128)S(1)} %get-tuple-element.40, f32[32]{0:T(128)S(1)} %get-tuple-element.42, f32[32]{0:T(128)S(1)} %get-tuple-element.41), kind=kLoop, calls=%fused_computation.6 | loop fusion | flops 21725184 | bytes 17957248 | tf_op jit(solution)/shard_map/reduce_sum | solution.py:156
  104.6 8.6 %collective-permute-start.11 = (f32[3,9,17]{2,1,0:T(8,128)S(1)}, f32[3,9,17]{2,1,0:T(8,128)S(1)}, u32[]{:S(2)}, u32[]{:S(2)}) collective-permute-start(f32[3,9,17]{2,1,0:T(8,128)S(1)} %get-tuple-element.37), channel_id=1, source_target_pairs={{0,1},{1,2},{2,3},{3,4},{4,5},{5,6},{6,7},{7,8},{8,9},{9,10},{10,1... | collective-permute-start | bytes 5516 | tf_op jit(solution)/shard_map/ppermute | solution.py:189
  113.2 1.9 collective-permute-start.12
  115.2 3.2 %collective-permute-done.12 = f32[3,9,17]{2,1,0:T(8,128)S(1)} collective-permute-done((f32[3,9,17]{2,1,0:T(8,128)S(1)}, f32[3,9,17]{2,1,0:T(8,128)S(1)}, u32[]{:S(2)}, u32[]{:S(2)}) %collective-permute-start.12) | collective-permute-done | bytes 1868 | tf_op jit(solution)/shard_map/ppermute | solution.py:190
  118.6 3.2 %collective-permute-start.13 = (f32[3,3,9]{2,1,0:T(4,128)S(1)}, f32[3,3,9]{2,1,0:T(4,128)S(1)}, u32[]{:S(2)}, u32[]{:S(2)}) collective-permute-start(f32[3,3,9]{2,1,0:T(4,128)S(1)} %get-tuple-element.19), channel_id=1, source_target_pairs={{0,32},{32,64},{64,96},{1,33},{33,65},{65,97},{2,34},{34,66},{66,9... | collective-permute-start | bytes 980 | tf_op jit(solution)/shard_map/ppermute | solution.py:189
  123.4 2.8 %collective-permute-done.14 = f32[3,3,9]{2,1,0:T(4,128)S(1)} collective-permute-done((f32[3,3,9]{2,1,0:T(4,128)S(1)}, f32[3,3,9]{2,1,0:T(4,128)S(1)}, u32[]{:S(2)}, u32[]{:S(2)}) %collective-permute-start.14) | collective-permute-done | bytes 356 | tf_op jit(solution)/shard_map/ppermute | solution.py:190
  128.0 8.2 %multiply_reduce_fusion.3 = f32[32,128,256]{2,1,0:T(8,128)S(1)} fusion(f32[3,32,128,256]{3,2,1,0:T(8,128)} %get-tuple-element.5, f32[3,128,256]{2,1,0:T(8,128)S(1)} %get-tuple-element.30, f32[3,128,256]{2,1,0:T(8,128)S(1)} %get-tuple-element.31, f32[3,128,256]{2,1,0:T(8,128)S(1)} %get-tuple-element.29, f32[32]{0:T(128)S(1)} %get-tuple-element.41, ...), kind=kLoop, calls=%fused_computation.3 | loop fusion | flops 20971520 | bytes 17957248 | tf_op jit(solution)/shard_map/reduce_sum | solution.py:239
  136.3 2.2 fusion.103
  138.4 1.6 pad_maximum_fusion.3
  141.2 1.4 fusion.115
  142.6 1.8 collective-permute-start.16
  145.4 1.4 fusion.117
  146.8 5.3 %collective-permute-start.17 = (f32[2]{0:T(128)S(1)}, f32[2]{0:T(128)S(1)}, u32[]{:S(2)}, u32[]{:S(2)}) collective-permute-start(f32[2]{0:T(128)S(1)} %fusion.117), channel_id=1, source_target_pairs={{0,4},{1,5},{2,6},{3,7},{4,0},{5,1},{6,2},{7,3},{8,12},{9,13},{10,... | collective-permute-start | bytes 32 | tf_op jit(solution)/shard_map/ppermute | solution.py:177
  153.0 2.1 collective-permute-start.18
  156.0 3.4 %collective-permute-start.19 = (f32[2]{0:T(128)S(1)}, f32[2]{0:T(128)S(1)}, u32[]{:S(2)}, u32[]{:S(2)}) collective-permute-start(f32[2]{0:T(128)S(1)} %add.349), channel_id=1, source_target_pairs={{0,16},{1,17},{2,18},{3,19},{4,20},{5,21},{6,22},{7,23},{8,24},{9,... | collective-permute-start | bytes 32 | tf_op jit(solution)/shard_map/ppermute | solution.py:177
  161.4 1.4 collective-permute-done.20
  162.9 1.8 collective-permute-start.21
  164.6 2.1 collective-permute-done.21
  170.1 1.8 multiply_reduce_fusion.8
  172.2 3.7 %multiply_reduce_fusion.2 = (f32[3,128,256]{2,1,0:T(8,128)S(1)}, f32[3,128,256]{2,1,0:T(8,128)S(1)}, f32[3,128,256]{2,1,0:T(8,128)S(1)}) fusion(f32[3,32,128,256]{3,2,1,0:T(8,128)S(1)} %bitcast.122, f32[32,128,256]{2,1,0:T(8,128)S(1)} %get-tuple-element.22, f32[32]{0:T(128)S(1)} %get-tuple-element.40, f32[32]{0:T(128)S(1)} %get-tuple-element.42, ...), kind=kLoop, calls=%fused_computation.2 | loop fusion | flops 21725184 | bytes 17957248 | tf_op jit(solution)/shard_map/reduce_sum | solution.py:156
  177.8 42.6 %all_gather.3 = f32[128,2,689]{2,1,0:T(2,128)S(1)} all-gather(f32[1,2,689]{2,1,0:T(2,128)S(1)} %all_gather_reshape.3), channel_id=1, replica_groups=mesh['grp'=4,'dev'=32] {'grp','dev'}, dimensions={0}, use_global_device_ids=true | all-gather | bytes 711048 | tf_op jit(solution)/shard_map/all_gather | solution.py:258
  223.9 2.4 %fusion.5 = f32[4,3,65,9,17]{2,4,0,3,1:T(8,128)S(1)} fusion(f32[4,32,3,3,9,17]{1,0,5,4,3,2:T(4,128)S(1)} %reshape.189, s32[32,3]{0,1:T(4,128)S(1)} %iota_add_fusion.1), kind=kOutput, calls=%fused_computation.19 | convolution fusion | flops 137485920 | bytes 1182768 | tf_op jit(solution)/shard_map/pqcijk,qix->pcxjk/dot_general | solution.py:203
  226.3 2.2 fusion.9
  (105 shorter events, 32.9 us)
Async XLA Ops:
  0.6 11.9 %copy-start = (bf16[32,128,256]{2,1,0:T(8,128)(2,1)S(1)}, bf16[32,128,256]{2,1,0:T(8,128)(2,1)}, u32[]{:S(2)}) copy-start(bf16[32,128,256]{2,1,0:T(8,128)(2,1)} %param.5) | copy-start | bytes 6291460
  3.1 11.6 %collective-permute-start = (bf16[9,128,256]{2,1,0:T(8,128)(2,1)}, bf16[9,128,256]{2,1,0:T(8,128)(2,1)}, u32[]{:S(2)}, u32[]{:S(2)}) collective-permute-start(bf16[9,128,256]{2,1,0:T(8,128)(2,1)} %get-tuple-element.28), channel_id=1, source_target_pairs={{0,1},{1,2},{2,3},{3,4},{4,5},{5,6},{6,7},{7,8},{8,9},{9,10},{10,1... | collective-permute-start | bytes 1769480 | tf_op jit(solution)/shard_map/ppermute | solution.py:23
  7.6 11.5 %collective-permute-start.1 = (bf16[9,128,256]{2,1,0:T(8,128)(2,1)}, bf16[9,128,256]{2,1,0:T(8,128)(2,1)}, u32[]{:S(2)}, u32[]{:S(2)}) collective-permute-start(bf16[9,128,256]{2,1,0:T(8,128)(2,1)} %get-tuple-element.27), channel_id=1, source_target_pairs={{1,0},{2,1},{3,2},{4,3},{5,4},{6,5},{7,6},{8,7},{9,8},{10,9},{11,1... | collective-permute-start | bytes 1769480 | tf_op jit(solution)/shard_map/ppermute | solution.py:24
  9.6 6.2 %copy-start.5 = (bf16[32,128,256]{2,1,0:T(8,128)(2,1)S(1)}, bf16[32,128,256]{2,1,0:T(8,128)(2,1)}, u32[]{:S(2)}) copy-start(bf16[32,128,256]{2,1,0:T(8,128)(2,1)} %param.6) | copy-start | bytes 6291460
  20.3 1.7 copy-start.4
  26.5 7.2 %collective-permute-start.2 = (bf16[50,128,1]{1,0,2:T(8,128)(2,1)S(1)}, bf16[50,128,1]{1,0,2:T(8,128)(2,1)S(1)}, u32[]{:S(2)}, u32[]{:S(2)}) collective-permute-start(bf16[50,128,1]{1,0,2:T(8,128)(2,1)S(1)} %copy.34), channel_id=1, source_target_pairs={{0,32},{32,64},{64,96},{1,33},{33,65},{65,97},{2,34},{34,66},{66,9... | collective-permute-start | bytes 38408 | tf_op jit(solution)/shard_map/ppermute | solution.py:219
  31.7 4.5 %collective-permute-start.3 = (bf16[50,128,1]{1,0,2:T(8,128)(2,1)S(1)}, bf16[50,128,1]{1,0,2:T(8,128)(2,1)S(1)}, u32[]{:S(2)}, u32[]{:S(2)}) collective-permute-start(bf16[50,128,1]{1,0,2:T(8,128)(2,1)S(1)} %copy.35), channel_id=1, source_target_pairs={{32,0},{64,32},{96,64},{33,1},{65,33},{97,65},{34,2},{66,34},{98,6... | collective-permute-start | bytes 38408 | tf_op jit(solution)/shard_map/ppermute | solution.py:220
  50.6 8.2 %copy-start.1 = (f32[32,128,256]{2,1,0:T(8,128)S(1)}, f32[32,128,256]{2,1,0:T(8,128)}, u32[]{:S(2)}) copy-start(f32[32,128,256]{2,1,0:T(8,128)} %get-tuple-element.6) | copy-start | bytes 12582916
  58.9 39.9 %slice-start = ((s8[12582912]{0:T(1024)(128)(4,1)}), s8[4194304]{0:T(1024)(128)(4,1)S(1)}, s32[]{:S(2)}) async-start(s8[12582912]{0:T(1024)(128)(4,1)} %bitcast.119), calls=%async_computation | async-start | bytes 8388608
  58.9 39.9 %slice-start.1 = ((s8[12582912]{0:T(1024)(128)(4,1)}), s8[4194304]{0:T(1024)(128)(4,1)S(1)}, s32[]{:S(2)}) async-start(s8[12582912]{0:T(1024)(128)(4,1)} %bitcast.119), calls=%async_computation.1 | async-start | bytes 8388608
  64.0 1.2 collective-permute-start.4
  67.8 2.4 %collective-permute-start.5 = (f32[4]{0:T(128)S(1)}, f32[4]{0:T(128)S(1)}, u32[]{:S(2)}, u32[]{:S(2)}) collective-permute-start(f32[4]{0:T(128)S(1)} %fusion.116), channel_id=1, source_target_pairs={{0,2},{1,3},{2,0},{3,1},{4,6},{5,7},{6,4},{7,5},{8,10},{9,11},{10,... | collective-permute-start | bytes 56 | tf_op jit(solution)/shard_map/ppermute | solution.py:177
  72.9 5.6 %collective-permute-start.6 = (f32[4]{0:T(128)S(1)}, f32[4]{0:T(128)S(1)}, u32[]{:S(2)}, u32[]{:S(2)}) collective-permute-start(f32[4]{0:T(128)S(1)} %fusion.118), channel_id=1, source_target_pairs={{0,4},{1,5},{2,6},{3,7},{4,0},{5,1},{6,2},{7,3},{8,12},{9,13},{10,... | collective-permute-start | bytes 56 | tf_op jit(solution)/shard_map/ppermute | solution.py:177
  78.5 2.8 %collective-permute-start.7 = (f32[4]{0:T(128)S(1)}, f32[4]{0:T(128)S(1)}, u32[]{:S(2)}, u32[]{:S(2)}) collective-permute-start(f32[4]{0:T(128)S(1)} %add.329), channel_id=1, source_target_pairs={{0,8},{1,9},{2,10},{3,11},{4,12},{5,13},{6,14},{7,15},{8,0},{9,1},... | collective-permute-start | bytes 56 | tf_op jit(solution)/shard_map/ppermute | solution.py:177
  81.4 4.4 %collective-permute-start.8 = (f32[4]{0:T(128)S(1)}, f32[4]{0:T(128)S(1)}, u32[]{:S(2)}, u32[]{:S(2)}) collective-permute-start(f32[4]{0:T(128)S(1)} %add.330), channel_id=1, source_target_pairs={{0,16},{1,17},{2,18},{3,19},{4,20},{5,21},{6,22},{7,23},{8,24},{9,... | collective-permute-start | bytes 56 | tf_op jit(solution)/shard_map/ppermute | solution.py:177
  85.8 2.4 %collective-permute-start.9 = (f32[4]{0:T(128)S(1)}, f32[4]{0:T(128)S(1)}, u32[]{:S(2)}, u32[]{:S(2)}) collective-permute-start(f32[4]{0:T(128)S(1)} %add.331), channel_id=1, source_target_pairs={{0,32},{32,0},{64,96},{96,64},{1,33},{33,1},{65,97},{97,65},{2,34}... | collective-permute-start | bytes 56 | tf_op jit(solution)/shard_map/ppermute | solution.py:177
  88.2 3.9 %collective-permute-start.10 = (f32[4]{0:T(128)S(1)}, f32[4]{0:T(128)S(1)}, u32[]{:S(2)}, u32[]{:S(2)}) collective-permute-start(f32[4]{0:T(128)S(1)} %add.332), channel_id=1, source_target_pairs={{0,64},{32,96},{64,0},{96,32},{1,65},{33,97},{65,1},{97,33},{2,66}... | collective-permute-start | bytes 56 | tf_op jit(solution)/shard_map/ppermute | solution.py:177
  97.8 2.2 slice-start.2
  104.6 10.6 %collective-permute-start.11 = (f32[3,9,17]{2,1,0:T(8,128)S(1)}, f32[3,9,17]{2,1,0:T(8,128)S(1)}, u32[]{:S(2)}, u32[]{:S(2)}) collective-permute-start(f32[3,9,17]{2,1,0:T(8,128)S(1)} %get-tuple-element.37), channel_id=1, source_target_pairs={{0,1},{1,2},{2,3},{3,4},{4,5},{5,6},{6,7},{7,8},{8,9},{9,10},{10,1... | collective-permute-start | bytes 5516 | tf_op jit(solution)/shard_map/ppermute | solution.py:189
  113.2 5.1 %collective-permute-start.12 = (f32[3,9,17]{2,1,0:T(8,128)S(1)}, f32[3,9,17]{2,1,0:T(8,128)S(1)}, u32[]{:S(2)}, u32[]{:S(2)}) collective-permute-start(f32[3,9,17]{2,1,0:T(8,128)S(1)} %get-tuple-element.38), channel_id=1, source_target_pairs={{1,0},{2,1},{3,2},{4,3},{5,4},{6,5},{7,6},{8,7},{9,8},{10,9},{11,1... | collective-permute-start | bytes 5516 | tf_op jit(solution)/shard_map/ppermute | solution.py:190
  118.6 4.7 %collective-permute-start.13 = (f32[3,3,9]{2,1,0:T(4,128)S(1)}, f32[3,3,9]{2,1,0:T(4,128)S(1)}, u32[]{:S(2)}, u32[]{:S(2)}) collective-permute-start(f32[3,3,9]{2,1,0:T(4,128)S(1)} %get-tuple-element.19), channel_id=1, source_target_pairs={{0,32},{32,64},{64,96},{1,33},{33,65},{65,97},{2,34},{34,66},{66,9... | collective-permute-start | bytes 980 | tf_op jit(solution)/shard_map/ppermute | solution.py:189
  121.8 4.4 %collective-permute-start.14 = (f32[3,3,9]{2,1,0:T(4,128)S(1)}, f32[3,3,9]{2,1,0:T(4,128)S(1)}, u32[]{:S(2)}, u32[]{:S(2)}) collective-permute-start(f32[3,3,9]{2,1,0:T(4,128)S(1)} %get-tuple-element.20), channel_id=1, source_target_pairs={{32,0},{64,32},{96,64},{33,1},{65,33},{97,65},{34,2},{66,34},{98,6... | collective-permute-start | bytes 980 | tf_op jit(solution)/shard_map/ppermute | solution.py:190
  128.0 8.2 %copy-start.2 = (f32[32,128,256]{2,1,0:T(8,128)S(1)}, f32[32,128,256]{2,1,0:T(8,128)}, u32[]{:S(2)}) copy-start(f32[32,128,256]{2,1,0:T(8,128)} %get-tuple-element.6) | copy-start | bytes 12582916
  136.2 35.6 %slice-start.3 = ((s8[12582912]{0:T(1024)(128)(4,1)}), s8[4194304]{0:T(1024)(128)(4,1)S(1)}, s32[]{:S(2)}) async-start(s8[12582912]{0:T(1024)(128)(4,1)} %bitcast.121), calls=%async_computation.3 | async-start | bytes 8388608
  136.3 35.6 %slice-start.4 = ((s8[12582912]{0:T(1024)(128)(4,1)}), s8[4194304]{0:T(1024)(128)(4,1)S(1)}, s32[]{:S(2)}) async-start(s8[12582912]{0:T(1024)(128)(4,1)} %bitcast.121), calls=%async_computation.4 | async-start | bytes 8388608
  140.1 1.2 collective-permute-start.15
  142.6 2.8 %collective-permute-start.16 = (f32[2]{0:T(128)S(1)}, f32[2]{0:T(128)S(1)}, u32[]{:S(2)}, u32[]{:S(2)}) collective-permute-start(f32[2]{0:T(128)S(1)} %fusion.115), channel_id=1, source_target_pairs={{0,2},{1,3},{2,0},{3,1},{4,6},{5,7},{6,4},{7,5},{8,10},{9,11},{10,... | collective-permute-start | bytes 32 | tf_op jit(solution)/shard_map/ppermute | solution.py:177
  146.8 6.3 %collective-permute-start.17 = (f32[2]{0:T(128)S(1)}, f32[2]{0:T(128)S(1)}, u32[]{:S(2)}, u32[]{:S(2)}) collective-permute-start(f32[2]{0:T(128)S(1)} %fusion.117), channel_id=1, source_target_pairs={{0,4},{1,5},{2,6},{3,7},{4,0},{5,1},{6,2},{7,3},{8,12},{9,13},{10,... | collective-permute-start | bytes 32 | tf_op jit(solution)/shard_map/ppermute | solution.py:177
  153.0 3.0 %collective-permute-start.18 = (f32[2]{0:T(128)S(1)}, f32[2]{0:T(128)S(1)}, u32[]{:S(2)}, u32[]{:S(2)}) collective-permute-start(f32[2]{0:T(128)S(1)} %add.348), channel_id=1, source_target_pairs={{0,8},{1,9},{2,10},{3,11},{4,12},{5,13},{6,14},{7,15},{8,0},{9,1},... | collective-permute-start | bytes 32 | tf_op jit(solution)/shard_map/ppermute | solution.py:177
  156.0 4.4 %collective-permute-start.19 = (f32[2]{0:T(128)S(1)}, f32[2]{0:T(128)S(1)}, u32[]{:S(2)}, u32[]{:S(2)}) collective-permute-start(f32[2]{0:T(128)S(1)} %add.349), channel_id=1, source_target_pairs={{0,16},{1,17},{2,18},{3,19},{4,20},{5,21},{6,22},{7,23},{8,24},{9,... | collective-permute-start | bytes 32 | tf_op jit(solution)/shard_map/ppermute | solution.py:177
  160.4 2.4 %collective-permute-start.20 = (f32[2]{0:T(128)S(1)}, f32[2]{0:T(128)S(1)}, u32[]{:S(2)}, u32[]{:S(2)}) collective-permute-start(f32[2]{0:T(128)S(1)} %add.350), channel_id=1, source_target_pairs={{0,32},{32,0},{64,96},{96,64},{1,33},{33,1},{65,97},{97,65},{2,34}... | collective-permute-start | bytes 32 | tf_op jit(solution)/shard_map/ppermute | solution.py:177
  162.9 3.9 %collective-permute-start.21 = (f32[2]{0:T(128)S(1)}, f32[2]{0:T(128)S(1)}, u32[]{:S(2)}, u32[]{:S(2)}) collective-permute-start(f32[2]{0:T(128)S(1)} %add.351), channel_id=1, source_target_pairs={{0,64},{32,96},{64,0},{96,32},{1,65},{33,97},{65,1},{97,33},{2,66}... | collective-permute-start | bytes 32 | tf_op jit(solution)/shard_map/ppermute | solution.py:177
  170.0 2.2 slice-start.5
  171.8 4.1 %copy-start.3 = (f32[32,128,256]{2,1,0:T(8,128)}, f32[32,128,256]{2,1,0:T(8,128)S(1)}, u32[]{:S(2)}) copy-start(f32[32,128,256]{2,1,0:T(8,128)S(1)} %get-tuple-element.22) | copy-start | bytes 12582916
  223.8 2.4 %copy-start.6 = (f32[3,65,9,65]{3,1,2,0:T(8,128)S(1)}, f32[3,65,9,65]{3,1,2,0:T(8,128)}, u32[]{:S(2)}) copy-start(f32[3,65,9,65]{3,1,2,0:T(8,128)} %param.8) | copy-start | bytes 1368904
  223.9 2.4 %copy-start.7 = (f32[3,65,9,65]{3,1,2,0:T(8,128)S(1)}, f32[3,65,9,65]{3,1,2,0:T(8,128)}, u32[]{:S(2)}) copy-start(f32[3,65,9,65]{3,1,2,0:T(8,128)} %param.9) | copy-start | bytes 1368904

commit v6 on v4

--- a/solution.py
+++ b/solution.py
@@ -29,7 +29,7 @@
 from jax.experimental import pallas as pl
 from jax.experimental.pallas import tpu as pltpu
 
-PLANES = 8
+PLANES = 4
 
 
 def _native_kernel(offset_ref, w_ref, lo_ref, hi_ref, q_ref, sl_ref, wp_ref, mo_ref, keep_ref):

time: 233 us -> 233 us (level)
  no operation moved by 1% of the time
where the time goes in v6:
time: 233 us; the launch traced here: 232 us
  starting transfers between devices  58.5 us (25%)
  blocking collectives  45.3 us (19%)
  other arithmetic  40.3 us (17%)
  local copies, waits for them, and re-layouts  26.2 us (11%)
  waiting for transfers between devices  19.6 us (8%)
  matrix products  15.5 us (7%)
  Pallas kernels  14.8 us (6%)
  between operations  11.4 us (5%)
    all_gather x1, blocking collectives, local(): lax.all_gather(packed.reshape(2, -1), ('grp', 'dev'))  45.3 us
    ppermute x14, starting transfers between devices, allsum(): values = values + lax.ppermute(values, axis, pairs)  31.9 us
    pallas_call x1, Pallas kernels, native_slopes(): pl.pallas_call(_native_kernel, grid_spec=spec, out_shape=[jax.ShapeDtypeS...  14.8 us
    ppermute x14, waiting for transfers between devices, allsum(): values = values + lax.ppermute(values, axis, pairs)  14.4 us
    ppermute x2, starting transfers between devices, share_nodes(): before = lax.ppermute(last, axis, up)  12.3 us
    reduce_sum x2, other arithmetic, restrict(): jnp.sum(terms * hat_x[None, :, i, None, None], axis=1)  10.6 us
    reduce_sum x1, other arithmetic, local(): warped = warped + jnp.sum(shift_field * slopes, axis=0)  8.27 us
  transfers between devices with their start and end apart: 22, of which 17 were waited for; matrix products, arithmetic and copies ran while one was open for 6% of the time, Pallas kernels for 0%

profile of v6, /device:TPU:1, one launch (start us, length us, event | category | flops | bytes accessed | tf_op | source)
XLA Modules:
  0.0 231.7 jit_solution(9160734892073962967)
XLA Ops:
  0.6 2.5 %fusion.107 = (bf16[9,128,256]{2,1,0:T(8,128)(2,1)}, bf16[9,128,256]{2,1,0:T(8,128)(2,1)}) fusion(bf16[32,128,256]{2,1,0:T(8,128)(2,1)} %param.6), kind=kLoop, calls=%fused_computation.176 | loop fusion | bytes 2359296 | tf_op jit(solution)/shard_map/slice | solution.py:22
  3.1 4.5 %collective-permute-start = (bf16[9,128,256]{2,1,0:T(8,128)(2,1)}, bf16[9,128,256]{2,1,0:T(8,128)(2,1)S(1)}, u32[]{:S(2)}, u32[]{:S(2)}) collective-permute-start(bf16[9,128,256]{2,1,0:T(8,128)(2,1)} %get-tuple-element.27), channel_id=1, source_target_pairs={{0,1},{1,2},{2,3},{3,4},{4,5},{5,6},{6,7},{7,8},{8,9},{9,10},{10,1... | collective-permute-start | bytes 1769480 | tf_op jit(solution)/shard_map/ppermute | solution.py:23
  7.6 1.9 collective-permute-start.1
  10.7 1.3 constant_dynamic-slice_fusion
  12.4 2.8 %convolution_bitcast_fusion.1.q_ref = f32[3,3,128,256]{3,2,1,0:T(8,128)} fusion(f32[3,3,9,256]{3,2,1,0:T(8,128)S(1)} %fusion.29, f32[128]{0:T(128)} %get-tuple-element.51, s32[128]{0:T(128)} %get-tuple-element.48, f32[128]{0:T(128)} %get-tuple-element.52, s32[128]{0:T(128)} %get-tuple-element.47), kind=kOutput, calls=%fused_computation.20 | convolution fusion | flops 31856256 | bytes 1264640 | tf_op jit(solution)/shard_map/cijz,yj->ciyz/dot_general | solution.py:164
  15.2 1.7 convert_reduce_fusion
  17.2 1.9 collective-permute-done.1
  19.1 1.7 copy-done.3
  20.8 2.6 %fusion.106 = (bf16[50,128,1]{2,1,0:T(8,128)(2,1)}, bf16[50,128,1]{2,1,0:T(8,128)(2,1)}) fusion(bf16[50,128,256]{2,1,0:T(8,128)(2,1)S(1)} %constant_dynamic-update-slice_fusion.w_ref), kind=kLoop, calls=%fused_computation.175 | loop fusion | bytes 51200 | tf_op jit(solution)/shard_map/slice | solution.py:240
  23.3 2.0 copy.34
  25.4 3.2 %collective-permute-start.2 = (bf16[50,128,1]{1,0,2:T(8,128)(2,1)S(1)}, bf16[50,128,1]{1,0,2:T(8,128)(2,1)S(1)}, u32[]{:S(2)}, u32[]{:S(2)}) collective-permute-start(bf16[50,128,1]{1,0,2:T(8,128)(2,1)S(1)} %copy.34), channel_id=1, source_target_pairs={{0,32},{32,64},{64,96},{1,33},{33,65},{65,97},{2,34},{34,66},{66,9... | collective-permute-start | bytes 38408 | tf_op jit(solution)/shard_map/ppermute | solution.py:239
  28.6 2.0 copy.35
  30.6 1.3 collective-permute-start.3
  33.1 1.7 copy.37.lo_ref
  35.0 1.7 copy.38.hi_ref
  36.7 14.8 %shard_map.76 = (f32[3,32,128,256]{3,2,1,0:T(8,128)}, f32[32,128,256]{2,1,0:T(8,128)}, f32[2,128,256]{2,1,0:T(8,128)}) custom-call(s32[1]{0:T(128)} %bitcast.112.offset_ref, bf16[50,128,256]{2,1,0:T(8,128)(2,1)} %copy-done.3, bf16[50,128,1]{2,1,0:T(8,128)(2,1)} %copy.37.lo_ref, bf16[50,128,1]{2,1,0:T(8,128)(2,1)} %copy.38.hi_ref, ...), custom_call_target="tpu_custom_call" | custom-call | tf_op jit(solution)/shard_map/pallas_call | solution.py:114
  58.7 4.7 %collective-permute-start.6 = (f32[4]{0:T(128)S(1)}, f32[4]{0:T(128)S(1)}, u32[]{:S(2)}, u32[]{:S(2)}) collective-permute-start(f32[4]{0:T(128)S(1)} %add.295), channel_id=1, source_target_pairs={{0,4},{1,5},{2,6},{3,7},{4,0},{5,1},{6,2},{7,3},{8,12},{9,13},{10,... | collective-permute-start | bytes 56 | tf_op jit(solution)/shard_map/ppermute | solution.py:197
  64.3 2.0 collective-permute-start.7
  67.2 3.4 %collective-permute-start.8 = (f32[4]{0:T(128)S(1)}, f32[4]{0:T(128)S(1)}, u32[]{:S(2)}, u32[]{:S(2)}) collective-permute-start(f32[4]{0:T(128)S(1)} %add.297), channel_id=1, source_target_pairs={{0,16},{1,17},{2,18},{3,19},{4,20},{5,21},{6,22},{7,23},{8,24},{9,... | collective-permute-start | bytes 56 | tf_op jit(solution)/shard_map/ppermute | solution.py:197
  71.6 1.3 collective-permute-start.9
  74.0 2.9 %collective-permute-start.10 = (f32[4]{0:T(128)S(1)}, f32[4]{0:T(128)S(1)}, u32[]{:S(2)}, u32[]{:S(2)}) collective-permute-start(f32[4]{0:T(128)S(1)} %add.299), channel_id=1, source_target_pairs={{0,64},{32,96},{64,0},{96,32},{1,65},{33,97},{65,1},{97,33},{2,66}... | collective-permute-start | bytes 56 | tf_op jit(solution)/shard_map/ppermute | solution.py:197
  83.6 2.9 %fusion.1 = f32[32,128,256]{2,1,0:T(8,128)S(1)} fusion(bf16[32,128,256]{2,1,0:T(8,128)(2,1)S(1)} %copy-done, f32[32,128,256]{2,1,0:T(8,128)} %get-tuple-element.8, f32[]{:T(128)} %bitcast.13, f32[]{:T(128)} %bitcast.12, f32[]{:T(128)} %bitcast.11), kind=kLoop, calls=%fused_computation.11 | loop fusion | flops 5242880 | bytes 10485772 | tf_op jit(solution)/shard_map/sub | solution.py:279
  86.5 6.9 %multiply_reduce_fusion.6 = (f32[3,128,256]{2,1,0:T(8,128)S(1)}, f32[3,128,256]{2,1,0:T(8,128)S(1)}, f32[3,128,256]{2,1,0:T(8,128)S(1)}) fusion(f32[3,32,128,256]{3,2,1,0:T(8,128)} %get-tuple-element.6, f32[32]{0:T(128)S(1)} %get-tuple-element.38, f32[32,128,256]{2,1,0:T(8,128)S(1)} %fusion.1, f32[32]{0:T(128)S(1)} %get-tuple-element.37, ...), kind=kLoop, calls=%fused_computation.6 | loop fusion | flops 21725184 | bytes 17957248 | tf_op jit(solution)/shard_map/reduce_sum | solution.py:176
  94.4 8.8 %collective-permute-start.11 = (f32[3,9,17]{2,1,0:T(8,128)S(1)}, f32[3,9,17]{2,1,0:T(8,128)S(1)}, u32[]{:S(2)}, u32[]{:S(2)}) collective-permute-start(f32[3,9,17]{2,1,0:T(8,128)S(1)} %get-tuple-element.33), channel_id=1, source_target_pairs={{0,1},{1,2},{2,3},{3,4},{4,5},{5,6},{6,7},{7,8},{8,9},{9,10},{10,1... | collective-permute-start | bytes 5516 | tf_op jit(solution)/shard_map/ppermute | solution.py:209
  103.2 1.9 collective-permute-start.12
  105.2 3.2 %collective-permute-done.12 = f32[3,9,17]{2,1,0:T(8,128)S(1)} collective-permute-done((f32[3,9,17]{2,1,0:T(8,128)S(1)}, f32[3,9,17]{2,1,0:T(8,128)S(1)}, u32[]{:S(2)}, u32[]{:S(2)}) %collective-permute-start.12) | collective-permute-done | bytes 1868 | tf_op jit(solution)/shard_map/ppermute | solution.py:210
  109.1 3.5 %collective-permute-start.13 = (f32[3,3,9]{2,1,0:T(4,128)S(1)}, f32[3,3,9]{2,1,0:T(4,128)S(1)}, u32[]{:S(2)}, u32[]{:S(2)}) collective-permute-start(f32[3,3,9]{2,1,0:T(4,128)S(1)} %get-tuple-element.19), channel_id=1, source_target_pairs={{0,32},{32,64},{64,96},{1,33},{33,65},{65,97},{2,34},{34,66},{66,9... | collective-permute-start | bytes 980 | tf_op jit(solution)/shard_map/ppermute | solution.py:209
  112.6 1.5 collective-permute-start.14
  116.1 1.5 copy.44
  117.6 1.5 copy.45
  121.3 1.8 fusion.8
  123.2 8.3 %multiply_reduce_fusion.3 = f32[32,128,256]{2,1,0:T(8,128)S(1)} fusion(f32[3,32,128,256]{3,2,1,0:T(8,128)} %get-tuple-element.6, f32[3,128,256]{2,1,0:T(8,128)S(1)} %get-tuple-element.29, f32[3,128,256]{2,1,0:T(8,128)S(1)} %get-tuple-element.30, f32[3,128,256]{2,1,0:T(8,128)S(1)} %get-tuple-element.28, f32[32]{0:T(128)} %copy-done.8, f32[32]{0:T(128)} %copy-done.10, ...), kind=kLoop, calls=%fused_computation.3 | loop fusion | flops 20971520 | bytes 17957248 | tf_op jit(solution)/shard_map/reduce_sum | solution.py:266
  131.5 2.2 fusion.104
  133.7 1.6 pad_maximum_fusion.3
  136.5 1.4 fusion.115
  137.9 1.8 collective-permute-start.16
  140.6 1.4 fusion.117
  142.0 4.8 %collective-permute-start.17 = (f32[2]{0:T(128)S(1)}, f32[2]{0:T(128)S(1)}, u32[]{:S(2)}, u32[]{:S(2)}) collective-permute-start(f32[2]{0:T(128)S(1)} %fusion.117), channel_id=1, source_target_pairs={{0,4},{1,5},{2,6},{3,7},{4,0},{5,1},{6,2},{7,3},{8,12},{9,13},{10,... | collective-permute-start | bytes 32 | tf_op jit(solution)/shard_map/ppermute | solution.py:197
  147.8 1.8 collective-permute-start.18
  150.6 3.4 %collective-permute-start.19 = (f32[2]{0:T(128)S(1)}, f32[2]{0:T(128)S(1)}, u32[]{:S(2)}, u32[]{:S(2)}) collective-permute-start(f32[2]{0:T(128)S(1)} %add.319), channel_id=1, source_target_pairs={{0,16},{1,17},{2,18},{3,19},{4,20},{5,21},{6,22},{7,23},{8,24},{9,... | collective-permute-start | bytes 32 | tf_op jit(solution)/shard_map/ppermute | solution.py:197
  155.0 1.6 collective-permute-start.20
  157.5 2.8 %collective-permute-start.21 = (f32[2]{0:T(128)S(1)}, f32[2]{0:T(128)S(1)}, u32[]{:S(2)}, u32[]{:S(2)}) collective-permute-start(f32[2]{0:T(128)S(1)} %add.321), channel_id=1, source_target_pairs={{0,64},{32,96},{64,0},{96,32},{1,65},{33,97},{65,1},{97,33},{2,66}... | collective-permute-start | bytes 32 | tf_op jit(solution)/shard_map/ppermute | solution.py:197
  164.8 1.8 multiply_reduce_fusion.7
  167.0 3.7 %multiply_reduce_fusion.2 = (f32[3,128,256]{2,1,0:T(8,128)S(1)}, f32[3,128,256]{2,1,0:T(8,128)S(1)}, f32[3,128,256]{2,1,0:T(8,128)S(1)}) fusion(f32[3,32,128,256]{3,2,1,0:T(8,128)S(1)} %bitcast.114, f32[32,128,256]{2,1,0:T(8,128)S(1)} %get-tuple-element.22, f32[32]{0:T(128)S(1)} %copy-done.13, f32[32]{0:T(128)S(1)} %copy-done.11, f32[32]{0:T(128)S(1)} %copy-done.9), kind=kLoop, calls=%fused_computation.2 | loop fusion | flops 21725184 | bytes 17957248 | tf_op jit(solution)/shard_map/reduce_sum | solution.py:176
  172.6 45.3 %all_gather.3 = f32[128,2,689]{2,1,0:T(2,128)S(1)} all-gather(f32[1,2,689]{2,1,0:T(2,128)S(1)} %all_gather_reshape.3), channel_id=1, replica_groups=mesh['grp'=4,'dev'=32] {'grp','dev'}, dimensions={0}, use_global_device_ids=true | all-gather | bytes 711048 | tf_op jit(solution)/shard_map/all_gather | solution.py:286
  219.5 2.8 %reshape.189 = f32[4,32,3,3,9,17]{1,0,5,4,3,2:T(4,128)} reshape(f32[128,1377]{0,1:T(8,128)S(1)} %copy.59) | data formatting | bytes 1410048 | tf_op jit(solution)/shard_map/reshape | solution.py:287
  223.0 4.1 %fusion.5 = f32[4,3,65,9,17]{2,4,0,3,1:T(8,128)S(1)} fusion(f32[4,32,3,3,9,17]{1,0,5,4,3,2:T(4,128)} %reshape.189, s32[32,3]{0,1:T(4,128)S(1)} %copy-done.7), kind=kOutput, calls=%fused_computation.17 | convolution fusion | flops 137485920 | bytes 1182768 | tf_op jit(solution)/shard_map/pqcijk,qix->pcxjk/dot_general | solution.py:223
  227.1 3.4 %fusion.10 = f32[3,65,9,65]{3,1,2,0:T(8,128)} fusion(f32[3,65,9,65]{3,1,2,0:T(8,128)S(1)} %copy-done.6, f32[3,65,9,65]{3,1,2,0:T(8,128)} %param.9, f32[4,3,65,9,17]{2,4,0,3,1:T(8,128)S(1)} %fusion.5, s32[4,17]{1,0:T(4,128)S(1)} %copy-done.14), kind=kOutput, calls=%fused_computation.23 | convolution fusion | flops 93317768 | bytes 1846532 | tf_op jit(solution)/shard_map/pcxjk,pkz->cxjz/dot_general | solution.py:224
  (128 shorter events, 32.7 us)
Async XLA Ops:
  0.6 14.6 %copy-start = (bf16[32,128,256]{2,1,0:T(8,128)(2,1)S(1)}, bf16[32,128,256]{2,1,0:T(8,128)(2,1)}, u32[]{:S(2)}) copy-start(bf16[32,128,256]{2,1,0:T(8,128)(2,1)} %param.5) | copy-start | bytes 6291460
  3.1 13.8 %collective-permute-start = (bf16[9,128,256]{2,1,0:T(8,128)(2,1)}, bf16[9,128,256]{2,1,0:T(8,128)(2,1)S(1)}, u32[]{:S(2)}, u32[]{:S(2)}) collective-permute-start(bf16[9,128,256]{2,1,0:T(8,128)(2,1)} %get-tuple-element.27), channel_id=1, source_target_pairs={{0,1},{1,2},{2,3},{3,4},{4,5},{5,6},{6,7},{7,8},{8,9},{9,10},{10,1... | collective-permute-start | bytes 1769480 | tf_op jit(solution)/shard_map/ppermute | solution.py:23
  7.6 11.4 %collective-permute-start.1 = (bf16[9,128,256]{2,1,0:T(8,128)(2,1)}, bf16[9,128,256]{2,1,0:T(8,128)(2,1)S(1)}, u32[]{:S(2)}, u32[]{:S(2)}) collective-permute-start(bf16[9,128,256]{2,1,0:T(8,128)(2,1)} %get-tuple-element.26), channel_id=1, source_target_pairs={{1,0},{2,1},{3,2},{4,3},{5,4},{6,5},{7,6},{8,7},{9,8},{10,9},{11,1... | collective-permute-start | bytes 1769480 | tf_op jit(solution)/shard_map/ppermute | solution.py:24
  10.7 6.3 %copy-start.5 = (bf16[32,128,256]{2,1,0:T(8,128)(2,1)S(1)}, bf16[32,128,256]{2,1,0:T(8,128)(2,1)}, u32[]{:S(2)}) copy-start(bf16[32,128,256]{2,1,0:T(8,128)(2,1)} %param.6) | copy-start | bytes 6291460
  15.2 71.3 %copy-start.8 = (f32[32]{0:T(128)}, f32[32]{0:T(128)S(1)}, u32[]{:S(2)}) copy-start(f32[32]{0:T(128)S(1)} %get-tuple-element.36) | copy-start | bytes 388
  15.2 71.3 %copy-start.10 = (f32[32]{0:T(128)}, f32[32]{0:T(128)S(1)}, u32[]{:S(2)}) copy-start(f32[32]{0:T(128)S(1)} %get-tuple-element.37) | copy-start | bytes 388
  15.2 71.3 %copy-start.12 = (f32[32]{0:T(128)}, f32[32]{0:T(128)S(1)}, u32[]{:S(2)}) copy-start(f32[32]{0:T(128)S(1)} %get-tuple-element.38) | copy-start | bytes 388
  19.1 1.7 copy-start.3
  25.4 7.8 %collective-permute-start.2 = (bf16[50,128,1]{1,0,2:T(8,128)(2,1)S(1)}, bf16[50,128,1]{1,0,2:T(8,128)(2,1)S(1)}, u32[]{:S(2)}, u32[]{:S(2)}) collective-permute-start(bf16[50,128,1]{1,0,2:T(8,128)(2,1)S(1)} %copy.34), channel_id=1, source_target_pairs={{0,32},{32,64},{64,96},{1,33},{33,65},{65,97},{2,34},{34,66},{66,9... | collective-permute-start | bytes 38408 | tf_op jit(solution)/shard_map/ppermute | solution.py:239
  30.6 4.5 %collective-permute-start.3 = (bf16[50,128,1]{1,0,2:T(8,128)(2,1)S(1)}, bf16[50,128,1]{1,0,2:T(8,128)(2,1)S(1)}, u32[]{:S(2)}, u32[]{:S(2)}) collective-permute-start(bf16[50,128,1]{1,0,2:T(8,128)(2,1)S(1)} %copy.35), channel_id=1, source_target_pairs={{32,0},{64,32},{96,64},{33,1},{65,33},{97,65},{34,2},{66,34},{98,6... | collective-permute-start | bytes 38408 | tf_op jit(solution)/shard_map/ppermute | solution.py:240
  53.8 1.2 collective-permute-start.4
  56.2 2.4 %collective-permute-start.5 = (f32[4]{0:T(128)S(1)}, f32[4]{0:T(128)S(1)}, u32[]{:S(2)}, u32[]{:S(2)}) collective-permute-start(f32[4]{0:T(128)S(1)} %fusion.116), channel_id=1, source_target_pairs={{0,2},{1,3},{2,0},{3,1},{4,6},{5,7},{6,4},{7,5},{8,10},{9,11},{10,... | collective-permute-start | bytes 56 | tf_op jit(solution)/shard_map/ppermute | solution.py:197
  58.7 5.6 %collective-permute-start.6 = (f32[4]{0:T(128)S(1)}, f32[4]{0:T(128)S(1)}, u32[]{:S(2)}, u32[]{:S(2)}) collective-permute-start(f32[4]{0:T(128)S(1)} %add.295), channel_id=1, source_target_pairs={{0,4},{1,5},{2,6},{3,7},{4,0},{5,1},{6,2},{7,3},{8,12},{9,13},{10,... | collective-permute-start | bytes 56 | tf_op jit(solution)/shard_map/ppermute | solution.py:197
  64.3 3.0 %collective-permute-start.7 = (f32[4]{0:T(128)S(1)}, f32[4]{0:T(128)S(1)}, u32[]{:S(2)}, u32[]{:S(2)}) collective-permute-start(f32[4]{0:T(128)S(1)} %add.296), channel_id=1, source_target_pairs={{0,8},{1,9},{2,10},{3,11},{4,12},{5,13},{6,14},{7,15},{8,0},{9,1},... | collective-permute-start | bytes 56 | tf_op jit(solution)/shard_map/ppermute | solution.py:197
  67.2 4.4 %collective-permute-start.8 = (f32[4]{0:T(128)S(1)}, f32[4]{0:T(128)S(1)}, u32[]{:S(2)}, u32[]{:S(2)}) collective-permute-start(f32[4]{0:T(128)S(1)} %add.297), channel_id=1, source_target_pairs={{0,16},{1,17},{2,18},{3,19},{4,20},{5,21},{6,22},{7,23},{8,24},{9,... | collective-permute-start | bytes 56 | tf_op jit(solution)/shard_map/ppermute | solution.py:197
  71.6 2.4 %collective-permute-start.9 = (f32[4]{0:T(128)S(1)}, f32[4]{0:T(128)S(1)}, u32[]{:S(2)}, u32[]{:S(2)}) collective-permute-start(f32[4]{0:T(128)S(1)} %add.298), channel_id=1, source_target_pairs={{0,32},{32,0},{64,96},{96,64},{1,33},{33,1},{65,97},{97,65},{2,34}... | collective-permute-start | bytes 56 | tf_op jit(solution)/shard_map/ppermute | solution.py:197
  74.0 3.9 %collective-permute-start.10 = (f32[4]{0:T(128)S(1)}, f32[4]{0:T(128)S(1)}, u32[]{:S(2)}, u32[]{:S(2)}) collective-permute-start(f32[4]{0:T(128)S(1)} %add.299), channel_id=1, source_target_pairs={{0,64},{32,96},{64,0},{96,32},{1,65},{33,97},{65,1},{97,33},{2,66}... | collective-permute-start | bytes 56 | tf_op jit(solution)/shard_map/ppermute | solution.py:197
  86.5 6.9 %copy-start.16 = (s32[128]{0:T(128)S(1)}, s32[128]{0:T(128)}, u32[]{:S(2)}) copy-start(s32[128]{0:T(128)} %get-tuple-element.47) | copy-start | bytes 1540
  86.5 6.9 %copy-start.18 = (s32[128]{0:T(128)S(1)}, s32[128]{0:T(128)}, u32[]{:S(2)}) copy-start(s32[128]{0:T(128)} %get-tuple-element.48) | copy-start | bytes 1540
  86.5 6.9 %copy-start.20 = (f32[128]{0:T(128)S(1)}, f32[128]{0:T(128)}, u32[]{:S(2)}) copy-start(f32[128]{0:T(128)} %get-tuple-element.51) | copy-start | bytes 1540
  86.5 6.9 %copy-start.22 = (f32[128]{0:T(128)S(1)}, f32[128]{0:T(128)}, u32[]{:S(2)}) copy-start(f32[128]{0:T(128)} %get-tuple-element.52) | copy-start | bytes 1540
  93.4 27.8 %copy-start.4 = (f32[3,3,128,256]{3,2,1,0:T(8,128)S(1)}, f32[3,3,128,256]{3,2,1,0:T(8,128)}, u32[]{:S(2)}) copy-start(f32[3,3,128,256]{3,2,1,0:T(8,128)} %convolution_bitcast_fusion.1.q_ref) | copy-start | bytes 3538948
  94.4 10.7 %collective-permute-start.11 = (f32[3,9,17]{2,1,0:T(8,128)S(1)}, f32[3,9,17]{2,1,0:T(8,128)S(1)}, u32[]{:S(2)}, u32[]{:S(2)}) collective-permute-start(f32[3,9,17]{2,1,0:T(8,128)S(1)} %get-tuple-element.33), channel_id=1, source_target_pairs={{0,1},{1,2},{2,3},{3,4},{4,5},{5,6},{6,7},{7,8},{8,9},{9,10},{10,1... | collective-permute-start | bytes 5516 | tf_op jit(solution)/shard_map/ppermute | solution.py:209
  103.2 5.1 %collective-permute-start.12 = (f32[3,9,17]{2,1,0:T(8,128)S(1)}, f32[3,9,17]{2,1,0:T(8,128)S(1)}, u32[]{:S(2)}, u32[]{:S(2)}) collective-permute-start(f32[3,9,17]{2,1,0:T(8,128)S(1)} %get-tuple-element.34), channel_id=1, source_target_pairs={{1,0},{2,1},{3,2},{4,3},{5,4},{6,5},{7,6},{8,7},{9,8},{10,9},{11,1... | collective-permute-start | bytes 5516 | tf_op jit(solution)/shard_map/ppermute | solution.py:210
  109.1 6.4 %collective-permute-start.13 = (f32[3,3,9]{2,1,0:T(4,128)S(1)}, f32[3,3,9]{2,1,0:T(4,128)S(1)}, u32[]{:S(2)}, u32[]{:S(2)}) collective-permute-start(f32[3,3,9]{2,1,0:T(4,128)S(1)} %get-tuple-element.19), channel_id=1, source_target_pairs={{0,32},{32,64},{64,96},{1,33},{33,65},{65,97},{2,34},{34,66},{66,9... | collective-permute-start | bytes 980 | tf_op jit(solution)/shard_map/ppermute | solution.py:209
  112.6 4.9 %collective-permute-start.14 = (f32[3,3,9]{2,1,0:T(4,128)}, f32[3,3,9]{2,1,0:T(4,128)}, u32[]{:S(2)}, u32[]{:S(2)}) collective-permute-start(f32[3,3,9]{2,1,0:T(4,128)} %get-tuple-element.20), channel_id=1, source_target_pairs={{32,0},{64,32},{96,64},{33,1},{65,33},{97,65},{34,2},{66,34},{98,6... | collective-permute-start | bytes 980 | tf_op jit(solution)/shard_map/ppermute | solution.py:210
  123.2 8.3 %copy-start.1 = (f32[32,128,256]{2,1,0:T(8,128)S(1)}, f32[32,128,256]{2,1,0:T(8,128)}, u32[]{:S(2)}) copy-start(f32[32,128,256]{2,1,0:T(8,128)} %get-tuple-element.8) | copy-start | bytes 12582916
  131.5 35.1 %slice-start = ((s8[12582912]{0:T(1024)(128)(4,1)}), s8[4194304]{0:T(1024)(128)(4,1)S(1)}, s32[]{:S(2)}) async-start(s8[12582912]{0:T(1024)(128)(4,1)} %bitcast.113), calls=%async_computation | async-start | bytes 8388608
  131.5 35.1 %slice-start.1 = ((s8[12582912]{0:T(1024)(128)(4,1)}), s8[4194304]{0:T(1024)(128)(4,1)S(1)}, s32[]{:S(2)}) async-start(s8[12582912]{0:T(1024)(128)(4,1)} %bitcast.113), calls=%async_computation.1 | async-start | bytes 8388608
  135.3 1.2 collective-permute-start.15
  137.9 2.8 %collective-permute-start.16 = (f32[2]{0:T(128)S(1)}, f32[2]{0:T(128)S(1)}, u32[]{:S(2)}, u32[]{:S(2)}) collective-permute-start(f32[2]{0:T(128)S(1)} %fusion.115), channel_id=1, source_target_pairs={{0,2},{1,3},{2,0},{3,1},{4,6},{5,7},{6,4},{7,5},{8,10},{9,11},{10,... | collective-permute-start | bytes 32 | tf_op jit(solution)/shard_map/ppermute | solution.py:197
  142.0 5.8 %collective-permute-start.17 = (f32[2]{0:T(128)S(1)}, f32[2]{0:T(128)S(1)}, u32[]{:S(2)}, u32[]{:S(2)}) collective-permute-start(f32[2]{0:T(128)S(1)} %fusion.117), channel_id=1, source_target_pairs={{0,4},{1,5},{2,6},{3,7},{4,0},{5,1},{6,2},{7,3},{8,12},{9,13},{10,... | collective-permute-start | bytes 32 | tf_op jit(solution)/shard_map/ppermute | solution.py:197
  147.8 2.8 %collective-permute-start.18 = (f32[2]{0:T(128)S(1)}, f32[2]{0:T(128)S(1)}, u32[]{:S(2)}, u32[]{:S(2)}) collective-permute-start(f32[2]{0:T(128)S(1)} %add.318), channel_id=1, source_target_pairs={{0,8},{1,9},{2,10},{3,11},{4,12},{5,13},{6,14},{7,15},{8,0},{9,1},... | collective-permute-start | bytes 32 | tf_op jit(solution)/shard_map/ppermute | solution.py:197
  150.6 4.4 %collective-permute-start.19 = (f32[2]{0:T(128)S(1)}, f32[2]{0:T(128)S(1)}, u32[]{:S(2)}, u32[]{:S(2)}) collective-permute-start(f32[2]{0:T(128)S(1)} %add.319), channel_id=1, source_target_pairs={{0,16},{1,17},{2,18},{3,19},{4,20},{5,21},{6,22},{7,23},{8,24},{9,... | collective-permute-start | bytes 32 | tf_op jit(solution)/shard_map/ppermute | solution.py:197
  155.0 2.5 %collective-permute-start.20 = (f32[2]{0:T(128)S(1)}, f32[2]{0:T(128)S(1)}, u32[]{:S(2)}, u32[]{:S(2)}) collective-permute-start(f32[2]{0:T(128)S(1)} %add.320), channel_id=1, source_target_pairs={{0,32},{32,0},{64,96},{96,64},{1,33},{33,1},{65,97},{97,65},{2,34}... | collective-permute-start | bytes 32 | tf_op jit(solution)/shard_map/ppermute | solution.py:197
  157.5 3.9 %collective-permute-start.21 = (f32[2]{0:T(128)S(1)}, f32[2]{0:T(128)S(1)}, u32[]{:S(2)}, u32[]{:S(2)}) collective-permute-start(f32[2]{0:T(128)S(1)} %add.321), channel_id=1, source_target_pairs={{0,64},{32,96},{64,0},{96,32},{1,65},{33,97},{65,1},{97,33},{2,66}... | collective-permute-start | bytes 32 | tf_op jit(solution)/shard_map/ppermute | solution.py:197
  164.7 2.2 slice-start.2
  164.7 2.2 copy-start.9
  164.7 2.2 copy-start.11
  164.8 2.2 copy-start.13
  166.6 4.1 %copy-start.2 = (f32[32,128,256]{2,1,0:T(8,128)}, f32[32,128,256]{2,1,0:T(8,128)S(1)}, u32[]{:S(2)}) copy-start(f32[32,128,256]{2,1,0:T(8,128)S(1)} %get-tuple-element.22) | copy-start | bytes 12582916
  166.9 3.8 %copy-start.17 = (s32[128]{0:T(128)S(1)}, s32[128]{0:T(128)}, u32[]{:S(2)}) copy-start(s32[128]{0:T(128)} %get-tuple-element.47) | copy-start | bytes 1540
  166.9 3.8 %copy-start.19 = (s32[128]{0:T(128)S(1)}, s32[128]{0:T(128)}, u32[]{:S(2)}) copy-start(s32[128]{0:T(128)} %get-tuple-element.48) | copy-start | bytes 1540
  166.9 3.8 %copy-start.21 = (f32[128]{0:T(128)S(1)}, f32[128]{0:T(128)}, u32[]{:S(2)}) copy-start(f32[128]{0:T(128)} %get-tuple-element.51) | copy-start | bytes 1540
  167.0 3.8 %copy-start.23 = (f32[128]{0:T(128)S(1)}, f32[128]{0:T(128)}, u32[]{:S(2)}) copy-start(f32[128]{0:T(128)} %get-tuple-element.52) | copy-start | bytes 1540
  171.4 51.6 %copy-start.7 = (s32[32,3]{0,1:T(4,128)S(1)}, s32[32,3]{0,1:T(4,128)}, u32[]{:S(2)}) copy-start(s32[32,3]{0,1:T(4,128)} %iota_add_fusion.1) | copy-start | bytes 1156
  219.5 7.6 %copy-start.6 = (f32[3,65,9,65]{3,1,2,0:T(8,128)S(1)}, f32[3,65,9,65]{3,1,2,0:T(8,128)}, u32[]{:S(2)}) copy-start(f32[3,65,9,65]{3,1,2,0:T(8,128)} %param.8) | copy-start | bytes 1368904
  219.5 7.6 %copy-start.14 = (s32[4,17]{1,0:T(4,128)S(1)}, s32[4,17]{1,0:T(4,128)}, u32[]{:S(2)}) copy-start(s32[4,17]{1,0:T(4,128)} %iota_add_fusion) | copy-start | bytes 820
  (1 other events, 0.6 us)

commit v7 on v3

--- a/solution.py
+++ b/solution.py
@@ -32,7 +32,7 @@
 PLANES = 8
 
 
-def _native_kernel(offset_ref, w_ref, lo_ref, hi_ref, sl_ref, sm_ref, keep_ref):
+def _native_kernel(offset_ref, w_ref, lo_ref, hi_ref, sl_ref, keep_ref):
     step = pl.program_id(0)
     _, wy, wz = w_ref.shape
     row = lax.broadcasted_iota(jnp.int32, (wy, wz), 0)
@@ -71,7 +71,6 @@
         sl_ref[0, k] = 0.5 * (nxt[0] - prev[0])
         sl_ref[1, k] = (prev[1] + 4.0 * mid[1] + nxt[1]) * sixth
         sl_ref[2, k] = (prev[2] + 4.0 * mid[2] + nxt[2]) * sixth
-        sm_ref[k] = mid[3]
     for t in range(2):
         for n, value in enumerate(window[PLANES + t]):
             keep_ref[t, n] = value
@@ -89,7 +88,6 @@
         scratch_shapes=[pltpu.VMEM((2, 4, wy, wz), jnp.float32)],
         out_specs=[
             pl.BlockSpec((3, PLANES, wy, wz), lambda i, o: (0, i, 0, 0)),
-            pl.BlockSpec((PLANES, wy, wz), lambda i, o: (i, 0, 0)),
         ],
     )
     return pl.pallas_call(
@@ -97,7 +95,6 @@
         grid_spec=spec,
         out_shape=[
             jax.ShapeDtypeStruct((3, width_x, wy, wz), jnp.float32),
-            jax.ShapeDtypeStruct((width_x, wy, wz), jnp.float32),
         ],
         interpret=interpret,
     )(offset, widened, below, above)
@@ -218,7 +215,8 @@
     down = [(j, i) for i, j in up]
     below = lax.ppermute(widened[:, :, -1:], "grp", up)
     above = lax.ppermute(widened[:, :, :1], "grp", down)
-    slopes, sample = native_slopes(offset.reshape(1), widened, below, above, width_x)
+    (slopes,) = native_slopes(offset.reshape(1), widened, below, above, width_x)
+    sample = lax.dynamic_slice_in_dim(widened, offset + margin, width_x, 0).astype(jnp.float32)
     target = ref_volume.astype(jnp.float32)
     elements_x = width_x // E
     elements_z = depth_z // E

time: 230 us -> 236 us (1.026)
  waiting for transfers between devices: 26.4 us -> 20.2 us
  local copies, waits for them, and re-layouts: 23.7 us -> 27.2 us
  other arithmetic: 46.7 us -> 49.7 us
  blocking collectives: 42.6 us -> 45.2 us
    ppermute x2, waiting for transfers between devices: 5.96 us -> 3.2 us  [share_nodes(): after = lax.ppermute(first, axis, down)]
    all_gather x1, blocking collectives: 42.6 us -> 45.2 us  [local(): lax.all_gather(packed.reshape(2, -1), ('grp', 'dev'))]
    unnamed x31 -> x67, local copies, waits for them, and re-layouts: 4.88 us -> 3.53 us
  transfers between devices with their start and end apart: 22 -> 22, of which waited for: 19 -> 17; matrix products, arithmetic and copies ran while one was open for 4% -> 6% of each run, Pallas kernels for 0% -> 0%
where the time goes in v7:
time: 236 us; the launch traced here: 235 us
  starting transfers between devices  58.4 us (25%)
  other arithmetic  49.7 us (21%)
  blocking collectives  45.2 us (19%)
  local copies, waits for them, and re-layouts  27.2 us (12%)
  waiting for transfers between devices  20.2 us (9%)
  Pallas kernels  12 us (5%)
  between operations  11.5 us (5%)
  matrix products  10.9 us (5%)
    all_gather x1, blocking collectives, local(): lax.all_gather(packed.reshape(2, -1), ('grp', 'dev'))  45.2 us
    ppermute x14, starting transfers between devices, allsum(): values = values + lax.ppermute(values, axis, pairs)  31.9 us
    reduce_sum x2, other arithmetic, local(): warped = sample + jnp.sum(shift_field * slopes, axis=0)  18.2 us
    ppermute x14, waiting for transfers between devices, allsum(): values = values + lax.ppermute(values, axis, pairs)  14.2 us
    ppermute x2, starting transfers between devices, share_nodes(): before = lax.ppermute(last, axis, up)  12.4 us
    pallas_call x1, Pallas kernels, native_slopes(): pl.pallas_call(_native_kernel, grid_spec=spec, out_shape=[jax.ShapeDtypeS...  12 us
    add x14, other arithmetic, allsum(): values = values + lax.ppermute(values, axis, pairs)  7.98 us
    reduce_sum x2, other arithmetic, restrict(): jnp.sum(terms * hat_x[None, :, i, None, None], axis=1)  7.41 us
  transfers between devices with their start and end apart: 22, of which 17 were waited for; matrix products, arithmetic and copies ran while one was open for 6% of the time, Pallas kernels for 0%

profile of v7, /device:TPU:1, one launch (start us, length us, event | category | flops | bytes accessed | tf_op | source)
XLA Modules:
  0.0 235.1 jit_solution(7396600461547476446)
XLA Ops:
  0.6 2.3 fusion.107
  2.9 4.5 %collective-permute-start = (bf16[9,128,256]{2,1,0:T(8,128)(2,1)S(1)}, bf16[9,128,256]{2,1,0:T(8,128)(2,1)}, u32[]{:S(2)}, u32[]{:S(2)}) collective-permute-start(bf16[9,128,256]{2,1,0:T(8,128)(2,1)S(1)} %get-tuple-element.22), channel_id=1, source_target_pairs={{0,1},{1,2},{2,3},{3,4},{4,5},{5,6},{6,7},{7,8},{8,9},{9,10},{10,1... | collective-permute-start | bytes 1769480 | tf_op jit(solution)/shard_map/ppermute | solution.py:23
  7.4 1.9 collective-permute-start.1
  9.5 1.3 constant_dynamic-slice_fusion
  13.4 1.7 convert_reduce_fusion
  16.4 2.6 %collective-permute-done.1 = bf16[9,128,256]{2,1,0:T(8,128)(2,1)} collective-permute-done((bf16[9,128,256]{2,1,0:T(8,128)(2,1)}, bf16[9,128,256]{2,1,0:T(8,128)(2,1)}, u32[]{:S(2)}, u32[]{:S(2)}) %collective-permute-start.1) | collective-permute-done | bytes 589856 | tf_op jit(solution)/shard_map/ppermute | solution.py:24
  20.1 2.8 %fusion.106 = (bf16[50,128,1]{2,1,0:T(8,128)(2,1)}, bf16[50,128,1]{2,1,0:T(8,128)(2,1)}) fusion(bf16[50,128,256]{2,1,0:T(8,128)(2,1)S(1)} %constant_dynamic-update-slice_fusion.w_ref), kind=kLoop, calls=%fused_computation.182 | loop fusion | bytes 51200 | tf_op jit(solution)/shard_map/slice | solution.py:217
  22.9 2.0 copy.34
  24.9 3.2 %collective-permute-start.2 = (bf16[50,128,1]{1,0,2:T(8,128)(2,1)S(1)}, bf16[50,128,1]{1,0,2:T(8,128)(2,1)S(1)}, u32[]{:S(2)}, u32[]{:S(2)}) collective-permute-start(bf16[50,128,1]{1,0,2:T(8,128)(2,1)S(1)} %copy.34), channel_id=1, source_target_pairs={{0,32},{32,64},{64,96},{1,33},{33,65},{65,97},{2,34},{34,66},{66,9... | collective-permute-start | bytes 38408 | tf_op jit(solution)/shard_map/ppermute | solution.py:216
  28.1 2.0 copy.35
  30.1 1.3 collective-permute-start.3
  32.7 1.7 copy.36.lo_ref
  34.6 1.7 copy.37.hi_ref
  36.2 12.0 %shard_map.76 = f32[3,32,128,256]{3,2,1,0:T(8,128)} custom-call(s32[1]{0:T(128)} %bitcast.120.offset_ref, bf16[50,128,256]{2,1,0:T(8,128)(2,1)} %copy-done, bf16[50,128,1]{2,1,0:T(8,128)(2,1)} %copy.36.lo_ref, bf16[50,128,1]{2,1,0:T(8,128)(2,1)} %copy.37.hi_ref), custom_call_target="tpu_custom_call" | custom-call | tf_op jit(solution)/shard_map/pallas_call | solution.py:93
  48.2 9.2 %multiply_reduce_fusion.7 = f32[32,128,256]{2,1,0:T(8,128)S(1)} fusion(f32[3,32,128,256]{3,2,1,0:T(8,128)} %shard_map.76, f32[3,128,256]{2,1,0:T(8,128)} %get-tuple-element.27, f32[32]{0:T(128)S(1)} %get-tuple-element.35, f32[3,128,256]{2,1,0:T(8,128)} %get-tuple-element.28, f32[32]{0:T(128)S(1)} %get-tuple-element.36, f32[3,128,256]{2,1,0:T(8,128)} %get-tuple-element.26, ...), kind=kLoop, calls=%fused_computation.7 | loop fusion | flops 20971520 | bytes 17957248 | tf_op jit(solution)/shard_map/reduce_sum | solution.py:237
  57.4 1.8 fusion.28
  59.3 2.6 %pad_maximum_fusion.2 = f32[4]{0:T(128)S(1)} fusion(f32[1]{0:T(128)} %bitcast.20, f32[1]{0:T(128)} %bitcast.19, f32[1]{0:T(128)} %bitcast.6, f32[1]{0:T(128)} %bitcast.5), kind=kLoop, calls=%fused_computation.156 | loop fusion | flops 12 | bytes 32 | tf_op jit(solution)/shard_map/concatenate | solution.py:240
  63.1 2.6 %fusion.116 = f32[4]{0:T(128)S(1)} fusion(f32[4]{0:T(128)S(1)} %collective-permute-done.4, f32[1]{0:T(128)} %bitcast.20, f32[1]{0:T(128)} %bitcast.19, f32[1]{0:T(128)} %bitcast.6, f32[1]{0:T(128)} %bitcast.5), kind=kLoop, calls=%fused_computation.187 | loop fusion | flops 16 | bytes 48 | tf_op jit(solution)/shard_map/add | solution.py:174
  68.1 2.6 %fusion.118 = f32[4]{0:T(128)S(1)} fusion(f32[4]{0:T(128)S(1)} %collective-permute-done.5, f32[4]{0:T(128)S(1)} %collective-permute-done.4, f32[1]{0:T(128)} %bitcast.20, f32[1]{0:T(128)} %bitcast.19, f32[1]{0:T(128)} %bitcast.6, f32[1]{0:T(128)} %bitcast.5), kind=kLoop, calls=%fused_computation.189 | loop fusion | flops 20 | bytes 64 | tf_op jit(solution)/shard_map/add | solution.py:174
  70.7 4.7 %collective-permute-start.6 = (f32[4]{0:T(128)S(1)}, f32[4]{0:T(128)S(1)}, u32[]{:S(2)}, u32[]{:S(2)}) collective-permute-start(f32[4]{0:T(128)S(1)} %fusion.118), channel_id=1, source_target_pairs={{0,4},{1,5},{2,6},{3,7},{4,0},{5,1},{6,2},{7,3},{8,12},{9,13},{10,... | collective-permute-start | bytes 56 | tf_op jit(solution)/shard_map/ppermute | solution.py:174
  76.4 1.9 collective-permute-start.7
  79.2 3.4 %collective-permute-start.8 = (f32[4]{0:T(128)S(1)}, f32[4]{0:T(128)S(1)}, u32[]{:S(2)}, u32[]{:S(2)}) collective-permute-start(f32[4]{0:T(128)S(1)} %add.348), channel_id=1, source_target_pairs={{0,16},{1,17},{2,18},{3,19},{4,20},{5,21},{6,22},{7,23},{8,24},{9,... | collective-permute-start | bytes 56 | tf_op jit(solution)/shard_map/ppermute | solution.py:174
  83.6 1.4 collective-permute-start.9
  86.0 3.0 %collective-permute-start.10 = (f32[4]{0:T(128)S(1)}, f32[4]{0:T(128)S(1)}, u32[]{:S(2)}, u32[]{:S(2)}) collective-permute-start(f32[4]{0:T(128)S(1)} %add.350), channel_id=1, source_target_pairs={{0,64},{32,96},{64,0},{96,32},{1,65},{33,97},{65,1},{97,33},{2,66}... | collective-permute-start | bytes 56 | tf_op jit(solution)/shard_map/ppermute | solution.py:174
  97.8 3.7 %multiply_reduce_fusion.6 = (f32[3,128,256]{2,1,0:T(8,128)S(1)}, f32[3,128,256]{2,1,0:T(8,128)S(1)}, f32[3,128,256]{2,1,0:T(8,128)S(1)}) fusion(f32[3,32,128,256]{3,2,1,0:T(8,128)S(1)} %bitcast.122, f32[32,128,256]{2,1,0:T(8,128)S(1)} %fusion.1, f32[32]{0:T(128)S(1)} %get-tuple-element.34, f32[32]{0:T(128)S(1)} %get-tuple-element.36, f32[32]{0:T(128)S(1)} %get-tuple-element.35), kind=kLoop, calls=%fused_computation.6 | loop fusion | flops 21725184 | bytes 17957248 | tf_op jit(solution)/shard_map/reduce_sum | solution.py:153
  102.5 8.9 %collective-permute-start.11 = (f32[3,9,17]{2,1,0:T(8,128)S(1)}, f32[3,9,17]{2,1,0:T(8,128)S(1)}, u32[]{:S(2)}, u32[]{:S(2)}) collective-permute-start(f32[3,9,17]{2,1,0:T(8,128)S(1)} %get-tuple-element.31), channel_id=1, source_target_pairs={{0,1},{1,2},{2,3},{3,4},{4,5},{5,6},{6,7},{7,8},{8,9},{9,10},{10,1... | collective-permute-start | bytes 5516 | tf_op jit(solution)/shard_map/ppermute | solution.py:186
  111.4 1.9 collective-permute-start.12
  113.3 3.2 %collective-permute-done.12 = f32[3,9,17]{2,1,0:T(8,128)S(1)} collective-permute-done((f32[3,9,17]{2,1,0:T(8,128)S(1)}, f32[3,9,17]{2,1,0:T(8,128)S(1)}, u32[]{:S(2)}, u32[]{:S(2)}) %collective-permute-start.12) | collective-permute-done | bytes 1868 | tf_op jit(solution)/shard_map/ppermute | solution.py:187
  117.3 3.5 %collective-permute-start.13 = (f32[3,3,9]{2,1,0:T(4,128)S(1)}, f32[3,3,9]{2,1,0:T(4,128)S(1)}, u32[]{:S(2)}, u32[]{:S(2)}) collective-permute-start(f32[3,3,9]{2,1,0:T(4,128)S(1)} %get-tuple-element.15), channel_id=1, source_target_pairs={{0,32},{32,64},{64,96},{1,33},{33,65},{65,97},{2,34},{34,66},{66,9... | collective-permute-start | bytes 980 | tf_op jit(solution)/shard_map/ppermute | solution.py:186
  124.1 1.5 copy.44
  125.5 1.5 copy.45
  129.2 1.8 convolution_bitcast_fusion
  131.2 9.0 %multiply_reduce_fusion.3 = f32[32,128,256]{2,1,0:T(8,128)S(1)} fusion(f32[3,32,128,256]{3,2,1,0:T(8,128)} %shard_map.76, f32[3,128,256]{2,1,0:T(8,128)S(1)} %get-tuple-element.24, f32[3,128,256]{2,1,0:T(8,128)S(1)} %get-tuple-element.25, f32[3,128,256]{2,1,0:T(8,128)S(1)} %get-tuple-element.23, f32[32]{0:T(128)S(1)} %copy-done.12, f32[32]{0:T(128)S(1)} %copy-done.14, ...), kind=kLoop, calls=%fused_computation.3 | loop fusion | flops 20971520 | bytes 17957248 | tf_op jit(solution)/shard_map/reduce_sum | solution.py:237
  140.3 1.8 fusion.29
  142.1 1.4 pad_maximum_fusion.3
  144.7 1.4 fusion.115
  146.0 1.8 collective-permute-start.16
  148.8 1.4 fusion.117
  150.2 4.7 %collective-permute-start.17 = (f32[2]{0:T(128)S(1)}, f32[2]{0:T(128)S(1)}, u32[]{:S(2)}, u32[]{:S(2)}) collective-permute-start(f32[2]{0:T(128)S(1)} %fusion.117), channel_id=1, source_target_pairs={{0,4},{1,5},{2,6},{3,7},{4,0},{5,1},{6,2},{7,3},{8,12},{9,13},{10,... | collective-permute-start | bytes 32 | tf_op jit(solution)/shard_map/ppermute | solution.py:174
  155.9 2.0 collective-permute-start.18
  158.8 3.4 %collective-permute-start.19 = (f32[2]{0:T(128)S(1)}, f32[2]{0:T(128)S(1)}, u32[]{:S(2)}, u32[]{:S(2)}) collective-permute-start(f32[2]{0:T(128)S(1)} %add.367), channel_id=1, source_target_pairs={{0,16},{1,17},{2,18},{3,19},{4,20},{5,21},{6,22},{7,23},{8,24},{9,... | collective-permute-start | bytes 32 | tf_op jit(solution)/shard_map/ppermute | solution.py:174
  163.2 1.4 collective-permute-start.20
  165.7 2.9 %collective-permute-start.21 = (f32[2]{0:T(128)S(1)}, f32[2]{0:T(128)S(1)}, u32[]{:S(2)}, u32[]{:S(2)}) collective-permute-start(f32[2]{0:T(128)S(1)} %add.369), channel_id=1, source_target_pairs={{0,64},{32,96},{64,0},{96,32},{1,65},{33,97},{65,1},{97,33},{2,66}... | collective-permute-start | bytes 32 | tf_op jit(solution)/shard_map/ppermute | solution.py:174
  172.9 1.9 multiply_reduce_fusion.8
  175.1 3.7 %multiply_reduce_fusion.2 = (f32[3,128,256]{2,1,0:T(8,128)S(1)}, f32[3,128,256]{2,1,0:T(8,128)S(1)}, f32[3,128,256]{2,1,0:T(8,128)S(1)}) fusion(f32[3,32,128,256]{3,2,1,0:T(8,128)S(1)} %bitcast.124, f32[32,128,256]{2,1,0:T(8,128)S(1)} %get-tuple-element.18, f32[32]{0:T(128)S(1)} %copy-done.10, f32[32]{0:T(128)S(1)} %copy-done.14, f32[32]{0:T(128)S(1)} %copy-done.12), kind=kLoop, calls=%fused_computation.2 | loop fusion | flops 21725184 | bytes 17957248 | tf_op jit(solution)/shard_map/reduce_sum | solution.py:153
  180.6 45.2 %all_gather.3 = f32[128,2,689]{2,1,0:T(2,128)S(1)} all-gather(f32[1,2,689]{2,1,0:T(2,128)S(1)} %all_gather_reshape.3), channel_id=1, replica_groups=mesh['grp'=4,'dev'=32] {'grp','dev'}, dimensions={0}, use_global_device_ids=true | all-gather | bytes 711048 | tf_op jit(solution)/shard_map/all_gather | solution.py:256
  229.4 2.4 %fusion.5 = f32[4,3,65,9,17]{2,4,0,3,1:T(8,128)S(1)} fusion(f32[4,32,3,3,9,17]{1,0,5,4,3,2:T(4,128)S(1)} %reshape.193, s32[32,3]{0,1:T(4,128)S(1)} %copy-done.15), kind=kOutput, calls=%fused_computation.21 | convolution fusion | flops 137485920 | bytes 1182768 | tf_op jit(solution)/shard_map/pqcijk,qix->pcxjk/dot_general | solution.py:200
  231.8 2.2 fusion.9
  (141 shorter events, 36.8 us)
Async XLA Ops:
  0.6 12.7 %copy-start.2 = (bf16[32,128,256]{2,1,0:T(8,128)(2,1)S(1)}, bf16[32,128,256]{2,1,0:T(8,128)(2,1)}, u32[]{:S(2)}) copy-start(bf16[32,128,256]{2,1,0:T(8,128)(2,1)} %param.5) | copy-start | bytes 6291460
  2.9 12.2 %collective-permute-start = (bf16[9,128,256]{2,1,0:T(8,128)(2,1)S(1)}, bf16[9,128,256]{2,1,0:T(8,128)(2,1)}, u32[]{:S(2)}, u32[]{:S(2)}) collective-permute-start(bf16[9,128,256]{2,1,0:T(8,128)(2,1)S(1)} %get-tuple-element.22), channel_id=1, source_target_pairs={{0,1},{1,2},{2,3},{3,4},{4,5},{5,6},{6,7},{7,8},{8,9},{9,10},{10,1... | collective-permute-start | bytes 1769480 | tf_op jit(solution)/shard_map/ppermute | solution.py:23
  7.4 11.5 %collective-permute-start.1 = (bf16[9,128,256]{2,1,0:T(8,128)(2,1)}, bf16[9,128,256]{2,1,0:T(8,128)(2,1)}, u32[]{:S(2)}, u32[]{:S(2)}) collective-permute-start(bf16[9,128,256]{2,1,0:T(8,128)(2,1)} %get-tuple-element.21), channel_id=1, source_target_pairs={{1,0},{2,1},{3,2},{4,3},{5,4},{6,5},{7,6},{8,7},{9,8},{10,9},{11,1... | collective-permute-start | bytes 1769480 | tf_op jit(solution)/shard_map/ppermute | solution.py:24
  9.4 92.1 %copy-start.18 = (s32[128]{0:T(128)}, s32[128]{0:T(128)S(1)}, u32[]{:S(2)}) copy-start(s32[128]{0:T(128)S(1)} %get-tuple-element.47) | copy-start | bytes 1540
  9.4 92.1 %copy-start.20 = (s32[128]{0:T(128)}, s32[128]{0:T(128)S(1)}, u32[]{:S(2)}) copy-start(s32[128]{0:T(128)S(1)} %get-tuple-element.48) | copy-start | bytes 1540
  9.4 92.1 %copy-start.22 = (f32[128]{0:T(128)}, f32[128]{0:T(128)S(1)}, u32[]{:S(2)}) copy-start(f32[128]{0:T(128)S(1)} %get-tuple-element.53) | copy-start | bytes 1540
  9.5 92.1 %copy-start.24 = (f32[128]{0:T(128)}, f32[128]{0:T(128)S(1)}, u32[]{:S(2)}) copy-start(f32[128]{0:T(128)S(1)} %get-tuple-element.54) | copy-start | bytes 1540
  9.5 6.7 %copy-start.6 = (bf16[32,128,256]{2,1,0:T(8,128)(2,1)S(1)}, bf16[32,128,256]{2,1,0:T(8,128)(2,1)}, u32[]{:S(2)}) copy-start(bf16[32,128,256]{2,1,0:T(8,128)(2,1)} %param.6) | copy-start | bytes 6291460
  13.3 83.4 %copy-start.9 = (f32[32]{0:T(128)}, f32[32]{0:T(128)S(1)}, u32[]{:S(2)}) copy-start(f32[32]{0:T(128)S(1)} %get-tuple-element.34) | copy-start | bytes 388
  13.3 83.4 %copy-start.11 = (f32[32]{0:T(128)}, f32[32]{0:T(128)S(1)}, u32[]{:S(2)}) copy-start(f32[32]{0:T(128)S(1)} %get-tuple-element.35) | copy-start | bytes 388
  13.3 83.4 %copy-start.13 = (f32[32]{0:T(128)}, f32[32]{0:T(128)S(1)}, u32[]{:S(2)}) copy-start(f32[32]{0:T(128)S(1)} %get-tuple-element.36) | copy-start | bytes 388
  20.1 10.0 %copy-start = (bf16[50,128,256]{2,1,0:T(8,128)(2,1)}, bf16[50,128,256]{2,1,0:T(8,128)(2,1)S(1)}, u32[]{:S(2)}) copy-start(bf16[50,128,256]{2,1,0:T(8,128)(2,1)S(1)} %constant_dynamic-update-slice_fusion.w_ref) | copy-start | bytes 9830404
  24.9 7.8 %collective-permute-start.2 = (bf16[50,128,1]{1,0,2:T(8,128)(2,1)S(1)}, bf16[50,128,1]{1,0,2:T(8,128)(2,1)S(1)}, u32[]{:S(2)}, u32[]{:S(2)}) collective-permute-start(bf16[50,128,1]{1,0,2:T(8,128)(2,1)S(1)} %copy.34), channel_id=1, source_target_pairs={{0,32},{32,64},{64,96},{1,33},{33,65},{65,97},{2,34},{34,66},{66,9... | collective-permute-start | bytes 38408 | tf_op jit(solution)/shard_map/ppermute | solution.py:216
  30.1 4.5 %collective-permute-start.3 = (bf16[50,128,1]{1,0,2:T(8,128)(2,1)S(1)}, bf16[50,128,1]{1,0,2:T(8,128)(2,1)S(1)}, u32[]{:S(2)}, u32[]{:S(2)}) collective-permute-start(bf16[50,128,1]{1,0,2:T(8,128)(2,1)S(1)} %copy.35), channel_id=1, source_target_pairs={{32,0},{64,32},{96,64},{33,1},{65,33},{97,65},{34,2},{66,34},{98,6... | collective-permute-start | bytes 38408 | tf_op jit(solution)/shard_map/ppermute | solution.py:217
  48.2 9.2 %copy-start.1 = (bf16[50,128,256]{2,1,0:T(8,128)(2,1)S(1)}, bf16[50,128,256]{2,1,0:T(8,128)(2,1)}, u32[]{:S(2)}) copy-start(bf16[50,128,256]{2,1,0:T(8,128)(2,1)} %copy-done) | copy-start | bytes 9830404
  48.2 48.5 %slice-start = ((s8[12582912]{0:T(1024)(128)(4,1)}), s8[4194304]{0:T(1024)(128)(4,1)S(1)}, s32[]{:S(2)}) async-start(s8[12582912]{0:T(1024)(128)(4,1)} %bitcast.121), calls=%async_computation | async-start | bytes 8388608
  48.2 48.6 %slice-start.1 = ((s8[12582912]{0:T(1024)(128)(4,1)}), s8[4194304]{0:T(1024)(128)(4,1)S(1)}, s32[]{:S(2)}) async-start(s8[12582912]{0:T(1024)(128)(4,1)} %bitcast.121), calls=%async_computation.1 | async-start | bytes 8388608
  57.4 38.2 %copy-start.3 = (bf16[32,128,256]{2,1,0:T(8,128)(2,1)S(1)}, bf16[32,128,256]{2,1,0:T(8,128)(2,1)}, u32[]{:S(2)}) copy-start(bf16[32,128,256]{2,1,0:T(8,128)(2,1)} %param.5) | copy-start | bytes 6291460
  61.9 1.2 collective-permute-start.4
  65.7 2.4 %collective-permute-start.5 = (f32[4]{0:T(128)S(1)}, f32[4]{0:T(128)S(1)}, u32[]{:S(2)}, u32[]{:S(2)}) collective-permute-start(f32[4]{0:T(128)S(1)} %fusion.116), channel_id=1, source_target_pairs={{0,2},{1,3},{2,0},{3,1},{4,6},{5,7},{6,4},{7,5},{8,10},{9,11},{10,... | collective-permute-start | bytes 56 | tf_op jit(solution)/shard_map/ppermute | solution.py:174
  70.7 5.6 %collective-permute-start.6 = (f32[4]{0:T(128)S(1)}, f32[4]{0:T(128)S(1)}, u32[]{:S(2)}, u32[]{:S(2)}) collective-permute-start(f32[4]{0:T(128)S(1)} %fusion.118), channel_id=1, source_target_pairs={{0,4},{1,5},{2,6},{3,7},{4,0},{5,1},{6,2},{7,3},{8,12},{9,13},{10,... | collective-permute-start | bytes 56 | tf_op jit(solution)/shard_map/ppermute | solution.py:174
  76.4 2.8 %collective-permute-start.7 = (f32[4]{0:T(128)S(1)}, f32[4]{0:T(128)S(1)}, u32[]{:S(2)}, u32[]{:S(2)}) collective-permute-start(f32[4]{0:T(128)S(1)} %add.347), channel_id=1, source_target_pairs={{0,8},{1,9},{2,10},{3,11},{4,12},{5,13},{6,14},{7,15},{8,0},{9,1},... | collective-permute-start | bytes 56 | tf_op jit(solution)/shard_map/ppermute | solution.py:174
  79.2 4.4 %collective-permute-start.8 = (f32[4]{0:T(128)S(1)}, f32[4]{0:T(128)S(1)}, u32[]{:S(2)}, u32[]{:S(2)}) collective-permute-start(f32[4]{0:T(128)S(1)} %add.348), channel_id=1, source_target_pairs={{0,16},{1,17},{2,18},{3,19},{4,20},{5,21},{6,22},{7,23},{8,24},{9,... | collective-permute-start | bytes 56 | tf_op jit(solution)/shard_map/ppermute | solution.py:174
  83.6 2.4 %collective-permute-start.9 = (f32[4]{0:T(128)S(1)}, f32[4]{0:T(128)S(1)}, u32[]{:S(2)}, u32[]{:S(2)}) collective-permute-start(f32[4]{0:T(128)S(1)} %add.349), channel_id=1, source_target_pairs={{0,32},{32,0},{64,96},{96,64},{1,33},{33,1},{65,97},{97,65},{2,34}... | collective-permute-start | bytes 56 | tf_op jit(solution)/shard_map/ppermute | solution.py:174
  86.0 4.0 %collective-permute-start.10 = (f32[4]{0:T(128)S(1)}, f32[4]{0:T(128)S(1)}, u32[]{:S(2)}, u32[]{:S(2)}) collective-permute-start(f32[4]{0:T(128)S(1)} %add.350), channel_id=1, source_target_pairs={{0,64},{32,96},{64,0},{96,32},{1,65},{33,97},{65,1},{97,33},{2,66}... | collective-permute-start | bytes 56 | tf_op jit(solution)/shard_map/ppermute | solution.py:174
  102.5 10.8 %collective-permute-start.11 = (f32[3,9,17]{2,1,0:T(8,128)S(1)}, f32[3,9,17]{2,1,0:T(8,128)S(1)}, u32[]{:S(2)}, u32[]{:S(2)}) collective-permute-start(f32[3,9,17]{2,1,0:T(8,128)S(1)} %get-tuple-element.31), channel_id=1, source_target_pairs={{0,1},{1,2},{2,3},{3,4},{4,5},{5,6},{6,7},{7,8},{8,9},{9,10},{10,1... | collective-permute-start | bytes 5516 | tf_op jit(solution)/shard_map/ppermute | solution.py:186
  111.4 5.1 %collective-permute-start.12 = (f32[3,9,17]{2,1,0:T(8,128)S(1)}, f32[3,9,17]{2,1,0:T(8,128)S(1)}, u32[]{:S(2)}, u32[]{:S(2)}) collective-permute-start(f32[3,9,17]{2,1,0:T(8,128)S(1)} %get-tuple-element.32), channel_id=1, source_target_pairs={{1,0},{2,1},{3,2},{4,3},{5,4},{6,5},{7,6},{8,7},{9,8},{10,9},{11,1... | collective-permute-start | bytes 5516 | tf_op jit(solution)/shard_map/ppermute | solution.py:187
  117.3 6.2 %collective-permute-start.13 = (f32[3,3,9]{2,1,0:T(4,128)S(1)}, f32[3,3,9]{2,1,0:T(4,128)S(1)}, u32[]{:S(2)}, u32[]{:S(2)}) collective-permute-start(f32[3,3,9]{2,1,0:T(4,128)S(1)} %get-tuple-element.15), channel_id=1, source_target_pairs={{0,32},{32,64},{64,96},{1,33},{33,65},{65,97},{2,34},{34,66},{66,9... | collective-permute-start | bytes 980 | tf_op jit(solution)/shard_map/ppermute | solution.py:186
  120.8 4.7 %collective-permute-start.14 = (f32[3,3,9]{2,1,0:T(4,128)}, f32[3,3,9]{2,1,0:T(4,128)}, u32[]{:S(2)}, u32[]{:S(2)}) collective-permute-start(f32[3,3,9]{2,1,0:T(4,128)} %get-tuple-element.16), channel_id=1, source_target_pairs={{32,0},{64,32},{96,64},{33,1},{65,33},{97,65},{34,2},{66,34},{98,6... | collective-permute-start | bytes 980 | tf_op jit(solution)/shard_map/ppermute | solution.py:187
  127.0 4.2 %copy-start.10 = (f32[32]{0:T(128)S(1)}, f32[32]{0:T(128)}, u32[]{:S(2)}) copy-start(f32[32]{0:T(128)} %copy-done.9) | copy-start | bytes 388
  127.0 4.2 %copy-start.12 = (f32[32]{0:T(128)S(1)}, f32[32]{0:T(128)}, u32[]{:S(2)}) copy-start(f32[32]{0:T(128)} %copy-done.11) | copy-start | bytes 388
  127.0 4.2 %copy-start.14 = (f32[32]{0:T(128)S(1)}, f32[32]{0:T(128)}, u32[]{:S(2)}) copy-start(f32[32]{0:T(128)} %copy-done.13) | copy-start | bytes 388
  131.2 43.5 %slice-start.3 = ((s8[12582912]{0:T(1024)(128)(4,1)}), s8[4194304]{0:T(1024)(128)(4,1)S(1)}, s32[]{:S(2)}) async-start(s8[12582912]{0:T(1024)(128)(4,1)} %bitcast.123), calls=%async_computation.3 | async-start | bytes 8388608
  131.2 43.5 %slice-start.4 = ((s8[12582912]{0:T(1024)(128)(4,1)}), s8[4194304]{0:T(1024)(128)(4,1)S(1)}, s32[]{:S(2)}) async-start(s8[12582912]{0:T(1024)(128)(4,1)} %bitcast.123), calls=%async_computation.4 | async-start | bytes 8388608
  140.3 32.6 %copy-start.4 = (bf16[32,128,256]{2,1,0:T(8,128)(2,1)S(1)}, bf16[32,128,256]{2,1,0:T(8,128)(2,1)}, u32[]{:S(2)}) copy-start(bf16[32,128,256]{2,1,0:T(8,128)(2,1)} %param.5) | copy-start | bytes 6291460
  143.5 1.2 collective-permute-start.15
  146.0 2.8 %collective-permute-start.16 = (f32[2]{0:T(128)S(1)}, f32[2]{0:T(128)S(1)}, u32[]{:S(2)}, u32[]{:S(2)}) collective-permute-start(f32[2]{0:T(128)S(1)} %fusion.115), channel_id=1, source_target_pairs={{0,2},{1,3},{2,0},{3,1},{4,6},{5,7},{6,4},{7,5},{8,10},{9,11},{10,... | collective-permute-start | bytes 32 | tf_op jit(solution)/shard_map/ppermute | solution.py:174
  150.2 5.7 %collective-permute-start.17 = (f32[2]{0:T(128)S(1)}, f32[2]{0:T(128)S(1)}, u32[]{:S(2)}, u32[]{:S(2)}) collective-permute-start(f32[2]{0:T(128)S(1)} %fusion.117), channel_id=1, source_target_pairs={{0,4},{1,5},{2,6},{3,7},{4,0},{5,1},{6,2},{7,3},{8,12},{9,13},{10,... | collective-permute-start | bytes 32 | tf_op jit(solution)/shard_map/ppermute | solution.py:174
  155.9 3.0 %collective-permute-start.18 = (f32[2]{0:T(128)S(1)}, f32[2]{0:T(128)S(1)}, u32[]{:S(2)}, u32[]{:S(2)}) collective-permute-start(f32[2]{0:T(128)S(1)} %add.366), channel_id=1, source_target_pairs={{0,8},{1,9},{2,10},{3,11},{4,12},{5,13},{6,14},{7,15},{8,0},{9,1},... | collective-permute-start | bytes 32 | tf_op jit(solution)/shard_map/ppermute | solution.py:174
  158.8 4.4 %collective-permute-start.19 = (f32[2]{0:T(128)S(1)}, f32[2]{0:T(128)S(1)}, u32[]{:S(2)}, u32[]{:S(2)}) collective-permute-start(f32[2]{0:T(128)S(1)} %add.367), channel_id=1, source_target_pairs={{0,16},{1,17},{2,18},{3,19},{4,20},{5,21},{6,22},{7,23},{8,24},{9,... | collective-permute-start | bytes 32 | tf_op jit(solution)/shard_map/ppermute | solution.py:174
  163.2 2.4 %collective-permute-start.20 = (f32[2]{0:T(128)S(1)}, f32[2]{0:T(128)S(1)}, u32[]{:S(2)}, u32[]{:S(2)}) collective-permute-start(f32[2]{0:T(128)S(1)} %add.368), channel_id=1, source_target_pairs={{0,32},{32,0},{64,96},{96,64},{1,33},{33,1},{65,97},{97,65},{2,34}... | collective-permute-start | bytes 32 | tf_op jit(solution)/shard_map/ppermute | solution.py:174
  165.7 3.9 %collective-permute-start.21 = (f32[2]{0:T(128)S(1)}, f32[2]{0:T(128)S(1)}, u32[]{:S(2)}, u32[]{:S(2)}) collective-permute-start(f32[2]{0:T(128)S(1)} %add.369), channel_id=1, source_target_pairs={{0,64},{32,96},{64,0},{96,32},{1,65},{33,97},{65,1},{97,33},{2,66}... | collective-permute-start | bytes 32 | tf_op jit(solution)/shard_map/ppermute | solution.py:174
  174.7 4.0 %copy-start.5 = (f32[32,128,256]{2,1,0:T(8,128)}, f32[32,128,256]{2,1,0:T(8,128)S(1)}, u32[]{:S(2)}) copy-start(f32[32,128,256]{2,1,0:T(8,128)S(1)} %get-tuple-element.18) | copy-start | bytes 12582916
  175.0 3.7 %copy-start.21 = (s32[128]{0:T(128)S(1)}, s32[128]{0:T(128)}, u32[]{:S(2)}) copy-start(s32[128]{0:T(128)} %copy-done.20) | copy-start | bytes 1540
  175.0 3.8 %copy-start.23 = (f32[128]{0:T(128)S(1)}, f32[128]{0:T(128)}, u32[]{:S(2)}) copy-start(f32[128]{0:T(128)} %copy-done.22) | copy-start | bytes 1540
  175.1 3.8 %copy-start.25 = (f32[128]{0:T(128)S(1)}, f32[128]{0:T(128)}, u32[]{:S(2)}) copy-start(f32[128]{0:T(128)} %copy-done.24) | copy-start | bytes 1540
  179.5 49.9 %copy-start.15 = (s32[32,3]{0,1:T(4,128)S(1)}, s32[32,3]{0,1:T(4,128)}, u32[]{:S(2)}) copy-start(s32[32,3]{0,1:T(4,128)} %iota_add_fusion.1) | copy-start | bytes 1156
  227.4 4.3 %copy-start.16 = (s32[4,17]{1,0:T(4,128)S(1)}, s32[4,17]{1,0:T(4,128)}, u32[]{:S(2)}) copy-start(s32[4,17]{1,0:T(4,128)} %iota_add_fusion) | copy-start | bytes 820
  (6 other events, 13.5 us)
